TPU v7x, 32 devices: a whole 2x2x4 slice. The times are simulated.
32 devices in a mesh: dp: 4 (over x, core), label: 8 (over z, y).
Axes of the slice: x: 2, y: 2, z: 4, core: 2. Of those that a mesh axis runs over, the one named last changes fastest.
Arguments:
- token_ids: int32 [64, 2, 32], P(('dp', 'label')), may hold values from 0 to 4095
- labeled: int32 [64], P(('dp', 'label')), may hold values from 0 to 1, as said below
- positive_ids: int32 [64, 16], P(('dp', 'label')), may hold values from 0 to 163839
- vocab_table: bfloat16 [4096, 768], P(('dp', 'label')), may hold values from -6 to 6
- enc_weight: bfloat16 [768, 768], replicated, may hold values from -0.21875 to 0.21875
- label_matrix: bfloat16 [163840, 768], P(('dp', 'label')), may hold values from -0.21875 to 0.21875
- label_log_rates: float32 [163840], P(('dp', 'label')), may hold values from -11.5 to -6.9
Outputs:
- loss: float32 [], replicated
- grad_weight: float32 [768, 768], replicated
- new_log_rates: float32 [163840], P(('dp', 'label'))
Inputs may be any that keep to these rules, and one draw needn't show every extreme that they name: At least one document has labeled = 1.
All inputs are finite; a program needn't handle non-finite values.
Results may differ from a plain program's by a relative error of at most 0.0042.
Values may be sent and summed in bfloat16 or wider, within the bound.
No kernel may reach another device: no remote copies, remote signals or barrier semaphores. Data moves between devices by JAX's collectives and lax.ppermute only.
A program may use at most 128 MiB of HBM per device.

v0:
```python
import jax
import jax.numpy as jnp
from jax import lax
from jax.sharding import PartitionSpec as P


def encode(pooled_rows, enc_weight):
    pre = jnp.dot(pooled_rows, enc_weight, preferred_element_type=jnp.float32)
    inv_norm = lax.rsqrt(jnp.sum(pre * pre, axis=-1, keepdims=True) + 1e-06)
    return (pre * inv_norm, inv_norm)


def tangent(grad_emb, unit_strong, inv_strong):
    return (
        grad_emb - unit_strong * jnp.sum(unit_strong * grad_emb, axis=-1, keepdims=True)
    ) * inv_strong


def outer_sum(pooled_strong, grad_pre):
    return jnp.einsum("dk,dj->kj", pooled_strong, grad_pre, precision=lax.Precision.HIGHEST)


def shards(
    token_ids, labeled, positive_ids, vocab_table, enc_weight, label_matrix, label_log_rates
):
    own_docs = token_ids.shape[0]
    title = token_ids.shape[2]
    width = vocab_table.shape[1]
    vocab_rows = vocab_table.shape[0]
    label_rows = label_matrix.shape[0]
    shard_index = lax.axis_index(("dp", "label"))
    all_tokens, all_labeled, all_positives = (
        lax.all_gather(token_ids, ("dp", "label"), axis=0, tiled=True),
        lax.all_gather(labeled, ("dp", "label"), axis=0, tiled=True),
        lax.all_gather(positive_ids, ("dp", "label"), axis=0, tiled=True),
    )
    docs_all = all_tokens.shape[0]
    flat_tokens = all_tokens.reshape(docs_all * 2, title)
    local_ids = flat_tokens - shard_index * vocab_rows
    vocab_codes = jnp.arange(vocab_rows, dtype=jnp.int32)
    rows = local_ids
    tally = jnp.zeros((lax.axis_size(("dp", "label")) * (own_docs * 2), vocab_rows), jnp.float32)
    for position in range(title):
        tally = tally + (rows[:, position : position + 1] == vocab_codes[None, :]).astype(
            jnp.float32
        )
    pooled_rows = lax.psum_scatter(
        jnp.dot(tally.astype(jnp.bfloat16), vocab_table, preferred_element_type=jnp.float32)
        * (1.0 / title),
        ("dp", "label"),
        scatter_dimension=0,
        tiled=True,
    ).astype(jnp.bfloat16)
    pooled_own = jnp.transpose(pooled_rows.reshape(own_docs, 2, width), (1, 0, 2))
    unit_own, inv_own = encode(pooled_own.reshape(2 * own_docs, width), enc_weight)
    emb_own = unit_own.astype(jnp.bfloat16).reshape(2, own_docs, width)
    scores = (
        jnp.einsum(
            "vrk,lk->vrl",
            lax.all_gather(emb_own, ("dp", "label"), axis=1, tiled=True),
            label_matrix,
            preferred_element_type=jnp.float32,
        )
        * 16.0
        - 6.0
    )
    weak = scores[0]
    strong = scores[1]
    teacher = jax.nn.sigmoid(weak)
    mean_teacher = jnp.mean(teacher, axis=0)
    label_codes = shard_index * label_rows + jnp.arange(label_rows, dtype=jnp.int32)
    hit = jnp.zeros((docs_all, label_rows), dtype=bool)
    for column in range(all_positives.shape[1]):
        hit = hit | (all_positives[:, column : column + 1] == label_codes[None, :])
    flag = (all_labeled == 1)[:, None]
    rates = jnp.exp(label_log_rates)
    target = jnp.where(
        flag, hit.astype(jnp.float32), teacher * rates[None, :] / mean_teacher[None, :]
    )
    total_local = jnp.sum(target)
    loss_local = jnp.sum(jax.nn.softplus(strong) - target * strong)
    slope = (jax.nn.sigmoid(strong) - target).astype(jnp.bfloat16)
    labeled_count = jnp.sum(all_labeled).astype(jnp.float32)
    batch_rate = jnp.sum((flag & hit).astype(jnp.float32), axis=0) / labeled_count
    new_log_rates = jnp.log(0.9 * rates + 0.1 * batch_rate)
    factor = jnp.float32(16.0)
    rows = slope
    grad_emb = lax.psum_scatter(
        jnp.dot(rows, label_matrix, preferred_element_type=jnp.float32) * factor,
        ("dp", "label"),
        scatter_dimension=0,
        tiled=True,
    )
    grad_pre = tangent(grad_emb, unit_own[own_docs:], inv_own[own_docs:])
    weight_local = outer_sum(pooled_own[1].astype(jnp.float32), grad_pre)
    weight_sum, total, loss_sum = lax.psum((weight_local, total_local, loss_local), ("dp", "label"))
    grad_weight = weight_sum / total
    loss = loss_sum / total
    return (loss, grad_weight, new_log_rates)


def solution(mesh):
    return jax.shard_map(
        shards,
        mesh=mesh,
        in_specs=(
            P(("dp", "label"), None, None),
            P(("dp", "label")),
            P(("dp", "label"), None),
            P(("dp", "label"), None),
            P(),
            P(("dp", "label"), None),
            P(("dp", "label")),
        ),
        out_specs=(P(), P(), P(("dp", "label"))),
        check_vma=False,
    )
```

profile of v0, /device:TPU:0, one launch (start us, length us, event | category | flops | bytes accessed | tf_op | source)
XLA Modules:
  0.0 601.3 jit_solution(3730162300531680459)
XLA Ops:
  7.2 0.9 dynamic-update-slice
  8.2 42.0 %all-reduce = s32[64]{0:T(128)S(1)} all-reduce(s32[64]{0:T(128)S(1)} %dynamic-update-slice), channel_id=1, replica_groups=mesh['dp'=4,'label'=8] {'dp','label'}, use_global_device_ids=true, to_apply=%add | all-reduce | flops 64 | bytes 512
  50.2 0.6 reduce_sum.69
  50.8 0.5 broadcast_compare_fusion
  51.3 66.4 %all_gather.12 = s32[64,2,32]{2,1,0:T(2,128)S(1)} all-gather(s32[2,2,32]{2,1,0:T(2,128)} %param.7), channel_id=1, replica_groups=mesh['dp'=4,'label'=8] {'dp','label'}, dimensions={0}, use_global_device_ids=true | all-gather | bytes 16896 | tf_op jit(solution)/shard_map/all_gather | solution.py:33
  117.7 0.3 fusion.64
  118.0 0.4 fusion.63
  119.1 63.5 %all-gather = s32[32,2,16]{2,1,0:T(2,128)S(1)} all-gather(s32[1,2,16]{2,1,0:T(2,128)S(1)} %bitcast.122), channel_id=1, replica_groups=mesh['dp'=4,'label'=8] {'dp','label'}, dimensions={0}, use_global_device_ids=true | all-gather | bytes 4224 | tf_op jit(solution)/shard_map/all_gather | solution.py:35
  182.6 0.8 fusion.65
  183.4 0.8 copy.190
  184.2 0.8 copy.204
  185.1 0.8 copy.203
  185.9 0.8 copy.202
  186.8 0.8 copy.201
  187.6 0.8 copy.200
  188.4 0.8 copy.199
  189.3 1.4 copy.198
  190.6 1.3 copy.197
  192.0 0.7 copy.196
  193.1 0.1 copy.159
  193.2 0.1 copy.170
  193.2 0.1 copy.169
  193.5 0.1 copy.166
  193.7 0.1 copy.163
  193.9 0.1 copy.161
  194.1 0.1 copy.158
  194.4 0.1 copy.186
  194.8 0.1 copy.181
  195.0 0.1 copy.178
  195.3 0.1 copy.175
  195.4 0.1 copy.173
  195.7 0.8 convolution_multiply_fusion
  196.5 43.1 %all-reduce.11 = bf16[128,768]{1,0:T(8,128)(2,1)S(1)} all-reduce(f32[128,768]{1,0:T(8,128)S(1)} %convolution_multiply_fusion), channel_id=2, replica_groups=mesh['dp'=4,'label'=8] {'dp','label'}, use_global_device_ids=true, to_apply=%region_0.0.clone | all-reduce | flops 98304 | bytes 589824
  239.6 0.4 multiply_reduce_fusion
  240.2 65.1 %all_gather.13 = bf16[2,64,768]{2,0,1:T(2,128)(2,1)S(1)} all-gather(bf16[2,2,768]{2,0,1:T(2,128)(2,1)S(1)} %copy.140), channel_id=1, replica_groups=mesh['dp'=4,'label'=8] {'dp','label'}, dimensions={1}, use_global_device_ids=true | all-gather | bytes 202752 | tf_op jit(solution)/shard_map/all_gather | solution.py:60
  305.3 5.9 fusion.5
  311.2 0.4 fusion.16
  311.6 0.2 copy-done.2
  311.9 2.7 convert_reduce_fusion
  314.6 0.6 add_log_fusion
  315.3 3.4 fusion.60
  318.6 5.5 convolution_multiply_fusion.1
  324.2 122.2 %all-reduce.10.cloned.1.call-done = f32[64,768]{1,0:T(8,128)} async-done(((f32[64,768]{1,0:T(8,128)}), f32[64,768]{1,0:T(8,128)}) %all-reduce.10.cloned.1.call-update) | async-done | bytes 196624
  446.4 0.9 multiply_reduce_fusion.1
  447.3 3.3 fusion.50
  450.6 41.7 %all-reduce.3 = (f32[]{:T(128)}, f32[]{:T(128)}) all-reduce(f32[]{:T(128)} %get-tuple-element.4, f32[]{:T(128)} %get-tuple-element.3), channel_id=1, replica_groups=mesh['dp'=4,'label'=8] {'dp','label'}, use_global_device_ids=true, to_apply=%region_4.5 | all-reduce | flops 2 | bytes 16 | tf_op jit(solution)/shard_map/psum | solution.py:96
  493.6 95.9 %all-reduce.8.cloned.1.call-done = f32[768,768]{1,0:T(8,128)} async-done(((f32[768,768]{1,0:T(8,128)}), f32[768,768]{1,0:T(8,128)}) %all-reduce.8.cloned.1.call-update) | async-done | bytes 2359312 | tf_op jit(solution)/shard_map/psum | solution.py:96
  589.5 3.9 broadcast_divide_fusion
  (58 shorter events, 2.5 us)
Async XLA Ops:
  7.2 232.5 %copy-start = (bf16[768,768]{1,0:T(8,128)(2,1)S(1)}, bf16[768,768]{1,0:T(8,128)(2,1)}, u32[]{:S(2)}) copy-start(bf16[768,768]{1,0:T(8,128)(2,1)} %param.11) | copy-start | bytes 3538948
  7.2 439.2 %all-reduce.10.cloned.1.call-start = ((), (), s32[]{:S(2)}) async-start(), calls=%async_computation.1 | async-start | bytes 393216
  118.0 1.1 copy-start.6
  193.0 2.6 copy-start.7
  311.2 0.7 copy-start.2
  311.2 0.7 copy-start.3
  311.2 0.7 copy-start.4
  311.2 0.7 copy-start.5
  311.2 3.4 copy-start.1
  324.1 265.4 %all-reduce.8.cloned.1.call-start = ((), (), s32[]{:S(2)}) async-start(), calls=%async_computation | async-start | bytes 4718592 | tf_op jit(solution)/shard_map/psum | solution.py:96
Sparse Core Ops, SparseCore 0:
  324.2 122.1 all-reduce.9
  452.5 136.9 all-reduce.7
where the time goes:
time: 603 us; the launch traced here: 601 us
  blocking collectives  322 us (53%)
  waiting for transfers between devices  218 us (36%)
  between operations  17.4 us (3%)
  matrix products  15.8 us (3%)
  local copies, waits for them, and re-layouts  15.1 us (3%)
  other arithmetic  13 us (2%)
    unnamed x3, waiting for transfers between devices  122 us
    psum x1, waiting for transfers between devices, shards(): lax.psum((weight_local, total_local, loss_local), ('dp', 'label'))  95.9 us
    unnamed x2, blocking collectives  85 us
    all_gather x1, blocking collectives, shards(): lax.all_gather(token_ids, ('dp', 'label'), axis=0, tiled=True)  66.4 us
    all_gather x1, blocking collectives, shards(): lax.all_gather(emb_own, ('dp', 'label'), axis=1, tiled=True)  65.1 us
    all_gather x1, blocking collectives, shards(): lax.all_gather(positive_ids, ('dp', 'label'), axis=0, tiled=True)  63.5 us
    psum x1, blocking collectives, shards(): lax.psum((weight_local, total_local, loss_local), ('dp', 'label'))  41.7 us
    unnamed x66, local copies, waits for them, and re-layouts  13.5 us
  transfers between devices with their start and end apart: 2, of which 2 were waited for; matrix products, arithmetic and copies ran while one was open for 0% of the time, Pallas kernels for 0%

commit v1 on v0

v1 whole, which is shorter than its diff:
```python
import jax
import jax.numpy as jnp
from jax import lax
from jax.sharding import PartitionSpec as P

AXES = ("dp", "label")


def butterfly_sum(x, n):
    step = 1
    while step < n:
        x = x + lax.ppermute(x, AXES, [(i, i ^ step) for i in range(n)])
        step *= 2
    return x


def make_shards(n):
    def shards(
        token_ids, labeled, positive_ids, vocab_table, enc_weight, label_matrix, label_log_rates
    ):
        own_docs, views, title = token_ids.shape
        n_pos = positive_ids.shape[1]
        vocab_rows, width = vocab_table.shape
        label_rows = label_matrix.shape[0]
        me = lax.axis_index(AXES)
        docs = own_docs * n

        packed = jnp.concatenate(
            [token_ids.reshape(own_docs, views * title), positive_ids, labeled[:, None]], axis=1
        )
        slots = jnp.zeros((n, own_docs, packed.shape[1]), jnp.int32)
        slots = lax.dynamic_update_slice(slots, packed[None], (me, 0, 0))
        every = butterfly_sum(slots, n).reshape(docs, packed.shape[1])
        all_tokens = every[:, : views * title].reshape(docs, views, title)
        all_positives = every[:, views * title : views * title + n_pos]
        all_labeled = every[:, views * title + n_pos]

        rows = jnp.transpose(all_tokens, (1, 0, 2)).reshape(views * docs, title) - me * vocab_rows
        codes = jnp.arange(vocab_rows, dtype=jnp.int32)
        tally = jnp.zeros((views * docs, vocab_rows), jnp.float32)
        for position in range(title):
            tally = tally + (rows[:, position : position + 1] == codes[None, :]).astype(jnp.float32)
        partial = jnp.dot(tally.astype(jnp.bfloat16), vocab_table, preferred_element_type=jnp.float32)
        pooled = (butterfly_sum(partial, n) * (1.0 / title)).astype(jnp.bfloat16)

        pre = jnp.dot(pooled, enc_weight, preferred_element_type=jnp.float32)
        inv_norm = lax.rsqrt(jnp.sum(pre * pre, axis=-1, keepdims=True) + 1e-06)
        unit = pre * inv_norm
        emb = unit.astype(jnp.bfloat16)

        scores = (
            jnp.einsum("rk,lk->rl", emb, label_matrix, preferred_element_type=jnp.float32) * 16.0
            - 6.0
        )
        weak = scores[:docs]
        strong = scores[docs:]
        teacher = jax.nn.sigmoid(weak)
        mean_teacher = jnp.mean(teacher, axis=0)
        label_codes = me * label_rows + jnp.arange(label_rows, dtype=jnp.int32)
        hit = jnp.zeros((docs, label_rows), dtype=bool)
        for column in range(n_pos):
            hit = hit | (all_positives[:, column : column + 1] == label_codes[None, :])
        flag = (all_labeled == 1)[:, None]
        rates = jnp.exp(label_log_rates)
        target = jnp.where(
            flag, hit.astype(jnp.float32), teacher * rates[None, :] / mean_teacher[None, :]
        )
        total_local = jnp.sum(target)
        loss_local = jnp.sum(jax.nn.softplus(strong) - target * strong)
        slope = (jax.nn.sigmoid(strong) - target).astype(jnp.bfloat16)
        labeled_count = jnp.sum(all_labeled).astype(jnp.float32)
        batch_rate = jnp.sum((flag & hit).astype(jnp.float32), axis=0) / labeled_count
        new_log_rates = jnp.log(0.9 * rates + 0.1 * batch_rate)

        grad_local = jnp.dot(slope, label_matrix, preferred_element_type=jnp.float32)
        extra = jnp.zeros((1, width), jnp.float32).at[0, 0].set(total_local).at[0, 1].set(loss_local)
        summed = butterfly_sum(jnp.concatenate([grad_local, extra], axis=0), n)
        total = summed[docs, 0]
        loss_sum = summed[docs, 1]
        grad_emb = summed[:docs] * (16.0 / total)
        unit_strong = unit[docs:]
        grad_pre = (
            grad_emb - unit_strong * jnp.sum(unit_strong * grad_emb, axis=-1, keepdims=True)
        ) * inv_norm[docs:]
        grad_weight = jnp.einsum(
            "dk,dj->kj", pooled[docs:].astype(jnp.float32), grad_pre, precision=lax.Precision.HIGHEST
        )
        loss = loss_sum / total
        return (loss, grad_weight, new_log_rates)

    return shards


def solution(mesh):
    n = mesh.shape["dp"] * mesh.shape["label"]
    assert n & (n - 1) == 0, "n not pow2"
    return jax.shard_map(
        make_shards(n),
        mesh=mesh,
        in_specs=(
            P(AXES, None, None),
            P(AXES),
            P(AXES, None),
            P(AXES, None),
            P(),
            P(AXES, None),
            P(AXES),
        ),
        out_specs=(P(), P(), P(AXES)),
        check_vma=False,
    )
```

time: 603 us -> 134 us (0.22)
  blocking collectives: 322 us -> 0 us
  waiting for transfers between devices: 218 us -> 70.5 us
  starting transfers between devices: 0.08 us -> 24.8 us
  between operations: 17.4 us -> 6.09 us
  local copies, waits for them, and re-layouts: 15.1 us -> 5.74 us
    all_gather x3 -> x0, blocking collectives: 195 us -> none  [the longest x1 66.4 us: shards(): lax.all_gather(token_ids, ('dp', 'label'), axis=0, tiled=True)]
    unnamed x3 -> x0, waiting for transfers between devices: 122 us -> none
    psum x1 -> x0, waiting for transfers between devices: 95.9 us -> none  [shards(): lax.psum((weight_local, total_local, loss_local), ('dp', 'label'))]
    unnamed x2 -> x0, blocking collectives: 85 us -> none
    ppermute x0 -> x15, waiting for transfers between devices: none -> 70.5 us  [butterfly_sum(): x = x + lax.ppermute(x, AXES, [(i, i ^ step) for i in range(n)])]
    psum x1 -> x0, blocking collectives: 41.7 us -> none  [shards(): lax.psum((weight_local, total_local, loss_local), ('dp', 'label'))]
    ppermute x0 -> x15, starting transfers between devices: none -> 24.8 us  [butterfly_sum(): x = x + lax.ppermute(x, AXES, [(i, i ^ step) for i in range(n)])]
    unnamed x66 -> x26, local copies, waits for them, and re-layouts: 13.5 us -> 1.34 us
  transfers between devices with their start and end apart: 2 -> 15, of which waited for: 2 -> 14; matrix products, arithmetic and copies ran while one was open for 0% -> 6% of each run, Pallas kernels for 0% -> 0%
where the time goes in v1:
time: 134 us
  waiting for transfers between devices  70.5 us (53%)
  starting transfers between devices  24.8 us (19%)
  other arithmetic  14.1 us (11%)
  matrix products  12.2 us (9%)
  between operations  6.09 us (5%)
  local copies, waits for them, and re-layouts  5.74 us (4%)
    ppermute x15, waiting for transfers between devices, butterfly_sum(): x = x + lax.ppermute(x, AXES, [(i, i ^ step) for i in range(n)])  70.5 us
    ppermute x15, starting transfers between devices, butterfly_sum(): x = x + lax.ppermute(x, AXES, [(i, i ^ step) for i in range(n)])  24.8 us
    dot_general x1, matrix products, shards(): jnp.einsum('rk,lk->rl', emb, label_matrix, preferred_element_type=jnp.flo...  6.02 us
    another operation x3, other arithmetic  3.84 us
    reduce_sum x1, other arithmetic, shards(): loss_local = jnp.sum(jax.nn.softplus(strong) - target * strong)  3.4 us
    reduce_sum x1, other arithmetic, shards(): jnp.sum((flag & hit).astype(jnp.float32), axis=0) / labeled_count  2.71 us
  transfers between devices with their start and end apart: 15, of which 14 were waited for; matrix products, arithmetic and copies ran while one was open for 6% of the time, Pallas kernels for 0%

profile of v1, /device:TPU:0, one launch (start us, length us, event | category | flops | bytes accessed | tf_op | source)
XLA Modules:
  0.0 133.5 jit_solution(6285115024234494696)
XLA Ops:
  0.7 0.8 copy.48
  1.5 0.8 reshape.111
  2.3 0.8 constant_dynamic-update-slice_fusion
  3.0 3.0 %collective-permute-start = (s32[32,2,81]{2,1,0:T(2,128)S(1)}, s32[32,2,81]{2,1,0:T(2,128)S(1)}, u32[]{:S(2)}, u32[]{:S(2)}) collective-permute-start(s32[32,2,81]{2,1,0:T(2,128)S(1)} %constant_dynamic-update-slice_fusion), channel_id=1, source_target_pairs={{0,1},{1,0},{2,3},{3,2},{4,5},{5,4},{6,7},{7,6},{8,9},{9,8},{10,11... | collective-permute-start | bytes 62216 | tf_op jit(solution)/shard_map/ppermute | solution.py:12
  6.0 1.9 %collective-permute-done = s32[32,2,81]{2,1,0:T(2,128)S(1)} collective-permute-done((s32[32,2,81]{2,1,0:T(2,128)S(1)}, s32[32,2,81]{2,1,0:T(2,128)S(1)}, u32[]{:S(2)}, u32[]{:S(2)}) %collective-permute-start) | collective-permute-done | bytes 20768 | tf_op jit(solution)/shard_map/ppermute | solution.py:12
  7.9 0.8 add_dynamic-update-slice_fusion
  8.7 2.1 %collective-permute-start.1 = (s32[32,2,81]{2,1,0:T(2,128)S(1)}, s32[32,2,81]{2,1,0:T(2,128)S(1)}, u32[]{:S(2)}, u32[]{:S(2)}) collective-permute-start(s32[32,2,81]{2,1,0:T(2,128)S(1)} %add_dynamic-update-slice_fusion), channel_id=1, source_target_pairs={{0,2},{1,3},{2,0},{3,1},{4,6},{5,7},{6,4},{7,5},{8,10},{9,11},{10,... | collective-permute-start | bytes 62216 | tf_op jit(solution)/shard_map/ppermute | solution.py:12
  10.8 1.9 %collective-permute-done.1 = s32[32,2,81]{2,1,0:T(2,128)S(1)} collective-permute-done((s32[32,2,81]{2,1,0:T(2,128)S(1)}, s32[32,2,81]{2,1,0:T(2,128)S(1)}, u32[]{:S(2)}, u32[]{:S(2)}) %collective-permute-start.1) | collective-permute-done | bytes 20768 | tf_op jit(solution)/shard_map/ppermute | solution.py:12
  12.7 3.1 %collective-permute-start.2 = (s32[32,2,81]{2,1,0:T(2,128)S(1)}, s32[32,2,81]{2,1,0:T(2,128)S(1)}, u32[]{:S(2)}, u32[]{:S(2)}) collective-permute-start(s32[32,2,81]{2,1,0:T(2,128)S(1)} %add.194), channel_id=1, source_target_pairs={{0,4},{1,5},{2,6},{3,7},{4,0},{5,1},{6,2},{7,3},{8,12},{9,13},{10,... | collective-permute-start | bytes 62216 | tf_op jit(solution)/shard_map/ppermute | solution.py:12
  15.8 1.9 %collective-permute-done.2 = s32[32,2,81]{2,1,0:T(2,128)S(1)} collective-permute-done((s32[32,2,81]{2,1,0:T(2,128)S(1)}, s32[32,2,81]{2,1,0:T(2,128)S(1)}, u32[]{:S(2)}, u32[]{:S(2)}) %collective-permute-start.2) | collective-permute-done | bytes 20768 | tf_op jit(solution)/shard_map/ppermute | solution.py:12
  17.8 1.2 collective-permute-done.3
  19.0 1.9 %collective-permute-start.4 = (s32[32,2,81]{2,1,0:T(2,128)S(1)}, s32[32,2,81]{2,1,0:T(2,128)S(1)}, u32[]{:S(2)}, u32[]{:S(2)}) collective-permute-start(s32[32,2,81]{2,1,0:T(2,128)S(1)} %add.196), channel_id=1, source_target_pairs={{0,16},{1,17},{2,18},{3,19},{4,20},{5,21},{6,22},{7,23},{8,24},{9,... | collective-permute-start | bytes 62216 | tf_op jit(solution)/shard_map/ppermute | solution.py:12
  20.9 2.1 %collective-permute-done.4 = s32[32,2,81]{2,1,0:T(2,128)S(1)} collective-permute-done((s32[32,2,81]{2,1,0:T(2,128)S(1)}, s32[32,2,81]{2,1,0:T(2,128)S(1)}, u32[]{:S(2)}, u32[]{:S(2)}) %collective-permute-start.4) | collective-permute-done | bytes 20768 | tf_op jit(solution)/shard_map/ppermute | solution.py:12
  23.2 1.7 %fusion.19 = f32[128,768]{1,0:T(8,128)S(1)} fusion(bf16[128,768]{1,0:T(8,128)(2,1)} %param.14, s32[128]{0:T(128)S(1)} %get-tuple-element.52, s32[128]{0:T(128)S(1)} %get-tuple-element.53, s32[128]{0:T(128)S(1)} %get-tuple-element.54, s32[128]{0:T(128)S(1)} %get-tuple-element.55, s32[128]{0:T(128)S(1)} %get-tuple-element.56, s32[128]{0:T(128)S(1)} %get-tuple-element.57, ...), kind=kOutput, calls=%fused_computation.65 | convolution fusion | flops 26738688 | bytes 606208 | tf_op jit(solution)/shard_map/dot_general | solution.py:43
  25.0 1.9 %collective-permute-start.5 = (f32[128,768]{1,0:T(8,128)S(1)}, f32[128,768]{1,0:T(8,128)S(1)}, u32[]{:S(2)}, u32[]{:S(2)}) collective-permute-start(f32[128,768]{1,0:T(8,128)S(1)} %fusion.19), channel_id=1, source_target_pairs={{0,1},{1,0},{2,3},{3,2},{4,5},{5,4},{6,7},{7,6},{8,9},{9,8},{10,11... | collective-permute-start | bytes 1179656 | tf_op jit(solution)/shard_map/ppermute | solution.py:12
  26.9 8.3 %collective-permute-done.5 = f32[128,768]{1,0:T(8,128)S(1)} collective-permute-done((f32[128,768]{1,0:T(8,128)S(1)}, f32[128,768]{1,0:T(8,128)S(1)}, u32[]{:S(2)}, u32[]{:S(2)}) %collective-permute-start.5) | collective-permute-done | bytes 393248 | tf_op jit(solution)/shard_map/ppermute | solution.py:12
  35.2 1.9 %collective-permute-start.6 = (f32[128,768]{1,0:T(8,128)S(1)}, f32[128,768]{1,0:T(8,128)S(1)}, u32[]{:S(2)}, u32[]{:S(2)}) collective-permute-start(f32[128,768]{1,0:T(8,128)S(1)} %add.229), channel_id=1, source_target_pairs={{0,2},{1,3},{2,0},{3,1},{4,6},{5,7},{6,4},{7,5},{8,10},{9,11},{10,... | collective-permute-start | bytes 1179656 | tf_op jit(solution)/shard_map/ppermute | solution.py:12
  37.1 7.5 %collective-permute-done.6 = f32[128,768]{1,0:T(8,128)S(1)} collective-permute-done((f32[128,768]{1,0:T(8,128)S(1)}, f32[128,768]{1,0:T(8,128)S(1)}, u32[]{:S(2)}, u32[]{:S(2)}) %collective-permute-start.6) | collective-permute-done | bytes 393248 | tf_op jit(solution)/shard_map/ppermute | solution.py:12
  44.6 2.8 %collective-permute-start.7 = (f32[128,768]{1,0:T(8,128)S(1)}, f32[128,768]{1,0:T(8,128)S(1)}, u32[]{:S(2)}, u32[]{:S(2)}) collective-permute-start(f32[128,768]{1,0:T(8,128)S(1)} %add.230), channel_id=1, source_target_pairs={{0,4},{1,5},{2,6},{3,7},{4,0},{5,1},{6,2},{7,3},{8,12},{9,13},{10,... | collective-permute-start | bytes 1179656 | tf_op jit(solution)/shard_map/ppermute | solution.py:12
  47.5 0.6 slice.279
  48.1 0.6 compare_reduce_fusion.1
  48.7 0.7 compare_reduce_fusion
  49.4 13.1 %collective-permute-done.7 = f32[128,768]{1,0:T(8,128)S(1)} collective-permute-done((f32[128,768]{1,0:T(8,128)S(1)}, f32[128,768]{1,0:T(8,128)S(1)}, u32[]{:S(2)}, u32[]{:S(2)}) %collective-permute-start.7) | collective-permute-done | bytes 393248 | tf_op jit(solution)/shard_map/ppermute | solution.py:12
  62.7 0.8 slice_reduce_fusion
  65.0 1.6 %collective-permute-start.9 = (f32[128,768]{1,0:T(8,128)S(1)}, f32[128,768]{1,0:T(8,128)S(1)}, u32[]{:S(2)}, u32[]{:S(2)}) collective-permute-start(f32[128,768]{1,0:T(8,128)S(1)} %add.232), channel_id=1, source_target_pairs={{0,16},{1,17},{2,18},{3,19},{4,20},{5,21},{6,22},{7,23},{8,24},{9,... | collective-permute-start | bytes 1179656 | tf_op jit(solution)/shard_map/ppermute | solution.py:12
  66.5 2.7 %convert_reduce_fusion = f32[5120]{0:T(1024)S(1)} fusion(pred[64]{0:T(512)(128)(4,1)S(1)} %bitcast.144, s32[64]{0:T(128)S(1)} %bitcast.142, s32[64]{0:T(128)S(1)} %bitcast.140, s32[64]{0:T(128)S(1)} %bitcast.138, s32[64]{0:T(128)S(1)} %bitcast.136, s32[64]{0:T(128)S(1)} %bitcast.134, s32[64]{0:T(128)S(1)} %bitcast.132, s32[64]{0:T(128)S(1)} %bitcast.130, ...), kind=kLoop, calls=%fused_computation.9 | loop fusion | flops 11136000 | bytes 45120 | tf_op jit(solution)/shard_map/reduce_sum | solution.py:72
  69.9 0.6 add_log_fusion
  70.5 6.0 %collective-permute-done.9 = f32[128,768]{1,0:T(8,128)S(1)} collective-permute-done((f32[128,768]{1,0:T(8,128)S(1)}, f32[128,768]{1,0:T(8,128)S(1)}, u32[]{:S(2)}, u32[]{:S(2)}) %collective-permute-start.9) | collective-permute-done | bytes 393248 | tf_op jit(solution)/shard_map/ppermute | solution.py:12
  76.6 0.4 multiply_reduce_fusion
  77.0 0.1 broadcast_multiply_fusion
  77.2 6.0 %fusion = f32[128,5120]{1,0:T(8,128)S(1)} fusion(bf16[5120,768]{1,0:T(8,128)(2,1)} %param.16, f32[128,768]{1,0:T(8,128)S(1)} %broadcast_multiply_fusion), kind=kOutput, calls=%fused_computation.1 | convolution fusion | flops 1008041984 | bytes 10878976 | tf_op jit(solution)/shard_map/rk,lk->rl/dot_general | solution.py:52
  83.2 0.4 fusion.8
  83.6 3.4 %fusion.2 = (f32[]{:T(128)}, f32[]{:T(128)}, f32[64,5120]{1,0:T(8,128)S(1)}) fusion(f32[128,5120]{1,0:T(8,128)S(1)} %fusion, f32[5120]{0:T(1024)S(1)} %broadcast_multiply_fusion.1, f32[5120]{0:T(1024)S(1)} %get-tuple-element.50, s32[64]{0:T(128)S(1)} %bitcast.143, s32[64]{0:T(128)S(1)} %bitcast.141, s32[64]{0:T(128)S(1)} %bitcast.139, s32[64]{0:T(128)S(1)} %bitcast.137, ...), kind=kLoop, calls=%fused_computation.4 | loop fusion | flops 15728638 | bytes 3997768 | tf_op jit(solution)/shard_map/reduce_sum | solution.py:69
  87.0 1.5 %fusion.6 = f32[64,768]{1,0:T(8,128)S(1)} fusion(bf16[5120,768]{1,0:T(8,128)(2,1)S(1)} %bitcast.107, f32[64,5120]{1,0:T(8,128)S(1)} %get-tuple-element.29, f32[128,5120]{1,0:T(8,128)S(1)} %fusion), kind=kOutput, calls=%fused_computation.13 | convolution fusion | flops 504954880 | bytes 10682368 | tf_op jit(solution)/shard_map/dot_general | solution.py:75
  89.8 2.5 %fusion.55 = f32[1,1]{1,0:T(1,128)} fusion(pred[1,1]{1,0:T(4,128)(4,1)} %bitcast.55, f32[1,1]{1,0:T(1,128)} %bitcast.56, s32[]{:T(128)} %bitcast.57, f32[1,1]{1,0:T(1,128)} %bitcast.54), kind=kLoop, calls=%fused_computation.147 | loop fusion | flops 1 | bytes 17 | tf_op jit(solution)/shard_map/select.3
  92.3 1.4 %scatter.9 = f32[1,768]{1,0:T(1,128)S(1)} dynamic-update-slice(f32[1,768]{1,0:T(1,128)S(1)} %scatter.6, f32[1,1]{1,0:T(1,128)} %fusion.55, s32[]{:T(128)} %constant.80.clone.1, s32[]{:T(128)} %bitcast.57) | dynamic-update-slice | bytes 12 | tf_op jit(solution)/shard_map/scatter | solution.py:76
  93.7 1.6 %collective-permute-start.10 = (f32[65,768]{1,0:T(8,128)S(1)}, f32[65,768]{1,0:T(8,128)S(1)}, u32[]{:S(2)}, u32[]{:S(2)}) collective-permute-start(f32[65,768]{1,0:T(8,128)S(1)} %pad_maximum_fusion), channel_id=1, source_target_pairs={{0,1},{1,0},{2,3},{3,2},{4,5},{5,4},{6,7},{7,6},{8,9},{9,8},{10,11... | collective-permute-start | bytes 599048 | tf_op jit(solution)/shard_map/ppermute | solution.py:12
  95.3 5.4 %collective-permute-done.10 = f32[65,768]{1,0:T(8,128)S(1)} collective-permute-done((f32[65,768]{1,0:T(8,128)S(1)}, f32[65,768]{1,0:T(8,128)S(1)}, u32[]{:S(2)}, u32[]{:S(2)}) %collective-permute-start.10) | collective-permute-done | bytes 199712 | tf_op jit(solution)/shard_map/ppermute | solution.py:12
  100.8 0.8 collective-permute-start.11
  101.5 5.4 %collective-permute-done.11 = f32[65,768]{1,0:T(8,128)S(1)} collective-permute-done((f32[65,768]{1,0:T(8,128)S(1)}, f32[65,768]{1,0:T(8,128)S(1)}, u32[]{:S(2)}, u32[]{:S(2)}) %collective-permute-start.11) | collective-permute-done | bytes 199712 | tf_op jit(solution)/shard_map/ppermute | solution.py:12
  107.0 2.4 %collective-permute-start.12 = (f32[65,768]{1,0:T(8,128)S(1)}, f32[65,768]{1,0:T(8,128)S(1)}, u32[]{:S(2)}, u32[]{:S(2)}) collective-permute-start(f32[65,768]{1,0:T(8,128)S(1)} %add.242), channel_id=1, source_target_pairs={{0,4},{1,5},{2,6},{3,7},{4,0},{5,1},{6,2},{7,3},{8,12},{9,13},{10,... | collective-permute-start | bytes 599048 | tf_op jit(solution)/shard_map/ppermute | solution.py:12
  109.4 8.5 %collective-permute-done.12 = f32[65,768]{1,0:T(8,128)S(1)} collective-permute-done((f32[65,768]{1,0:T(8,128)S(1)}, f32[65,768]{1,0:T(8,128)S(1)}, u32[]{:S(2)}, u32[]{:S(2)}) %collective-permute-start.12) | collective-permute-done | bytes 199712 | tf_op jit(solution)/shard_map/ppermute | solution.py:12
  118.0 1.5 %collective-permute-done.13 = f32[65,768]{1,0:T(8,128)S(1)} collective-permute-done((f32[65,768]{1,0:T(8,128)S(1)}, f32[65,768]{1,0:T(8,128)S(1)}, u32[]{:S(2)}, u32[]{:S(2)}) %collective-permute-start.13) | collective-permute-done | bytes 199712 | tf_op jit(solution)/shard_map/ppermute | solution.py:12
  119.5 1.6 %collective-permute-start.14 = (f32[65,768]{1,0:T(8,128)S(1)}, f32[65,768]{1,0:T(8,128)S(1)}, u32[]{:S(2)}, u32[]{:S(2)}) collective-permute-start(f32[65,768]{1,0:T(8,128)S(1)} %add.244), channel_id=1, source_target_pairs={{0,16},{1,17},{2,18},{3,19},{4,20},{5,21},{6,22},{7,23},{8,24},{9,... | collective-permute-start | bytes 599048 | tf_op jit(solution)/shard_map/ppermute | solution.py:12
  121.2 5.9 %collective-permute-done.14 = f32[65,768]{1,0:T(8,128)S(1)} collective-permute-done((f32[65,768]{1,0:T(8,128)S(1)}, f32[65,768]{1,0:T(8,128)S(1)}, u32[]{:S(2)}, u32[]{:S(2)}) %collective-permute-start.14) | collective-permute-done | bytes 199712 | tf_op jit(solution)/shard_map/ppermute | solution.py:12
  127.1 0.6 fusion.54
  128.4 0.1 multiply_reduce_fusion.1
  129.8 2.6 %fusion.9 = f32[768,768]{1,0:T(8,128)} fusion(f32[128,768]{1,0:T(8,128)S(1)} %broadcast_multiply_fusion, f32[65,768]{1,0:T(8,128)S(1)} %add.245, bf16[128,768]{1,0:T(8,128)(2,1)S(1)} %multiply_convert_fusion, f32[64]{0:T(128)S(1)} %slice.285, f32[64]{0:T(128)S(1)} %multiply_reduce_fusion.1, f32[]{:T(128)} %bitcast.59), kind=kOutput, calls=%fused_computation.20 | convolution fusion | flops 453181440 | bytes 2851844 | tf_op jit(solution)/shard_map/dk,dj->kj/dot_general | solution.py:85
  (59 shorter events, 2.4 us)
Async XLA Ops:
  0.6 76.0 %copy-start = (bf16[768,768]{1,0:T(8,128)(2,1)S(1)}, bf16[768,768]{1,0:T(8,128)(2,1)}, u32[]{:S(2)}) copy-start(bf16[768,768]{1,0:T(8,128)(2,1)} %param.15) | copy-start | bytes 3538948
  3.0 4.9 %collective-permute-start = (s32[32,2,81]{2,1,0:T(2,128)S(1)}, s32[32,2,81]{2,1,0:T(2,128)S(1)}, u32[]{:S(2)}, u32[]{:S(2)}) collective-permute-start(s32[32,2,81]{2,1,0:T(2,128)S(1)} %constant_dynamic-update-slice_fusion), channel_id=1, source_target_pairs={{0,1},{1,0},{2,3},{3,2},{4,5},{5,4},{6,7},{7,6},{8,9},{9,8},{10,11... | collective-permute-start | bytes 62216 | tf_op jit(solution)/shard_map/ppermute | solution.py:12
  8.7 4.0 %collective-permute-start.1 = (s32[32,2,81]{2,1,0:T(2,128)S(1)}, s32[32,2,81]{2,1,0:T(2,128)S(1)}, u32[]{:S(2)}, u32[]{:S(2)}) collective-permute-start(s32[32,2,81]{2,1,0:T(2,128)S(1)} %add_dynamic-update-slice_fusion), channel_id=1, source_target_pairs={{0,2},{1,3},{2,0},{3,1},{4,6},{5,7},{6,4},{7,5},{8,10},{9,11},{10,... | collective-permute-start | bytes 62216 | tf_op jit(solution)/shard_map/ppermute | solution.py:12
  12.7 5.0 %collective-permute-start.2 = (s32[32,2,81]{2,1,0:T(2,128)S(1)}, s32[32,2,81]{2,1,0:T(2,128)S(1)}, u32[]{:S(2)}, u32[]{:S(2)}) collective-permute-start(s32[32,2,81]{2,1,0:T(2,128)S(1)} %add.194), channel_id=1, source_target_pairs={{0,4},{1,5},{2,6},{3,7},{4,0},{5,1},{6,2},{7,3},{8,12},{9,13},{10,... | collective-permute-start | bytes 62216 | tf_op jit(solution)/shard_map/ppermute | solution.py:12
  17.7 1.3 collective-permute-start.3
  19.0 4.0 %collective-permute-start.4 = (s32[32,2,81]{2,1,0:T(2,128)S(1)}, s32[32,2,81]{2,1,0:T(2,128)S(1)}, u32[]{:S(2)}, u32[]{:S(2)}) collective-permute-start(s32[32,2,81]{2,1,0:T(2,128)S(1)} %add.196), channel_id=1, source_target_pairs={{0,16},{1,17},{2,18},{3,19},{4,20},{5,21},{6,22},{7,23},{8,24},{9,... | collective-permute-start | bytes 62216 | tf_op jit(solution)/shard_map/ppermute | solution.py:12
  25.0 10.2 %collective-permute-start.5 = (f32[128,768]{1,0:T(8,128)S(1)}, f32[128,768]{1,0:T(8,128)S(1)}, u32[]{:S(2)}, u32[]{:S(2)}) collective-permute-start(f32[128,768]{1,0:T(8,128)S(1)} %fusion.19), channel_id=1, source_target_pairs={{0,1},{1,0},{2,3},{3,2},{4,5},{5,4},{6,7},{7,6},{8,9},{9,8},{10,11... | collective-permute-start | bytes 1179656 | tf_op jit(solution)/shard_map/ppermute | solution.py:12
  35.2 9.4 %collective-permute-start.6 = (f32[128,768]{1,0:T(8,128)S(1)}, f32[128,768]{1,0:T(8,128)S(1)}, u32[]{:S(2)}, u32[]{:S(2)}) collective-permute-start(f32[128,768]{1,0:T(8,128)S(1)} %add.229), channel_id=1, source_target_pairs={{0,2},{1,3},{2,0},{3,1},{4,6},{5,7},{6,4},{7,5},{8,10},{9,11},{10,... | collective-permute-start | bytes 1179656 | tf_op jit(solution)/shard_map/ppermute | solution.py:12
  44.6 17.9 %collective-permute-start.7 = (f32[128,768]{1,0:T(8,128)S(1)}, f32[128,768]{1,0:T(8,128)S(1)}, u32[]{:S(2)}, u32[]{:S(2)}) collective-permute-start(f32[128,768]{1,0:T(8,128)S(1)} %add.230), channel_id=1, source_target_pairs={{0,4},{1,5},{2,6},{3,7},{4,0},{5,1},{6,2},{7,3},{8,12},{9,13},{10,... | collective-permute-start | bytes 1179656 | tf_op jit(solution)/shard_map/ppermute | solution.py:12
  62.6 7.3 %copy-start.1 = (f32[5120]{0:T(1024)S(1)}, f32[5120]{0:T(1024)}, u32[]{:S(2)}) copy-start(f32[5120]{0:T(1024)} %param.17) | copy-start | bytes 61444
  62.6 2.3 %collective-permute-start.8 = (f32[128,768]{1,0:T(8,128)S(1)}, f32[128,768]{1,0:T(8,128)S(1)}, u32[]{:S(2)}, u32[]{:S(2)}) collective-permute-start(f32[128,768]{1,0:T(8,128)S(1)} %add.231), channel_id=1, source_target_pairs={{0,8},{1,9},{2,10},{3,11},{4,12},{5,13},{6,14},{7,15},{8,0},{9,1},... | collective-permute-start | bytes 1179656 | tf_op jit(solution)/shard_map/ppermute | solution.py:12
  65.0 11.6 %collective-permute-start.9 = (f32[128,768]{1,0:T(8,128)S(1)}, f32[128,768]{1,0:T(8,128)S(1)}, u32[]{:S(2)}, u32[]{:S(2)}) collective-permute-start(f32[128,768]{1,0:T(8,128)S(1)} %add.232), channel_id=1, source_target_pairs={{0,16},{1,17},{2,18},{3,19},{4,20},{5,21},{6,22},{7,23},{8,24},{9,... | collective-permute-start | bytes 1179656 | tf_op jit(solution)/shard_map/ppermute | solution.py:12
  77.0 10.0 %slice-start = ((s8[7864320]{0:T(1024)(128)(4,1)}), s8[4194304]{0:T(1024)(128)(4,1)S(1)}, s32[]{:S(2)}) async-start(s8[7864320]{0:T(1024)(128)(4,1)} %bitcast.106), calls=%async_computation | async-start | bytes 8388608
  77.1 9.8 %slice-start.1 = ((s8[7864320]{0:T(1024)(128)(4,1)}), s8[3670016]{0:T(1024)(128)(4,1)S(1)}, s32[]{:S(2)}) async-start(s8[7864320]{0:T(1024)(128)(4,1)} %bitcast.106), calls=%async_computation.1 | async-start | bytes 7340032
  93.7 7.0 %collective-permute-start.10 = (f32[65,768]{1,0:T(8,128)S(1)}, f32[65,768]{1,0:T(8,128)S(1)}, u32[]{:S(2)}, u32[]{:S(2)}) collective-permute-start(f32[65,768]{1,0:T(8,128)S(1)} %pad_maximum_fusion), channel_id=1, source_target_pairs={{0,1},{1,0},{2,3},{3,2},{4,5},{5,4},{6,7},{7,6},{8,9},{9,8},{10,11... | collective-permute-start | bytes 599048 | tf_op jit(solution)/shard_map/ppermute | solution.py:12
  100.8 6.2 %collective-permute-start.11 = (f32[65,768]{1,0:T(8,128)S(1)}, f32[65,768]{1,0:T(8,128)S(1)}, u32[]{:S(2)}, u32[]{:S(2)}) collective-permute-start(f32[65,768]{1,0:T(8,128)S(1)} %fusion.53), channel_id=1, source_target_pairs={{0,2},{1,3},{2,0},{3,1},{4,6},{5,7},{6,4},{7,5},{8,10},{9,11},{10,... | collective-permute-start | bytes 599048 | tf_op jit(solution)/shard_map/ppermute | solution.py:12
  107.0 10.9 %collective-permute-start.12 = (f32[65,768]{1,0:T(8,128)S(1)}, f32[65,768]{1,0:T(8,128)S(1)}, u32[]{:S(2)}, u32[]{:S(2)}) collective-permute-start(f32[65,768]{1,0:T(8,128)S(1)} %add.242), channel_id=1, source_target_pairs={{0,4},{1,5},{2,6},{3,7},{4,0},{5,1},{6,2},{7,3},{8,12},{9,13},{10,... | collective-permute-start | bytes 599048 | tf_op jit(solution)/shard_map/ppermute | solution.py:12
  117.9 1.5 %collective-permute-start.13 = (f32[65,768]{1,0:T(8,128)S(1)}, f32[65,768]{1,0:T(8,128)S(1)}, u32[]{:S(2)}, u32[]{:S(2)}) collective-permute-start(f32[65,768]{1,0:T(8,128)S(1)} %add.243), channel_id=1, source_target_pairs={{0,8},{1,9},{2,10},{3,11},{4,12},{5,13},{6,14},{7,15},{8,0},{9,1},... | collective-permute-start | bytes 599048 | tf_op jit(solution)/shard_map/ppermute | solution.py:12
  119.5 7.5 %collective-permute-start.14 = (f32[65,768]{1,0:T(8,128)S(1)}, f32[65,768]{1,0:T(8,128)S(1)}, u32[]{:S(2)}, u32[]{:S(2)}) collective-permute-start(f32[65,768]{1,0:T(8,128)S(1)} %add.244), channel_id=1, source_target_pairs={{0,16},{1,17},{2,18},{3,19},{4,20},{5,21},{6,22},{7,23},{8,24},{9,... | collective-permute-start | bytes 599048 | tf_op jit(solution)/shard_map/ppermute | solution.py:12

commit v2 on v1

--- a/solution.py
+++ b/solution.py
@@ -6,15 +6,26 @@
 AXES = ("dp", "label")
 
 
-def butterfly_sum(x, n):
+def butterfly_sum(x, n, pair_step=0):
+    if pair_step:
+        me = lax.axis_index(AXES)
+        upper = (me // pair_step) % 2 == 1
+        half = x.shape[1] // 2
+        low, high = x[:, :half], x[:, half:]
+        swap = [(i, i ^ pair_step) for i in range(n)]
+        x = jnp.where(upper, high, low) + lax.ppermute(jnp.where(upper, low, high), AXES, swap)
     step = 1
     while step < n:
-        x = x + lax.ppermute(x, AXES, [(i, i ^ step) for i in range(n)])
+        if step != pair_step:
+            x = x + lax.ppermute(x, AXES, [(i, i ^ step) for i in range(n)])
         step *= 2
+    if pair_step:
+        other = lax.ppermute(x, AXES, swap)
+        x = jnp.where(upper, jnp.concatenate([other, x], 1), jnp.concatenate([x, other], 1))
     return x
 
 
-def make_shards(n):
+def make_shards(n, pair_step):
     def shards(
         token_ids, labeled, positive_ids, vocab_table, enc_weight, label_matrix, label_log_rates
     ):
@@ -41,7 +52,7 @@
         for position in range(title):
             tally = tally + (rows[:, position : position + 1] == codes[None, :]).astype(jnp.float32)
         partial = jnp.dot(tally.astype(jnp.bfloat16), vocab_table, preferred_element_type=jnp.float32)
-        pooled = (butterfly_sum(partial, n) * (1.0 / title)).astype(jnp.bfloat16)
+        pooled = (butterfly_sum(partial, n, pair_step) * (1.0 / title)).astype(jnp.bfloat16)
 
         pre = jnp.dot(pooled, enc_weight, preferred_element_type=jnp.float32)
         inv_norm = lax.rsqrt(jnp.sum(pre * pre, axis=-1, keepdims=True) + 1e-06)
@@ -73,8 +84,9 @@
         new_log_rates = jnp.log(0.9 * rates + 0.1 * batch_rate)
 
         grad_local = jnp.dot(slope, label_matrix, preferred_element_type=jnp.float32)
-        extra = jnp.zeros((1, width), jnp.float32).at[0, 0].set(total_local).at[0, 1].set(loss_local)
-        summed = butterfly_sum(jnp.concatenate([grad_local, extra], axis=0), n)
+        lane = jnp.arange(width, dtype=jnp.int32)[None, :]
+        extra = jnp.where(lane == 0, total_local, jnp.where(lane == 1, loss_local, 0.0))
+        summed = butterfly_sum(jnp.concatenate([grad_local, extra], axis=0), n, pair_step)
         total = summed[docs, 0]
         loss_sum = summed[docs, 1]
         grad_emb = summed[:docs] * (16.0 / total)
@@ -95,7 +107,7 @@
     n = mesh.shape["dp"] * mesh.shape["label"]
     assert n & (n - 1) == 0, "n not pow2"
     return jax.shard_map(
-        make_shards(n),
+        make_shards(n, mesh.shape["label"]),
         mesh=mesh,
         in_specs=(
             P(AXES, None, None),

time: 134 us -> 102 us (0.76)
  waiting for transfers between devices: 70.5 us -> 42.5 us
  other arithmetic: 14.1 us -> 11.4 us
  local copies, waits for them, and re-layouts: 5.74 us -> 3.74 us
  starting transfers between devices: 24.8 us -> 26.5 us
    ppermute x15 -> x13, waiting for transfers between devices: 70.5 us -> 37.9 us  [butterfly_sum(): x = x + lax.ppermute(x, AXES, [(i, i ^ step) for i in range(n)])]
    ppermute x0 -> x4, waiting for transfers between devices: none -> 4.63 us  [the longest x2 2.61 us: butterfly_sum(): lax.ppermute(jnp.where(upper, low, high), AXES, swap)]
    another operation x3 -> x0, other arithmetic: 3.84 us -> none
    scatter x2 -> x0, local copies, waits for them, and re-layouts: 1.39 us -> none  [shards(): jnp.zeros((1, width), jnp.float32).at[0, 0].set(total_local).at[0, 1]]
    select_n x0 -> x4, other arithmetic: none -> 1.36 us  [the longest x1 1.3 us: shards(): jnp.where(lane == 0, total_local, jnp.where(lane == 1, loss_local, 0.0))]
    ppermute x15 -> x13, starting transfers between devices: 24.8 us -> 26.1 us  [butterfly_sum(): x = x + lax.ppermute(x, AXES, [(i, i ^ step) for i in range(n)])]
  transfers between devices with their start and end apart: 15 -> 17, of which waited for: 14 -> 17; matrix products, arithmetic and copies ran while one was open for 6% -> 5% of each run, Pallas kernels for 0% -> 0%
where the time goes in v2:
time: 102 us; the launch traced here: 101 us
  waiting for transfers between devices  42.5 us (42%)
  starting transfers between devices  26.5 us (26%)
  matrix products  12.2 us (12%)
  other arithmetic  11.4 us (11%)
  between operations  4.78 us (5%)
  local copies, waits for them, and re-layouts  3.74 us (4%)
    ppermute x13, waiting for transfers between devices, butterfly_sum(): x = x + lax.ppermute(x, AXES, [(i, i ^ step) for i in range(n)])  37.9 us
    ppermute x13, starting transfers between devices, butterfly_sum(): x = x + lax.ppermute(x, AXES, [(i, i ^ step) for i in range(n)])  26.1 us
    dot_general x1, matrix products, shards(): jnp.einsum('rk,lk->rl', emb, label_matrix, preferred_element_type=jnp.flo...  6.01 us
    reduce_sum x1, other arithmetic, shards(): total_local = jnp.sum(target)  3.38 us
    reduce_sum x1, other arithmetic, shards(): jnp.sum((flag & hit).astype(jnp.float32), axis=0) / labeled_count  2.72 us
    ppermute x2, waiting for transfers between devices, butterfly_sum(): lax.ppermute(jnp.where(upper, low, high), AXES, swap)  2.61 us
    dot_general x1, matrix products, shards(): jnp.einsum('dk,dj->kj', pooled[docs:].astype(jnp.float32), grad_pre, prec...  2.56 us
  transfers between devices with their start and end apart: 17, of which 17 were waited for; matrix products, arithmetic and copies ran while one was open for 5% of the time, Pallas kernels for 0%

profile of v2, /device:TPU:0, one launch (start us, length us, event | category | flops | bytes accessed | tf_op | source)
XLA Modules:
  0.0 101.1 jit_solution(9310594310390254944)
XLA Ops:
  0.7 0.9 reshape.71
  1.5 0.7 copy.48
  2.3 0.8 constant_dynamic-update-slice_fusion
  3.0 3.0 %collective-permute-start = (s32[32,2,81]{2,1,0:T(2,128)S(1)}, s32[32,2,81]{2,1,0:T(2,128)S(1)}, u32[]{:S(2)}, u32[]{:S(2)}) collective-permute-start(s32[32,2,81]{2,1,0:T(2,128)S(1)} %constant_dynamic-update-slice_fusion), channel_id=1, source_target_pairs={{0,1},{1,0},{2,3},{3,2},{4,5},{5,4},{6,7},{7,6},{8,9},{9,8},{10,11... | collective-permute-start | bytes 62216 | tf_op jit(solution)/shard_map/ppermute | solution.py:20
  6.0 1.9 %collective-permute-done = s32[32,2,81]{2,1,0:T(2,128)S(1)} collective-permute-done((s32[32,2,81]{2,1,0:T(2,128)S(1)}, s32[32,2,81]{2,1,0:T(2,128)S(1)}, u32[]{:S(2)}, u32[]{:S(2)}) %collective-permute-start) | collective-permute-done | bytes 20768 | tf_op jit(solution)/shard_map/ppermute | solution.py:20
  7.9 0.8 add_dynamic-update-slice_fusion
  8.7 2.1 %collective-permute-start.1 = (s32[32,2,81]{2,1,0:T(2,128)S(1)}, s32[32,2,81]{2,1,0:T(2,128)S(1)}, u32[]{:S(2)}, u32[]{:S(2)}) collective-permute-start(s32[32,2,81]{2,1,0:T(2,128)S(1)} %add_dynamic-update-slice_fusion), channel_id=1, source_target_pairs={{0,2},{1,3},{2,0},{3,1},{4,6},{5,7},{6,4},{7,5},{8,10},{9,11},{10,... | collective-permute-start | bytes 62216 | tf_op jit(solution)/shard_map/ppermute | solution.py:20
  10.8 1.9 %collective-permute-done.1 = s32[32,2,81]{2,1,0:T(2,128)S(1)} collective-permute-done((s32[32,2,81]{2,1,0:T(2,128)S(1)}, s32[32,2,81]{2,1,0:T(2,128)S(1)}, u32[]{:S(2)}, u32[]{:S(2)}) %collective-permute-start.1) | collective-permute-done | bytes 20768 | tf_op jit(solution)/shard_map/ppermute | solution.py:20
  12.7 3.1 %collective-permute-start.2 = (s32[32,2,81]{2,1,0:T(2,128)S(1)}, s32[32,2,81]{2,1,0:T(2,128)S(1)}, u32[]{:S(2)}, u32[]{:S(2)}) collective-permute-start(s32[32,2,81]{2,1,0:T(2,128)S(1)} %add.197), channel_id=1, source_target_pairs={{0,4},{1,5},{2,6},{3,7},{4,0},{5,1},{6,2},{7,3},{8,12},{9,13},{10,... | collective-permute-start | bytes 62216 | tf_op jit(solution)/shard_map/ppermute | solution.py:20
  15.8 1.9 %collective-permute-done.2 = s32[32,2,81]{2,1,0:T(2,128)S(1)} collective-permute-done((s32[32,2,81]{2,1,0:T(2,128)S(1)}, s32[32,2,81]{2,1,0:T(2,128)S(1)}, u32[]{:S(2)}, u32[]{:S(2)}) %collective-permute-start.2) | collective-permute-done | bytes 20768 | tf_op jit(solution)/shard_map/ppermute | solution.py:20
  17.8 1.2 %collective-permute-done.3 = s32[32,2,81]{2,1,0:T(2,128)S(1)} collective-permute-done((s32[32,2,81]{2,1,0:T(2,128)S(1)}, s32[32,2,81]{2,1,0:T(2,128)S(1)}, u32[]{:S(2)}, u32[]{:S(2)}) %collective-permute-start.3) | collective-permute-done | bytes 20768 | tf_op jit(solution)/shard_map/ppermute | solution.py:20
  19.0 1.9 %collective-permute-start.4 = (s32[32,2,81]{2,1,0:T(2,128)S(1)}, s32[32,2,81]{2,1,0:T(2,128)S(1)}, u32[]{:S(2)}, u32[]{:S(2)}) collective-permute-start(s32[32,2,81]{2,1,0:T(2,128)S(1)} %add.199), channel_id=1, source_target_pairs={{0,16},{1,17},{2,18},{3,19},{4,20},{5,21},{6,22},{7,23},{8,24},{9,... | collective-permute-start | bytes 62216 | tf_op jit(solution)/shard_map/ppermute | solution.py:20
  20.9 2.1 %collective-permute-done.4 = s32[32,2,81]{2,1,0:T(2,128)S(1)} collective-permute-done((s32[32,2,81]{2,1,0:T(2,128)S(1)}, s32[32,2,81]{2,1,0:T(2,128)S(1)}, u32[]{:S(2)}, u32[]{:S(2)}) %collective-permute-start.4) | collective-permute-done | bytes 20768 | tf_op jit(solution)/shard_map/ppermute | solution.py:20
  23.2 1.7 %fusion.22 = f32[128,768]{1,0:T(8,128)S(1)} fusion(bf16[128,768]{1,0:T(8,128)(2,1)} %param.10, s32[128]{0:T(128)S(1)} %get-tuple-element.28, s32[128]{0:T(128)S(1)} %get-tuple-element.29, s32[128]{0:T(128)S(1)} %get-tuple-element.30, s32[128]{0:T(128)S(1)} %get-tuple-element.31, s32[128]{0:T(128)S(1)} %get-tuple-element.32, s32[128]{0:T(128)S(1)} %get-tuple-element.33, ...), kind=kOutput, calls=%fused_computation.75 | convolution fusion | flops 26738688 | bytes 606208 | tf_op jit(solution)/shard_map/dot_general | solution.py:54
  25.1 1.4 %collective-permute-done.5 = f32[128,384]{1,0:T(8,128)S(1)} collective-permute-done((f32[128,384]{1,0:T(8,128)S(1)}, f32[128,384]{1,0:T(8,128)S(1)}, u32[]{:S(2)}, u32[]{:S(2)}) %collective-permute-start.5) | collective-permute-done | bytes 196640 | tf_op jit(solution)/shard_map/ppermute | solution.py:16
  26.5 1.9 %collective-permute-start.6 = (f32[128,384]{1,0:T(8,128)S(1)}, f32[128,384]{1,0:T(8,128)S(1)}, u32[]{:S(2)}, u32[]{:S(2)}) collective-permute-start(f32[128,384]{1,0:T(8,128)S(1)} %select_add_fusion), channel_id=1, source_target_pairs={{0,1},{1,0},{2,3},{3,2},{4,5},{5,4},{6,7},{7,6},{8,9},{9,8},{10,11... | collective-permute-start | bytes 589832 | tf_op jit(solution)/shard_map/ppermute | solution.py:20
  28.5 5.2 %collective-permute-done.6 = f32[128,384]{1,0:T(8,128)S(1)} collective-permute-done((f32[128,384]{1,0:T(8,128)S(1)}, f32[128,384]{1,0:T(8,128)S(1)}, u32[]{:S(2)}, u32[]{:S(2)}) %collective-permute-start.6) | collective-permute-done | bytes 196640 | tf_op jit(solution)/shard_map/ppermute | solution.py:20
  33.7 1.9 %collective-permute-start.7 = (f32[128,384]{1,0:T(8,128)S(1)}, f32[128,384]{1,0:T(8,128)S(1)}, u32[]{:S(2)}, u32[]{:S(2)}) collective-permute-start(f32[128,384]{1,0:T(8,128)S(1)} %add.233), channel_id=1, source_target_pairs={{0,2},{1,3},{2,0},{3,1},{4,6},{5,7},{6,4},{7,5},{8,10},{9,11},{10,... | collective-permute-start | bytes 589832 | tf_op jit(solution)/shard_map/ppermute | solution.py:20
  35.7 4.2 %collective-permute-done.7 = f32[128,384]{1,0:T(8,128)S(1)} collective-permute-done((f32[128,384]{1,0:T(8,128)S(1)}, f32[128,384]{1,0:T(8,128)S(1)}, u32[]{:S(2)}, u32[]{:S(2)}) %collective-permute-start.7) | collective-permute-done | bytes 196640 | tf_op jit(solution)/shard_map/ppermute | solution.py:20
  40.0 2.8 %collective-permute-start.8 = (f32[128,384]{1,0:T(8,128)S(1)}, f32[128,384]{1,0:T(8,128)S(1)}, u32[]{:S(2)}, u32[]{:S(2)}) collective-permute-start(f32[128,384]{1,0:T(8,128)S(1)} %add.234), channel_id=1, source_target_pairs={{0,4},{1,5},{2,6},{3,7},{4,0},{5,1},{6,2},{7,3},{8,12},{9,13},{10,... | collective-permute-start | bytes 589832 | tf_op jit(solution)/shard_map/ppermute | solution.py:20
  42.8 0.8 slice_reduce_fusion
  45.5 5.1 %collective-permute-done.8 = f32[128,384]{1,0:T(8,128)S(1)} collective-permute-done((f32[128,384]{1,0:T(8,128)S(1)}, f32[128,384]{1,0:T(8,128)S(1)}, u32[]{:S(2)}, u32[]{:S(2)}) %collective-permute-start.8) | collective-permute-done | bytes 196640 | tf_op jit(solution)/shard_map/ppermute | solution.py:20
  50.6 1.6 %collective-permute-start.9 = (f32[128,384]{1,0:T(8,128)S(1)}, f32[128,384]{1,0:T(8,128)S(1)}, u32[]{:S(2)}, u32[]{:S(2)}) collective-permute-start(f32[128,384]{1,0:T(8,128)S(1)} %add.235), channel_id=1, source_target_pairs={{0,16},{1,17},{2,18},{3,19},{4,20},{5,21},{6,22},{7,23},{8,24},{9,... | collective-permute-start | bytes 589832 | tf_op jit(solution)/shard_map/ppermute | solution.py:20
  52.2 2.7 %convert_reduce_fusion = f32[5120]{0:T(1024)S(1)} fusion(pred[64]{0:T(512)(128)(4,1)S(1)} %bitcast.140, s32[64]{0:T(128)S(1)} %bitcast.138, s32[64]{0:T(128)S(1)} %bitcast.108, s32[64]{0:T(128)S(1)} %bitcast.110, s32[64]{0:T(128)S(1)} %bitcast.112, s32[64]{0:T(128)S(1)} %bitcast.114, s32[64]{0:T(128)S(1)} %bitcast.116, s32[64]{0:T(128)S(1)} %bitcast.118, ...), kind=kLoop, calls=%fused_computation.9 | loop fusion | flops 11136000 | bytes 45120 | tf_op jit(solution)/shard_map/reduce_sum | solution.py:83
  54.9 1.5 %collective-permute-done.9 = f32[128,384]{1,0:T(8,128)S(1)} collective-permute-done((f32[128,384]{1,0:T(8,128)S(1)}, f32[128,384]{1,0:T(8,128)S(1)}, u32[]{:S(2)}, u32[]{:S(2)}) %collective-permute-start.9) | collective-permute-done | bytes 196640 | tf_op jit(solution)/shard_map/ppermute | solution.py:20
  56.5 0.6 add_log_fusion
  57.1 0.8 collective-permute-done.10
  58.0 0.4 multiply_reduce_fusion
  58.4 0.1 broadcast_multiply_fusion
  58.5 6.0 %fusion = f32[128,5120]{1,0:T(8,128)S(1)} fusion(bf16[5120,768]{1,0:T(8,128)(2,1)} %param.12, f32[128,768]{1,0:T(8,128)S(1)} %broadcast_multiply_fusion), kind=kOutput, calls=%fused_computation.1 | convolution fusion | flops 1008041984 | bytes 10878976 | tf_op jit(solution)/shard_map/rk,lk->rl/dot_general | solution.py:63
  64.5 0.4 fusion.10
  64.9 3.4 %fusion.56 = (f32[]{:T(128)}, f32[]{:T(128)}, f32[64,5120]{1,0:T(8,128)S(1)}) fusion(f32[128,5120]{1,0:T(8,128)S(1)} %fusion, f32[5120]{0:T(1024)S(1)} %broadcast_multiply_fusion.1, f32[5120]{0:T(1024)S(1)} %get-tuple-element.26, s32[64]{0:T(128)S(1)} %bitcast.139, s32[64]{0:T(128)S(1)} %bitcast.109, s32[64]{0:T(128)S(1)} %bitcast.111, s32[64]{0:T(128)S(1)} %bitcast.113, ...), kind=kLoop, calls=%fused_computation.153 | loop fusion | flops 15728638 | bytes 3997768 | tf_op jit(solution)/shard_map/reduce_sum | solution.py:79
  68.3 1.5 %fusion.6 = f32[64,768]{1,0:T(8,128)S(1)} fusion(bf16[5120,768]{1,0:T(8,128)(2,1)S(1)} %bitcast.103, f32[64,5120]{1,0:T(8,128)S(1)} %get-tuple-element.5, f32[128,5120]{1,0:T(8,128)S(1)} %fusion), kind=kOutput, calls=%fused_computation.13 | convolution fusion | flops 504954880 | bytes 10682368 | tf_op jit(solution)/shard_map/dot_general | solution.py:86
  69.8 1.3 %compare_select_fusion.2 = f32[1,768]{1,0:T(1,128)S(1)} fusion(f32[]{:T(128)} %get-tuple-element.4, f32[]{:T(128)} %get-tuple-element.3), kind=kLoop, calls=%fused_computation.114 | loop fusion | flops 3072 | bytes 3080 | tf_op jit(solution)/shard_map/jit(_where)/select_n | solution.py:88
  71.2 0.2 collective-permute-start.11
  71.4 1.2 %collective-permute-done.11 = f32[65,384]{1,0:T(8,128)S(1)} collective-permute-done((f32[65,384]{1,0:T(8,128)S(1)}, f32[65,384]{1,0:T(8,128)S(1)}, u32[]{:S(2)}, u32[]{:S(2)}) %collective-permute-start.11) | collective-permute-done | bytes 99872 | tf_op jit(solution)/shard_map/ppermute | solution.py:16
  72.6 1.6 %collective-permute-start.12 = (f32[65,384]{1,0:T(8,128)S(1)}, f32[65,384]{1,0:T(8,128)S(1)}, u32[]{:S(2)}, u32[]{:S(2)}) collective-permute-start(f32[65,384]{1,0:T(8,128)S(1)} %select_add_fusion.1), channel_id=1, source_target_pairs={{0,1},{1,0},{2,3},{3,2},{4,5},{5,4},{6,7},{7,6},{8,9},{9,8},{10,11... | collective-permute-start | bytes 299528 | tf_op jit(solution)/shard_map/ppermute | solution.py:20
  74.2 3.6 %collective-permute-done.12 = f32[65,384]{1,0:T(8,128)S(1)} collective-permute-done((f32[65,384]{1,0:T(8,128)S(1)}, f32[65,384]{1,0:T(8,128)S(1)}, u32[]{:S(2)}, u32[]{:S(2)}) %collective-permute-start.12) | collective-permute-done | bytes 99872 | tf_op jit(solution)/shard_map/ppermute | solution.py:20
  77.8 1.6 %collective-permute-start.13 = (f32[65,384]{1,0:T(8,128)S(1)}, f32[65,384]{1,0:T(8,128)S(1)}, u32[]{:S(2)}, u32[]{:S(2)}) collective-permute-start(f32[65,384]{1,0:T(8,128)S(1)} %add.245), channel_id=1, source_target_pairs={{0,2},{1,3},{2,0},{3,1},{4,6},{5,7},{6,4},{7,5},{8,10},{9,11},{10,... | collective-permute-start | bytes 299528 | tf_op jit(solution)/shard_map/ppermute | solution.py:20
  79.4 3.2 %collective-permute-done.13 = f32[65,384]{1,0:T(8,128)S(1)} collective-permute-done((f32[65,384]{1,0:T(8,128)S(1)}, f32[65,384]{1,0:T(8,128)S(1)}, u32[]{:S(2)}, u32[]{:S(2)}) %collective-permute-start.13) | collective-permute-done | bytes 99872 | tf_op jit(solution)/shard_map/ppermute | solution.py:20
  82.6 3.0 %collective-permute-start.14 = (f32[65,384]{1,0:T(8,128)S(1)}, f32[65,384]{1,0:T(8,128)S(1)}, u32[]{:S(2)}, u32[]{:S(2)}) collective-permute-start(f32[65,384]{1,0:T(8,128)S(1)} %add.246), channel_id=1, source_target_pairs={{0,4},{1,5},{2,6},{3,7},{4,0},{5,1},{6,2},{7,3},{8,12},{9,13},{10,... | collective-permute-start | bytes 299528 | tf_op jit(solution)/shard_map/ppermute | solution.py:20
  85.6 2.8 %collective-permute-done.14 = f32[65,384]{1,0:T(8,128)S(1)} collective-permute-done((f32[65,384]{1,0:T(8,128)S(1)}, f32[65,384]{1,0:T(8,128)S(1)}, u32[]{:S(2)}, u32[]{:S(2)}) %collective-permute-start.14) | collective-permute-done | bytes 99872 | tf_op jit(solution)/shard_map/ppermute | solution.py:20
  88.4 1.5 %collective-permute-start.15 = (f32[65,384]{1,0:T(8,128)S(1)}, f32[65,384]{1,0:T(8,128)S(1)}, u32[]{:S(2)}, u32[]{:S(2)}) collective-permute-start(f32[65,384]{1,0:T(8,128)S(1)} %add.247), channel_id=1, source_target_pairs={{0,16},{1,17},{2,18},{3,19},{4,20},{5,21},{6,22},{7,23},{8,24},{9,... | collective-permute-start | bytes 299528 | tf_op jit(solution)/shard_map/ppermute | solution.py:20
  90.0 3.3 %collective-permute-done.15 = f32[65,384]{1,0:T(8,128)S(1)} collective-permute-done((f32[65,384]{1,0:T(8,128)S(1)}, f32[65,384]{1,0:T(8,128)S(1)}, u32[]{:S(2)}, u32[]{:S(2)}) %collective-permute-start.15) | collective-permute-done | bytes 99872 | tf_op jit(solution)/shard_map/ppermute | solution.py:20
  93.4 1.2 %collective-permute-done.16 = f32[65,384]{1,0:T(8,128)S(1)} collective-permute-done((f32[65,384]{1,0:T(8,128)S(1)}, f32[65,384]{1,0:T(8,128)S(1)}, u32[]{:S(2)}, u32[]{:S(2)}) %collective-permute-start.16) | collective-permute-done | bytes 99872 | tf_op jit(solution)/shard_map/ppermute | solution.py:23
  94.7 0.6 fusion.57
  97.3 0.1 multiply_reduce_fusion.1
  97.4 2.6 %fusion.11 = f32[768,768]{1,0:T(8,128)} fusion(f32[128,768]{1,0:T(8,128)S(1)} %broadcast_multiply_fusion, f32[65,768]{1,0:T(8,128)S(1)} %maximum_select_fusion.1, bf16[128,768]{1,0:T(8,128)(2,1)S(1)} %fusion.9, f32[64]{0:T(128)S(1)} %slice.265, f32[64]{0:T(128)S(1)} %multiply_reduce_fusion.1, f32[]{:T(128)} %bitcast.55), kind=kOutput, calls=%fused_computation.24 | convolution fusion | flops 453181440 | bytes 2851844 | tf_op jit(solution)/shard_map/dk,dj->kj/dot_general | solution.py:97
  (60 shorter events, 2.3 us)
Async XLA Ops:
  0.6 57.3 %copy-start = (bf16[768,768]{1,0:T(8,128)(2,1)S(1)}, bf16[768,768]{1,0:T(8,128)(2,1)}, u32[]{:S(2)}) copy-start(bf16[768,768]{1,0:T(8,128)(2,1)} %param.11) | copy-start | bytes 3538948
  3.0 4.9 %collective-permute-start = (s32[32,2,81]{2,1,0:T(2,128)S(1)}, s32[32,2,81]{2,1,0:T(2,128)S(1)}, u32[]{:S(2)}, u32[]{:S(2)}) collective-permute-start(s32[32,2,81]{2,1,0:T(2,128)S(1)} %constant_dynamic-update-slice_fusion), channel_id=1, source_target_pairs={{0,1},{1,0},{2,3},{3,2},{4,5},{5,4},{6,7},{7,6},{8,9},{9,8},{10,11... | collective-permute-start | bytes 62216 | tf_op jit(solution)/shard_map/ppermute | solution.py:20
  8.7 4.0 %collective-permute-start.1 = (s32[32,2,81]{2,1,0:T(2,128)S(1)}, s32[32,2,81]{2,1,0:T(2,128)S(1)}, u32[]{:S(2)}, u32[]{:S(2)}) collective-permute-start(s32[32,2,81]{2,1,0:T(2,128)S(1)} %add_dynamic-update-slice_fusion), channel_id=1, source_target_pairs={{0,2},{1,3},{2,0},{3,1},{4,6},{5,7},{6,4},{7,5},{8,10},{9,11},{10,... | collective-permute-start | bytes 62216 | tf_op jit(solution)/shard_map/ppermute | solution.py:20
  12.7 5.0 %collective-permute-start.2 = (s32[32,2,81]{2,1,0:T(2,128)S(1)}, s32[32,2,81]{2,1,0:T(2,128)S(1)}, u32[]{:S(2)}, u32[]{:S(2)}) collective-permute-start(s32[32,2,81]{2,1,0:T(2,128)S(1)} %add.197), channel_id=1, source_target_pairs={{0,4},{1,5},{2,6},{3,7},{4,0},{5,1},{6,2},{7,3},{8,12},{9,13},{10,... | collective-permute-start | bytes 62216 | tf_op jit(solution)/shard_map/ppermute | solution.py:20
  17.7 1.3 %collective-permute-start.3 = (s32[32,2,81]{2,1,0:T(2,128)S(1)}, s32[32,2,81]{2,1,0:T(2,128)S(1)}, u32[]{:S(2)}, u32[]{:S(2)}) collective-permute-start(s32[32,2,81]{2,1,0:T(2,128)S(1)} %add.198), channel_id=1, source_target_pairs={{0,8},{1,9},{2,10},{3,11},{4,12},{5,13},{6,14},{7,15},{8,0},{9,1},... | collective-permute-start | bytes 62216 | tf_op jit(solution)/shard_map/ppermute | solution.py:20
  19.0 4.0 %collective-permute-start.4 = (s32[32,2,81]{2,1,0:T(2,128)S(1)}, s32[32,2,81]{2,1,0:T(2,128)S(1)}, u32[]{:S(2)}, u32[]{:S(2)}) collective-permute-start(s32[32,2,81]{2,1,0:T(2,128)S(1)} %add.199), channel_id=1, source_target_pairs={{0,16},{1,17},{2,18},{3,19},{4,20},{5,21},{6,22},{7,23},{8,24},{9,... | collective-permute-start | bytes 62216 | tf_op jit(solution)/shard_map/ppermute | solution.py:20
  25.0 1.5 %collective-permute-start.5 = (f32[128,384]{1,0:T(8,128)S(1)}, f32[128,384]{1,0:T(8,128)S(1)}, u32[]{:S(2)}, u32[]{:S(2)}) collective-permute-start(f32[128,384]{1,0:T(8,128)S(1)} %slice_select_fusion), channel_id=1, source_target_pairs={{0,8},{1,9},{2,10},{3,11},{4,12},{5,13},{6,14},{7,15},{8,0},{9,1},... | collective-permute-start | bytes 589832 | tf_op jit(solution)/shard_map/ppermute | solution.py:16
  26.5 7.1 %collective-permute-start.6 = (f32[128,384]{1,0:T(8,128)S(1)}, f32[128,384]{1,0:T(8,128)S(1)}, u32[]{:S(2)}, u32[]{:S(2)}) collective-permute-start(f32[128,384]{1,0:T(8,128)S(1)} %select_add_fusion), channel_id=1, source_target_pairs={{0,1},{1,0},{2,3},{3,2},{4,5},{5,4},{6,7},{7,6},{8,9},{9,8},{10,11... | collective-permute-start | bytes 589832 | tf_op jit(solution)/shard_map/ppermute | solution.py:20
  33.7 6.3 %collective-permute-start.7 = (f32[128,384]{1,0:T(8,128)S(1)}, f32[128,384]{1,0:T(8,128)S(1)}, u32[]{:S(2)}, u32[]{:S(2)}) collective-permute-start(f32[128,384]{1,0:T(8,128)S(1)} %add.233), channel_id=1, source_target_pairs={{0,2},{1,3},{2,0},{3,1},{4,6},{5,7},{6,4},{7,5},{8,10},{9,11},{10,... | collective-permute-start | bytes 589832 | tf_op jit(solution)/shard_map/ppermute | solution.py:20
  40.0 16.5 %copy-start.1 = (f32[5120]{0:T(1024)S(1)}, f32[5120]{0:T(1024)}, u32[]{:S(2)}) copy-start(f32[5120]{0:T(1024)} %param.13) | copy-start | bytes 61444
  40.0 10.6 %collective-permute-start.8 = (f32[128,384]{1,0:T(8,128)S(1)}, f32[128,384]{1,0:T(8,128)S(1)}, u32[]{:S(2)}, u32[]{:S(2)}) collective-permute-start(f32[128,384]{1,0:T(8,128)S(1)} %add.234), channel_id=1, source_target_pairs={{0,4},{1,5},{2,6},{3,7},{4,0},{5,1},{6,2},{7,3},{8,12},{9,13},{10,... | collective-permute-start | bytes 589832 | tf_op jit(solution)/shard_map/ppermute | solution.py:20
  50.6 5.8 %collective-permute-start.9 = (f32[128,384]{1,0:T(8,128)S(1)}, f32[128,384]{1,0:T(8,128)S(1)}, u32[]{:S(2)}, u32[]{:S(2)}) collective-permute-start(f32[128,384]{1,0:T(8,128)S(1)} %add.235), channel_id=1, source_target_pairs={{0,16},{1,17},{2,18},{3,19},{4,20},{5,21},{6,22},{7,23},{8,24},{9,... | collective-permute-start | bytes 589832 | tf_op jit(solution)/shard_map/ppermute | solution.py:20
  56.4 1.5 %collective-permute-start.10 = (f32[128,384]{1,0:T(8,128)S(1)}, f32[128,384]{1,0:T(8,128)S(1)}, u32[]{:S(2)}, u32[]{:S(2)}) collective-permute-start(f32[128,384]{1,0:T(8,128)S(1)} %add.236), channel_id=1, source_target_pairs={{0,8},{1,9},{2,10},{3,11},{4,12},{5,13},{6,14},{7,15},{8,0},{9,1},... | collective-permute-start | bytes 589832 | tf_op jit(solution)/shard_map/ppermute | solution.py:23
  58.4 9.9 %slice-start = ((s8[7864320]{0:T(1024)(128)(4,1)}), s8[4194304]{0:T(1024)(128)(4,1)S(1)}, s32[]{:S(2)}) async-start(s8[7864320]{0:T(1024)(128)(4,1)} %bitcast.102), calls=%async_computation | async-start | bytes 8388608
  58.5 9.8 %slice-start.1 = ((s8[7864320]{0:T(1024)(128)(4,1)}), s8[3670016]{0:T(1024)(128)(4,1)S(1)}, s32[]{:S(2)}) async-start(s8[7864320]{0:T(1024)(128)(4,1)} %bitcast.102), calls=%async_computation.1 | async-start | bytes 7340032
  71.2 1.4 %collective-permute-start.11 = (f32[65,384]{1,0:T(8,128)S(1)}, f32[65,384]{1,0:T(8,128)S(1)}, u32[]{:S(2)}, u32[]{:S(2)}) collective-permute-start(f32[65,384]{1,0:T(8,128)S(1)} %broadcast_select_fusion), channel_id=1, source_target_pairs={{0,8},{1,9},{2,10},{3,11},{4,12},{5,13},{6,14},{7,15},{8,0},{9,1},... | collective-permute-start | bytes 299528 | tf_op jit(solution)/shard_map/ppermute | solution.py:16
  72.6 5.2 %collective-permute-start.12 = (f32[65,384]{1,0:T(8,128)S(1)}, f32[65,384]{1,0:T(8,128)S(1)}, u32[]{:S(2)}, u32[]{:S(2)}) collective-permute-start(f32[65,384]{1,0:T(8,128)S(1)} %select_add_fusion.1), channel_id=1, source_target_pairs={{0,1},{1,0},{2,3},{3,2},{4,5},{5,4},{6,7},{7,6},{8,9},{9,8},{10,11... | collective-permute-start | bytes 299528 | tf_op jit(solution)/shard_map/ppermute | solution.py:20
  77.8 4.8 %collective-permute-start.13 = (f32[65,384]{1,0:T(8,128)S(1)}, f32[65,384]{1,0:T(8,128)S(1)}, u32[]{:S(2)}, u32[]{:S(2)}) collective-permute-start(f32[65,384]{1,0:T(8,128)S(1)} %add.245), channel_id=1, source_target_pairs={{0,2},{1,3},{2,0},{3,1},{4,6},{5,7},{6,4},{7,5},{8,10},{9,11},{10,... | collective-permute-start | bytes 299528 | tf_op jit(solution)/shard_map/ppermute | solution.py:20
  82.6 5.8 %collective-permute-start.14 = (f32[65,384]{1,0:T(8,128)S(1)}, f32[65,384]{1,0:T(8,128)S(1)}, u32[]{:S(2)}, u32[]{:S(2)}) collective-permute-start(f32[65,384]{1,0:T(8,128)S(1)} %add.246), channel_id=1, source_target_pairs={{0,4},{1,5},{2,6},{3,7},{4,0},{5,1},{6,2},{7,3},{8,12},{9,13},{10,... | collective-permute-start | bytes 299528 | tf_op jit(solution)/shard_map/ppermute | solution.py:20
  88.4 4.8 %collective-permute-start.15 = (f32[65,384]{1,0:T(8,128)S(1)}, f32[65,384]{1,0:T(8,128)S(1)}, u32[]{:S(2)}, u32[]{:S(2)}) collective-permute-start(f32[65,384]{1,0:T(8,128)S(1)} %add.247), channel_id=1, source_target_pairs={{0,16},{1,17},{2,18},{3,19},{4,20},{5,21},{6,22},{7,23},{8,24},{9,... | collective-permute-start | bytes 299528 | tf_op jit(solution)/shard_map/ppermute | solution.py:20
  93.3 1.4 %collective-permute-start.16 = (f32[65,384]{1,0:T(8,128)S(1)}, f32[65,384]{1,0:T(8,128)S(1)}, u32[]{:S(2)}, u32[]{:S(2)}) collective-permute-start(f32[65,384]{1,0:T(8,128)S(1)} %add.248), channel_id=1, source_target_pairs={{0,8},{1,9},{2,10},{3,11},{4,12},{5,13},{6,14},{7,15},{8,0},{9,1},... | collective-permute-start | bytes 299528 | tf_op jit(solution)/shard_map/ppermute | solution.py:23

commit v3 on v1

--- a/solution.py
+++ b/solution.py
@@ -6,15 +6,27 @@
 AXES = ("dp", "label")
 
 
-def butterfly_sum(x, n):
-    step = 1
+def tree_sum(x, n, n_label):
+    me = lax.axis_index(AXES)
+    upper = (me // n_label) % 2 == 1
+    half = x.shape[1] // 2
+    low, high = x[:, :half], x[:, half:]
+    swap = [(i, i ^ n_label) for i in range(n)]
+    x = jnp.where(upper, high, low) + lax.ppermute(jnp.where(upper, low, high), AXES, swap)
+    rows = x.shape[0]
+    part = lax.all_to_all(x.reshape(n_label, rows // n_label, half), "label", 0, 0, tiled=False)
+    part = jnp.sum(part, axis=0)
+    step = 2 * n_label
     while step < n:
-        x = x + lax.ppermute(x, AXES, [(i, i ^ step) for i in range(n)])
+        part = part + lax.ppermute(part, AXES, [(i, i ^ step) for i in range(n)])
         step *= 2
-    return x
+    every = jnp.broadcast_to(part[None], (n_label,) + part.shape)
+    x = lax.all_to_all(every, "label", 0, 0, tiled=False).reshape(rows, half)
+    other = lax.ppermute(x, AXES, swap)
+    return jnp.where(upper, jnp.concatenate([other, x], 1), jnp.concatenate([x, other], 1))
 
 
-def make_shards(n):
+def make_shards(n, n_label):
     def shards(
         token_ids, labeled, positive_ids, vocab_table, enc_weight, label_matrix, label_log_rates
     ):
@@ -28,9 +40,8 @@
         packed = jnp.concatenate(
             [token_ids.reshape(own_docs, views * title), positive_ids, labeled[:, None]], axis=1
         )
-        slots = jnp.zeros((n, own_docs, packed.shape[1]), jnp.int32)
-        slots = lax.dynamic_update_slice(slots, packed[None], (me, 0, 0))
-        every = butterfly_sum(slots, n).reshape(docs, packed.shape[1])
+        spread = jnp.broadcast_to(packed[None], (n,) + packed.shape)
+        every = lax.all_to_all(spread, AXES, 0, 0, tiled=False).reshape(docs, packed.shape[1])
         all_tokens = every[:, : views * title].reshape(docs, views, title)
         all_positives = every[:, views * title : views * title + n_pos]
         all_labeled = every[:, views * title + n_pos]
@@ -41,7 +52,7 @@
         for position in range(title):
             tally = tally + (rows[:, position : position + 1] == codes[None, :]).astype(jnp.float32)
         partial = jnp.dot(tally.astype(jnp.bfloat16), vocab_table, preferred_element_type=jnp.float32)
-        pooled = (butterfly_sum(partial, n) * (1.0 / title)).astype(jnp.bfloat16)
+        pooled = (tree_sum(partial, n, n_label) * (1.0 / title)).astype(jnp.bfloat16)
 
         pre = jnp.dot(pooled, enc_weight, preferred_element_type=jnp.float32)
         inv_norm = lax.rsqrt(jnp.sum(pre * pre, axis=-1, keepdims=True) + 1e-06)
@@ -73,8 +84,10 @@
         new_log_rates = jnp.log(0.9 * rates + 0.1 * batch_rate)
 
         grad_local = jnp.dot(slope, label_matrix, preferred_element_type=jnp.float32)
-        extra = jnp.zeros((1, width), jnp.float32).at[0, 0].set(total_local).at[0, 1].set(loss_local)
-        summed = butterfly_sum(jnp.concatenate([grad_local, extra], axis=0), n)
+        lane = jnp.arange(width, dtype=jnp.int32)[None, :]
+        extra = jnp.where(lane == 0, total_local, jnp.where(lane == 1, loss_local, 0.0))
+        pad = jnp.zeros((n_label - 1 - (docs % n_label), width), jnp.float32)
+        summed = tree_sum(jnp.concatenate([grad_local, extra, pad], axis=0), n, n_label)
         total = summed[docs, 0]
         loss_sum = summed[docs, 1]
         grad_emb = summed[:docs] * (16.0 / total)
@@ -95,7 +108,7 @@
     n = mesh.shape["dp"] * mesh.shape["label"]
     assert n & (n - 1) == 0, "n not pow2"
     return jax.shard_map(
-        make_shards(n),
+        make_shards(n, mesh.shape["label"]),
         mesh=mesh,
         in_specs=(
             P(AXES, None, None),

time: 134 us -> 100 us (0.75)
  waiting for transfers between devices: 70.5 us -> 29.8 us
  blocking collectives: 0 us -> 21.7 us
  starting transfers between devices: 24.8 us -> 16 us
  other arithmetic: 14.1 us -> 11.4 us
  local copies, waits for them, and re-layouts: 5.74 us -> 3.95 us
  between operations: 6.09 us -> 4.72 us
    ppermute x15 -> x6, waiting for transfers between devices: 70.5 us -> 10.1 us  [the longest x2 5.55 us: tree_sum(): part = part + lax.ppermute(part, AXES, [(i, i ^ step) for i in range(n)])]
    ppermute x15 -> x6, starting transfers between devices: 24.8 us -> 1.85 us  [the longest x2 1.39 us: tree_sum(): part = part + lax.ppermute(part, AXES, [(i, i ^ step) for i in range(n)])]
    all_to_all x0 -> x2, blocking collectives: none -> 21.7 us  [the longest x1 11 us: tree_sum(): lax.all_to_all(x.reshape(n_label, rows // n_label, half), 'label', 0, 0,...]
    all_to_all x0 -> x3, waiting for transfers between devices: none -> 19.7 us  [the longest x1 7.55 us: tree_sum(): lax.all_to_all(x.reshape(n_label, rows // n_label, half), 'label', 0, 0,...]
    all_to_all x0 -> x3, starting transfers between devices: none -> 14.1 us  [the longest x1 7.33 us: shards(): lax.all_to_all(spread, AXES, 0, 0, tiled=False)]
    another operation x3 -> x0, other arithmetic: 3.84 us -> none
    scatter x2 -> x0, local copies, waits for them, and re-layouts: 1.39 us -> none  [shards(): jnp.zeros((1, width), jnp.float32).at[0, 0].set(total_local).at[0, 1]]
    select_n x0 -> x4, other arithmetic: none -> 1.35 us  [the longest x1 1.3 us: shards(): jnp.where(lane == 0, total_local, jnp.where(lane == 1, loss_local, 0.0))]
  transfers between devices with their start and end apart: 15 -> 9, of which waited for: 14 -> 9; matrix products, arithmetic and copies ran while one was open for 6% -> 5% of each run, Pallas kernels for 0% -> 0%
where the time goes in v3:
time: 100 us; the launch traced here: 99.7 us
  waiting for transfers between devices  29.8 us (30%)
  blocking collectives  21.7 us (22%)
  starting transfers between devices  16 us (16%)
  matrix products  12.2 us (12%)
  other arithmetic  11.4 us (11%)
  between operations  4.72 us (5%)
  local copies, waits for them, and re-layouts  3.95 us (4%)
    all_to_all x1, blocking collectives, tree_sum(): lax.all_to_all(x.reshape(n_label, rows // n_label, half), 'label', 0, 0,...  11 us
    all_to_all x1, blocking collectives, tree_sum(): x = lax.all_to_all(every, 'label', 0, 0, tiled=False).reshape(rows, half)  10.7 us
    all_to_all x1, waiting for transfers between devices, tree_sum(): lax.all_to_all(x.reshape(n_label, rows // n_label, half), 'label', 0, 0,...  7.55 us
    all_to_all x1, starting transfers between devices, shards(): lax.all_to_all(spread, AXES, 0, 0, tiled=False)  7.33 us
    all_to_all x1, waiting for transfers between devices, shards(): lax.all_to_all(spread, AXES, 0, 0, tiled=False)  7.15 us
    dot_general x1, matrix products, shards(): jnp.einsum('rk,lk->rl', emb, label_matrix, preferred_element_type=jnp.flo...  6.01 us
    ppermute x2, waiting for transfers between devices, tree_sum(): part = part + lax.ppermute(part, AXES, [(i, i ^ step) for i in range(n)])  5.55 us
    all_to_all x1, waiting for transfers between devices, tree_sum(): x = lax.all_to_all(every, 'label', 0, 0, tiled=False).reshape(rows, half)  4.96 us
  transfers between devices with their start and end apart: 9, of which 9 were waited for; matrix products, arithmetic and copies ran while one was open for 5% of the time, Pallas kernels for 0%

profile of v3, /device:TPU:0, one launch (start us, length us, event | category | flops | bytes accessed | tf_op | source)
XLA Modules:
  0.0 99.7 jit_solution(17212140465258019731)
XLA Ops:
  0.6 0.0 copy-start
  0.6 0.8 copy.17
  1.5 0.8 reshape.86
  2.2 0.8 pad_add_fusion
  3.0 0.6 broadcast_in_dim.27
  3.6 7.3 %all-to-all-start = ((s32[32,2,81]{2,1,0:T(2,128)}), s32[32,2,81]{2,1,0:T(2,128)S(1)}, u32[]{:S(2)}, u32[]{:S(2)}) async-start(s32[32,2,81]{2,1,0:T(2,128)} %broadcast_in_dim.27), calls=%async_computation | async-start | bytes 65536 | tf_op jit(solution)/shard_map/all_to_all | solution.py:44
  11.0 7.2 %all-to-all-done = s32[32,2,81]{2,1,0:T(2,128)S(1)} async-done(((s32[32,2,81]{2,1,0:T(2,128)}), s32[32,2,81]{2,1,0:T(2,128)S(1)}, u32[]{:S(2)}, u32[]{:S(2)}) %all-to-all-start) | async-done | bytes 20768 | tf_op jit(solution)/shard_map/all_to_all | solution.py:44
  18.2 0.1 copy.18
  18.3 0.1 sub.38
  18.4 1.7 %fusion.21 = f32[128,768]{1,0:T(8,128)S(1)} fusion(bf16[128,768]{1,0:T(8,128)(2,1)} %param.10, s32[128]{0:T(128)S(1)} %get-tuple-element.28, s32[128]{0:T(128)S(1)} %get-tuple-element.29, s32[128]{0:T(128)S(1)} %get-tuple-element.30, s32[128]{0:T(128)S(1)} %get-tuple-element.31, s32[128]{0:T(128)S(1)} %get-tuple-element.32, s32[128]{0:T(128)S(1)} %get-tuple-element.33, ...), kind=kOutput, calls=%fused_computation.72 | convolution fusion | flops 26738688 | bytes 606208 | tf_op jit(solution)/shard_map/dot_general | solution.py:54
  20.2 0.2 collective-permute-start
  20.4 1.3 %collective-permute-done = f32[128,384]{1,0:T(8,128)S(1)} collective-permute-done((f32[128,384]{1,0:T(8,128)S(1)}, f32[128,384]{1,0:T(8,128)S(1)}, u32[]{:S(2)}, u32[]{:S(2)}) %collective-permute-start) | collective-permute-done | bytes 196640 | tf_op jit(solution)/shard_map/ppermute | solution.py:15
  21.7 0.7 select_add_fusion
  22.4 3.4 %all-to-all-start.1 = ((f32[8,16,384]{2,1,0:T(8,128)}), f32[8,16,384]{2,1,0:T(8,128)S(1)}, u32[]{:S(2)}, u32[]{:S(2)}) async-start(f32[8,16,384]{2,1,0:T(8,128)} %bitcast.36), calls=%async_computation.1 | async-start | bytes 393216 | tf_op jit(solution)/shard_map/all_to_all | solution.py:17
  25.8 0.1 pad.6.clone
  25.9 0.8 slice_reduce_fusion.16
  26.7 7.5 %all-to-all-done.1 = f32[8,16,384]{2,1,0:T(8,128)S(1)} async-done(((f32[8,16,384]{2,1,0:T(8,128)}), f32[8,16,384]{2,1,0:T(8,128)S(1)}, u32[]{:S(2)}, u32[]{:S(2)}) %all-to-all-start.1) | async-done | bytes 196640 | tf_op jit(solution)/shard_map/all_to_all | solution.py:17
  34.3 0.7 collective-permute-start.1
  35.0 0.2 compare_reduce_fusion
  35.8 2.4 %collective-permute-done.1 = f32[16,384]{1,0:T(8,128)S(1)} collective-permute-done((f32[16,384]{1,0:T(8,128)S(1)}, f32[16,384]{1,0:T(8,128)S(1)}, u32[]{:S(2)}, u32[]{:S(2)}) %collective-permute-start.1) | collective-permute-done | bytes 24608 | tf_op jit(solution)/shard_map/ppermute | solution.py:21
  38.2 0.7 broadcast_in_dim.28
  38.9 3.4 %all-to-all-start.2 = ((f32[8,16,384]{2,1,0:T(8,128)}), f32[8,16,384]{2,1,0:T(8,128)S(1)}, u32[]{:S(2)}, u32[]{:S(2)}) async-start(f32[8,16,384]{2,1,0:T(8,128)} %broadcast_in_dim.28), calls=%async_computation.2 | async-start | bytes 393216 | tf_op jit(solution)/shard_map/all_to_all | solution.py:24
  42.3 2.7 %convert_reduce_fusion = f32[5120]{0:T(1024)S(1)} fusion(pred[64]{0:T(512)(128)(4,1)S(1)} %compare_reduce_fusion, s32[64]{0:T(128)S(1)} %get-tuple-element.6, s32[64]{0:T(128)S(1)} %get-tuple-element.7, s32[64]{0:T(128)S(1)} %get-tuple-element.8, s32[64]{0:T(128)S(1)} %get-tuple-element.9, s32[64]{0:T(128)S(1)} %get-tuple-element.10, ...), kind=kLoop, calls=%fused_computation.9 | loop fusion | flops 11136000 | bytes 45120 | tf_op jit(solution)/shard_map/reduce_sum | solution.py:83
  45.0 5.0 %all-to-all-done.2 = f32[8,16,384]{2,1,0:T(8,128)S(1)} async-done(((f32[8,16,384]{2,1,0:T(8,128)}), f32[8,16,384]{2,1,0:T(8,128)S(1)}, u32[]{:S(2)}, u32[]{:S(2)}) %all-to-all-start.2) | async-done | bytes 196640 | tf_op jit(solution)/shard_map/all_to_all | solution.py:24
  50.0 0.6 add_log_fusion
  50.6 0.8 collective-permute-done.2
  51.5 0.4 multiply_reduce_fusion
  51.9 0.0 slice-start
  51.9 0.1 broadcast_multiply_fusion
  52.0 0.0 slice-start.1
  52.0 6.0 %fusion = f32[128,5120]{1,0:T(8,128)S(1)} fusion(bf16[5120,768]{1,0:T(8,128)(2,1)} %param.12, f32[128,768]{1,0:T(8,128)S(1)} %broadcast_multiply_fusion), kind=kOutput, calls=%fused_computation.1 | convolution fusion | flops 1008041984 | bytes 10878976 | tf_op jit(solution)/shard_map/rk,lk->rl/dot_general | solution.py:63
  58.1 0.4 fusion.10
  58.5 3.4 %fusion.55 = (f32[]{:T(128)}, f32[]{:T(128)}, f32[64,5120]{1,0:T(8,128)S(1)}) fusion(f32[128,5120]{1,0:T(8,128)S(1)} %fusion, f32[5120]{0:T(1024)S(1)} %broadcast_multiply_fusion.1, f32[5120]{0:T(1024)S(1)} %get-tuple-element.26, s32[64]{0:T(128)S(1)} %get-tuple-element.6, s32[64]{0:T(128)S(1)} %get-tuple-element.7, s32[64]{0:T(128)S(1)} %get-tuple-element.8, ...), kind=kLoop, calls=%fused_computation.164 | loop fusion | flops 15728638 | bytes 3997768 | tf_op jit(solution)/shard_map/reduce_sum | solution.py:79
  61.9 1.5 %fusion.6 = f32[64,768]{1,0:T(8,128)S(1)} fusion(bf16[5120,768]{1,0:T(8,128)(2,1)S(1)} %bitcast.81, f32[64,5120]{1,0:T(8,128)S(1)} %get-tuple-element.22, f32[128,5120]{1,0:T(8,128)S(1)} %fusion), kind=kOutput, calls=%fused_computation.13 | convolution fusion | flops 504954880 | bytes 10682368 | tf_op jit(solution)/shard_map/dot_general | solution.py:86
  63.4 1.3 %compare_select_fusion.2 = f32[1,768]{1,0:T(1,128)S(1)} fusion(f32[]{:T(128)} %get-tuple-element.4, f32[]{:T(128)} %get-tuple-element.3), kind=kLoop, calls=%fused_computation.127 | loop fusion | flops 3072 | bytes 3080 | tf_op jit(solution)/shard_map/jit(_where)/select_n | solution.py:88
  64.7 0.1 maximum_maximum_fusion
  64.8 0.2 collective-permute-start.3
  65.0 1.2 %collective-permute-done.3 = f32[72,384]{1,0:T(8,128)S(1)} collective-permute-done((f32[72,384]{1,0:T(8,128)S(1)}, f32[72,384]{1,0:T(8,128)S(1)}, u32[]{:S(2)}, u32[]{:S(2)}) %collective-permute-start.3) | collective-permute-done | bytes 110624 | tf_op jit(solution)/shard_map/ppermute | solution.py:15
  66.2 11.0 %all_to_all.25 = f32[8,9,384]{2,1,0:T(8,128)S(1)} all-to-all(f32[8,9,384]{2,1,0:T(8,128)S(1)} %reshape.90), channel_id=1, replica_groups=mesh['dp'=4,'label'=8] {'label'}, dimensions={0} | all-to-all | bytes 221184 | tf_op jit(solution)/shard_map/all_to_all | solution.py:17
  77.2 0.7 collective-permute-start.4
  77.9 3.2 %collective-permute-done.4 = f32[9,384]{1,0:T(8,128)S(1)} collective-permute-done((f32[9,384]{1,0:T(8,128)S(1)}, f32[9,384]{1,0:T(8,128)S(1)}, u32[]{:S(2)}, u32[]{:S(2)}) %collective-permute-start.4) | collective-permute-done | bytes 13856 | tf_op jit(solution)/shard_map/ppermute | solution.py:21
  81.1 10.7 %all_to_all.26 = f32[8,9,384]{2,1,0:T(8,128)S(1)} all-to-all(f32[8,9,384]{2,1,0:T(8,128)S(1)} %broadcast_in_dim.35), channel_id=1, replica_groups=mesh['dp'=4,'label'=8] {'label'}, dimensions={0} | all-to-all | bytes 221184 | tf_op jit(solution)/shard_map/all_to_all | solution.py:24
  91.8 0.1 collective-permute-start.5
  91.9 0.1 slice.265
  92.0 1.2 %collective-permute-done.5 = f32[72,384]{1,0:T(8,128)S(1)} collective-permute-done((f32[72,384]{1,0:T(8,128)S(1)}, f32[72,384]{1,0:T(8,128)S(1)}, u32[]{:S(2)}, u32[]{:S(2)}) %collective-permute-start.5) | collective-permute-done | bytes 110624 | tf_op jit(solution)/shard_map/ppermute | solution.py:25
  93.3 0.6 fusion.56
  94.5 0.1 multiply_reduce_fusion.1
  96.0 2.6 %fusion.11 = f32[768,768]{1,0:T(8,128)} fusion(f32[128,768]{1,0:T(8,128)S(1)} %broadcast_multiply_fusion, f32[72,768]{1,0:T(8,128)S(1)} %maximum_select_fusion.1, bf16[128,768]{1,0:T(8,128)(2,1)S(1)} %fusion.9, f32[64]{0:T(128)S(1)} %slice.265, f32[64]{0:T(128)S(1)} %multiply_reduce_fusion.1, f32[]{:T(128)} %bitcast.39), kind=kOutput, calls=%fused_computation.23 | convolution fusion | flops 453181440 | bytes 2851844 | tf_op jit(solution)/shard_map/dk,dj->kj/dot_general | solution.py:98
  (27 shorter events, 0.3 us)
Async XLA Ops:
  0.6 50.8 %copy-start = (bf16[768,768]{1,0:T(8,128)(2,1)S(1)}, bf16[768,768]{1,0:T(8,128)(2,1)}, u32[]{:S(2)}) copy-start(bf16[768,768]{1,0:T(8,128)(2,1)} %param.11) | copy-start | bytes 3538948
  3.6 14.5 %all-to-all-start = ((s32[32,2,81]{2,1,0:T(2,128)}), s32[32,2,81]{2,1,0:T(2,128)S(1)}, u32[]{:S(2)}, u32[]{:S(2)}) async-start(s32[32,2,81]{2,1,0:T(2,128)} %broadcast_in_dim.27), calls=%async_computation | async-start | bytes 65536 | tf_op jit(solution)/shard_map/all_to_all | solution.py:44
  20.2 29.8 %copy-start.1 = (f32[5120]{0:T(1024)S(1)}, f32[5120]{0:T(1024)}, u32[]{:S(2)}) copy-start(f32[5120]{0:T(1024)} %param.13) | copy-start | bytes 61444
  20.2 1.5 %collective-permute-start = (f32[128,384]{1,0:T(8,128)S(1)}, f32[128,384]{1,0:T(8,128)S(1)}, u32[]{:S(2)}, u32[]{:S(2)}) collective-permute-start(f32[128,384]{1,0:T(8,128)S(1)} %slice_select_fusion), channel_id=1, source_target_pairs={{0,8},{1,9},{2,10},{3,11},{4,12},{5,13},{6,14},{7,15},{8,0},{9,1},... | collective-permute-start | bytes 589832 | tf_op jit(solution)/shard_map/ppermute | solution.py:15
  22.4 11.9 %all-to-all-start.1 = ((f32[8,16,384]{2,1,0:T(8,128)}), f32[8,16,384]{2,1,0:T(8,128)S(1)}, u32[]{:S(2)}, u32[]{:S(2)}) async-start(f32[8,16,384]{2,1,0:T(8,128)} %bitcast.36), calls=%async_computation.1 | async-start | bytes 393216 | tf_op jit(solution)/shard_map/all_to_all | solution.py:17
  34.3 3.9 %collective-permute-start.1 = (f32[16,384]{1,0:T(8,128)S(1)}, f32[16,384]{1,0:T(8,128)S(1)}, u32[]{:S(2)}, u32[]{:S(2)}) collective-permute-start(f32[16,384]{1,0:T(8,128)S(1)} %reduce_sum.81), channel_id=1, source_target_pairs={{0,16},{1,17},{2,18},{3,19},{4,20},{5,21},{6,22},{7,23},{8,24},{9,... | collective-permute-start | bytes 73736 | tf_op jit(solution)/shard_map/ppermute | solution.py:21
  38.9 11.1 %all-to-all-start.2 = ((f32[8,16,384]{2,1,0:T(8,128)}), f32[8,16,384]{2,1,0:T(8,128)S(1)}, u32[]{:S(2)}, u32[]{:S(2)}) async-start(f32[8,16,384]{2,1,0:T(8,128)} %broadcast_in_dim.28), calls=%async_computation.2 | async-start | bytes 393216 | tf_op jit(solution)/shard_map/all_to_all | solution.py:24
  50.0 1.4 %collective-permute-start.2 = (f32[128,384]{1,0:T(8,128)S(1)}, f32[128,384]{1,0:T(8,128)S(1)}, u32[]{:S(2)}, u32[]{:S(2)}) collective-permute-start(f32[128,384]{1,0:T(8,128)S(1)} %bitcast.85), channel_id=1, source_target_pairs={{0,8},{1,9},{2,10},{3,11},{4,12},{5,13},{6,14},{7,15},{8,0},{9,1},... | collective-permute-start | bytes 589832 | tf_op jit(solution)/shard_map/ppermute | solution.py:25
  51.9 9.9 %slice-start = ((s8[7864320]{0:T(1024)(128)(4,1)}), s8[4194304]{0:T(1024)(128)(4,1)S(1)}, s32[]{:S(2)}) async-start(s8[7864320]{0:T(1024)(128)(4,1)} %bitcast.80), calls=%async_computation.5 | async-start | bytes 8388608
  52.0 9.8 %slice-start.1 = ((s8[7864320]{0:T(1024)(128)(4,1)}), s8[3670016]{0:T(1024)(128)(4,1)S(1)}, s32[]{:S(2)}) async-start(s8[7864320]{0:T(1024)(128)(4,1)} %bitcast.80), calls=%async_computation.6 | async-start | bytes 7340032
  64.8 1.4 %collective-permute-start.3 = (f32[72,384]{1,0:T(8,128)S(1)}, f32[72,384]{1,0:T(8,128)S(1)}, u32[]{:S(2)}, u32[]{:S(2)}) collective-permute-start(f32[72,384]{1,0:T(8,128)S(1)} %slice_select_fusion.1), channel_id=1, source_target_pairs={{0,8},{1,9},{2,10},{3,11},{4,12},{5,13},{6,14},{7,15},{8,0},{9,1},... | collective-permute-start | bytes 331784 | tf_op jit(solution)/shard_map/ppermute | solution.py:15
  77.2 3.9 %collective-permute-start.4 = (f32[9,384]{1,0:T(8,128)S(1)}, f32[9,384]{1,0:T(8,128)S(1)}, u32[]{:S(2)}, u32[]{:S(2)}) collective-permute-start(f32[9,384]{1,0:T(8,128)S(1)} %reduce_sum.86), channel_id=1, source_target_pairs={{0,16},{1,17},{2,18},{3,19},{4,20},{5,21},{6,22},{7,23},{8,24},{9,... | collective-permute-start | bytes 41480 | tf_op jit(solution)/shard_map/ppermute | solution.py:21
  91.8 1.4 %collective-permute-start.5 = (f32[72,384]{1,0:T(8,128)S(1)}, f32[72,384]{1,0:T(8,128)S(1)}, u32[]{:S(2)}, u32[]{:S(2)}) collective-permute-start(f32[72,384]{1,0:T(8,128)S(1)} %reshape.91), channel_id=1, source_target_pairs={{0,8},{1,9},{2,10},{3,11},{4,12},{5,13},{6,14},{7,15},{8,0},{9,1},... | collective-permute-start | bytes 331784 | tf_op jit(solution)/shard_map/ppermute | solution.py:25

commit v4 on v3

--- a/solution.py
+++ b/solution.py
@@ -22,6 +22,22 @@
         step *= 2
     every = jnp.broadcast_to(part[None], (n_label,) + part.shape)
     x = lax.all_to_all(every, "label", 0, 0, tiled=False).reshape(rows, half)
+    other = lax.ppermute(x, AXES, swap)
+    return jnp.where(upper, jnp.concatenate([other, x], 1), jnp.concatenate([x, other], 1))
+
+
+def butterfly_sum(x, n, pair_step):
+    me = lax.axis_index(AXES)
+    upper = (me // pair_step) % 2 == 1
+    half = x.shape[1] // 2
+    low, high = x[:, :half], x[:, half:]
+    swap = [(i, i ^ pair_step) for i in range(n)]
+    x = jnp.where(upper, high, low) + lax.ppermute(jnp.where(upper, low, high), AXES, swap)
+    step = 1
+    while step < n:
+        if step != pair_step:
+            x = x + lax.ppermute(x, AXES, [(i, i ^ step) for i in range(n)])
+        step *= 2
     other = lax.ppermute(x, AXES, swap)
     return jnp.where(upper, jnp.concatenate([other, x], 1), jnp.concatenate([x, other], 1))
 
@@ -86,8 +102,7 @@
         grad_local = jnp.dot(slope, label_matrix, preferred_element_type=jnp.float32)
         lane = jnp.arange(width, dtype=jnp.int32)[None, :]
         extra = jnp.where(lane == 0, total_local, jnp.where(lane == 1, loss_local, 0.0))
-        pad = jnp.zeros((n_label - 1 - (docs % n_label), width), jnp.float32)
-        summed = tree_sum(jnp.concatenate([grad_local, extra, pad], axis=0), n, n_label)
+        summed = butterfly_sum(jnp.concatenate([grad_local, extra], axis=0), n, n_label)
         total = summed[docs, 0]
         loss_sum = summed[docs, 1]
         grad_emb = summed[:docs] * (16.0 / total)

time: 100 us -> 95.6 us (0.956)
  blocking collectives: 21.7 us -> 0 us
  waiting for transfers between devices: 29.8 us -> 46.4 us
    ppermute x0 -> x6, waiting for transfers between devices: none -> 22.2 us  [the longest x4 19.8 us: butterfly_sum(): x = x + lax.ppermute(x, AXES, [(i, i ^ step) for i in range(n)])]
    all_to_all x2 -> x0, blocking collectives: 21.7 us -> none  [the longest x1 11 us: tree_sum(): lax.all_to_all(x.reshape(n_label, rows // n_label, half), 'label', 0, 0,...]
    ppermute x2 -> x1, waiting for transfers between devices: 5.55 us -> 2.36 us  [tree_sum(): part = part + lax.ppermute(part, AXES, [(i, i ^ step) for i in range(n)])]
    ppermute x0 -> x6, starting transfers between devices: none -> 1.64 us  [the longest x4 1.36 us: butterfly_sum(): x = x + lax.ppermute(x, AXES, [(i, i ^ step) for i in range(n)])]
    ppermute x2 -> x1, waiting for transfers between devices: 2.04 us -> 0.81 us  [tree_sum(): other = lax.ppermute(x, AXES, swap)]
    ppermute x2 -> x1, waiting for transfers between devices: 2.51 us -> 1.33 us  [tree_sum(): lax.ppermute(jnp.where(upper, low, high), AXES, swap)]
  transfers between devices with their start and end apart: 9 -> 12, of which waited for: 9 -> 12; matrix products, arithmetic and copies ran while one was open for 5% -> 5% of each run, Pallas kernels for 0% -> 0%
where the time goes in v4:
time: 95.6 us; the launch traced here: 95.2 us
  waiting for transfers between devices  46.4 us (49%)
  starting transfers between devices  16.6 us (17%)
  matrix products  12.2 us (13%)
  other arithmetic  11.4 us (12%)
  between operations  4.71 us (5%)
  local copies, waits for them, and re-layouts  3.82 us (4%)
    ppermute x4, waiting for transfers between devices, butterfly_sum(): x = x + lax.ppermute(x, AXES, [(i, i ^ step) for i in range(n)])  19.8 us
    all_to_all x1, waiting for transfers between devices, tree_sum(): lax.all_to_all(x.reshape(n_label, rows // n_label, half), 'label', 0, 0,...  7.62 us
    all_to_all x1, starting transfers between devices, shards(): lax.all_to_all(spread, AXES, 0, 0, tiled=False)  7.33 us
    all_to_all x1, waiting for transfers between devices, shards(): lax.all_to_all(spread, AXES, 0, 0, tiled=False)  7.15 us
    dot_general x1, matrix products, shards(): jnp.einsum('rk,lk->rl', emb, label_matrix, preferred_element_type=jnp.flo...  6.01 us
    all_to_all x1, waiting for transfers between devices, tree_sum(): x = lax.all_to_all(every, 'label', 0, 0, tiled=False).reshape(rows, half)  4.96 us
    all_to_all x1, starting transfers between devices, tree_sum(): lax.all_to_all(x.reshape(n_label, rows // n_label, half), 'label', 0, 0,...  3.39 us
    all_to_all x1, starting transfers between devices, tree_sum(): x = lax.all_to_all(every, 'label', 0, 0, tiled=False).reshape(rows, half)  3.39 us
  transfers between devices with their start and end apart: 12, of which 12 were waited for; matrix products, arithmetic and copies ran while one was open for 5% of the time, Pallas kernels for 0%

profile of v4, /device:TPU:0, one launch (start us, length us, event | category | flops | bytes accessed | tf_op | source)
XLA Modules:
  0.0 95.2 jit_solution(8353993576909262695)
XLA Ops:
  0.6 0.0 copy-start
  0.6 0.9 reshape.79
  1.5 0.7 copy.17
  2.2 0.8 pad_add_fusion
  3.0 0.6 broadcast_in_dim.23
  3.6 7.3 %all-to-all-start = ((s32[32,2,81]{2,1,0:T(2,128)}), s32[32,2,81]{2,1,0:T(2,128)S(1)}, u32[]{:S(2)}, u32[]{:S(2)}) async-start(s32[32,2,81]{2,1,0:T(2,128)} %broadcast_in_dim.23), calls=%async_computation | async-start | bytes 65536 | tf_op jit(solution)/shard_map/all_to_all | solution.py:60
  11.0 7.2 %all-to-all-done = s32[32,2,81]{2,1,0:T(2,128)S(1)} async-done(((s32[32,2,81]{2,1,0:T(2,128)}), s32[32,2,81]{2,1,0:T(2,128)S(1)}, u32[]{:S(2)}, u32[]{:S(2)}) %all-to-all-start) | async-done | bytes 20768 | tf_op jit(solution)/shard_map/all_to_all | solution.py:60
  18.2 0.1 copy.18
  18.3 0.1 sub.38
  18.4 1.7 %fusion.22 = f32[128,768]{1,0:T(8,128)S(1)} fusion(bf16[128,768]{1,0:T(8,128)(2,1)} %param.10, s32[128]{0:T(128)S(1)} %get-tuple-element.28, s32[128]{0:T(128)S(1)} %get-tuple-element.29, s32[128]{0:T(128)S(1)} %get-tuple-element.30, s32[128]{0:T(128)S(1)} %get-tuple-element.31, s32[128]{0:T(128)S(1)} %get-tuple-element.32, s32[128]{0:T(128)S(1)} %get-tuple-element.33, ...), kind=kOutput, calls=%fused_computation.75 | convolution fusion | flops 26738688 | bytes 606208 | tf_op jit(solution)/shard_map/dot_general | solution.py:70
  20.2 0.2 collective-permute-start
  20.4 1.3 %collective-permute-done = f32[128,384]{1,0:T(8,128)S(1)} collective-permute-done((f32[128,384]{1,0:T(8,128)S(1)}, f32[128,384]{1,0:T(8,128)S(1)}, u32[]{:S(2)}, u32[]{:S(2)}) %collective-permute-start) | collective-permute-done | bytes 196640 | tf_op jit(solution)/shard_map/ppermute | solution.py:15
  21.7 0.7 select_add_fusion
  22.4 3.4 %all-to-all-start.1 = ((f32[8,16,384]{2,1,0:T(8,128)}), f32[8,16,384]{2,1,0:T(8,128)S(1)}, u32[]{:S(2)}, u32[]{:S(2)}) async-start(f32[8,16,384]{2,1,0:T(8,128)} %bitcast.36), calls=%async_computation.1 | async-start | bytes 393216 | tf_op jit(solution)/shard_map/all_to_all | solution.py:17
  25.8 0.8 slice_reduce_fusion.16
  26.6 7.6 %all-to-all-done.1 = f32[8,16,384]{2,1,0:T(8,128)S(1)} async-done(((f32[8,16,384]{2,1,0:T(8,128)}), f32[8,16,384]{2,1,0:T(8,128)S(1)}, u32[]{:S(2)}, u32[]{:S(2)}) %all-to-all-start.1) | async-done | bytes 196640 | tf_op jit(solution)/shard_map/all_to_all | solution.py:17
  34.3 0.7 collective-permute-start.1
  35.0 0.2 compare_reduce_fusion
  35.8 2.4 %collective-permute-done.1 = f32[16,384]{1,0:T(8,128)S(1)} collective-permute-done((f32[16,384]{1,0:T(8,128)S(1)}, f32[16,384]{1,0:T(8,128)S(1)}, u32[]{:S(2)}, u32[]{:S(2)}) %collective-permute-start.1) | collective-permute-done | bytes 24608 | tf_op jit(solution)/shard_map/ppermute | solution.py:21
  38.2 0.7 broadcast_in_dim.24
  38.9 3.4 %all-to-all-start.2 = ((f32[8,16,384]{2,1,0:T(8,128)}), f32[8,16,384]{2,1,0:T(8,128)S(1)}, u32[]{:S(2)}, u32[]{:S(2)}) async-start(f32[8,16,384]{2,1,0:T(8,128)} %broadcast_in_dim.24), calls=%async_computation.2 | async-start | bytes 393216 | tf_op jit(solution)/shard_map/all_to_all | solution.py:24
  42.3 2.7 %convert_reduce_fusion = f32[5120]{0:T(1024)S(1)} fusion(pred[64]{0:T(512)(128)(4,1)S(1)} %compare_reduce_fusion, s32[64]{0:T(128)S(1)} %get-tuple-element.6, s32[64]{0:T(128)S(1)} %get-tuple-element.7, s32[64]{0:T(128)S(1)} %get-tuple-element.8, s32[64]{0:T(128)S(1)} %get-tuple-element.9, s32[64]{0:T(128)S(1)} %get-tuple-element.10, ...), kind=kLoop, calls=%fused_computation.9 | loop fusion | flops 11136000 | bytes 45120 | tf_op jit(solution)/shard_map/reduce_sum | solution.py:99
  45.0 5.0 %all-to-all-done.2 = f32[8,16,384]{2,1,0:T(8,128)S(1)} async-done(((f32[8,16,384]{2,1,0:T(8,128)}), f32[8,16,384]{2,1,0:T(8,128)S(1)}, u32[]{:S(2)}, u32[]{:S(2)}) %all-to-all-start.2) | async-done | bytes 196640 | tf_op jit(solution)/shard_map/all_to_all | solution.py:24
  50.0 0.6 add_log_fusion
  50.6 0.8 collective-permute-done.2
  51.5 0.4 multiply_reduce_fusion
  51.9 0.1 broadcast_multiply_fusion
  52.1 6.0 %fusion = f32[128,5120]{1,0:T(8,128)S(1)} fusion(bf16[5120,768]{1,0:T(8,128)(2,1)} %param.12, f32[128,768]{1,0:T(8,128)S(1)} %broadcast_multiply_fusion), kind=kOutput, calls=%fused_computation.1 | convolution fusion | flops 1008041984 | bytes 10878976 | tf_op jit(solution)/shard_map/rk,lk->rl/dot_general | solution.py:79
  58.1 0.4 fusion.10
  58.5 3.4 %fusion.56 = (f32[]{:T(128)}, f32[]{:T(128)}, f32[64,5120]{1,0:T(8,128)S(1)}) fusion(f32[128,5120]{1,0:T(8,128)S(1)} %fusion, f32[5120]{0:T(1024)S(1)} %broadcast_multiply_fusion.1, f32[5120]{0:T(1024)S(1)} %get-tuple-element.26, s32[64]{0:T(128)S(1)} %get-tuple-element.6, s32[64]{0:T(128)S(1)} %get-tuple-element.7, s32[64]{0:T(128)S(1)} %get-tuple-element.8, ...), kind=kLoop, calls=%fused_computation.167 | loop fusion | flops 15728638 | bytes 3997768 | tf_op jit(solution)/shard_map/reduce_sum | solution.py:95
  61.9 1.5 %fusion.6 = f32[64,768]{1,0:T(8,128)S(1)} fusion(bf16[5120,768]{1,0:T(8,128)(2,1)S(1)} %bitcast.81, f32[64,5120]{1,0:T(8,128)S(1)} %get-tuple-element.22, f32[128,5120]{1,0:T(8,128)S(1)} %fusion), kind=kOutput, calls=%fused_computation.13 | convolution fusion | flops 504954880 | bytes 10682368 | tf_op jit(solution)/shard_map/dot_general | solution.py:102
  63.4 1.3 %compare_select_fusion.2 = f32[1,768]{1,0:T(1,128)S(1)} fusion(f32[]{:T(128)} %get-tuple-element.4, f32[]{:T(128)} %get-tuple-element.3), kind=kLoop, calls=%fused_computation.130 | loop fusion | flops 3072 | bytes 3080 | tf_op jit(solution)/shard_map/jit(_where)/select_n | solution.py:104
  64.7 0.2 collective-permute-start.3
  64.9 1.2 %collective-permute-done.3 = f32[65,384]{1,0:T(8,128)S(1)} collective-permute-done((f32[65,384]{1,0:T(8,128)S(1)}, f32[65,384]{1,0:T(8,128)S(1)}, u32[]{:S(2)}, u32[]{:S(2)}) %collective-permute-start.3) | collective-permute-done | bytes 99872 | tf_op jit(solution)/shard_map/ppermute | solution.py:35
  66.1 0.1 collective-permute-start.4
  66.2 5.1 %collective-permute-done.4 = f32[65,384]{1,0:T(8,128)S(1)} collective-permute-done((f32[65,384]{1,0:T(8,128)S(1)}, f32[65,384]{1,0:T(8,128)S(1)}, u32[]{:S(2)}, u32[]{:S(2)}) %collective-permute-start.4) | collective-permute-done | bytes 99872 | tf_op jit(solution)/shard_map/ppermute | solution.py:39
  71.3 0.1 collective-permute-start.5
  71.4 4.7 %collective-permute-done.5 = f32[65,384]{1,0:T(8,128)S(1)} collective-permute-done((f32[65,384]{1,0:T(8,128)S(1)}, f32[65,384]{1,0:T(8,128)S(1)}, u32[]{:S(2)}, u32[]{:S(2)}) %collective-permute-start.5) | collective-permute-done | bytes 99872 | tf_op jit(solution)/shard_map/ppermute | solution.py:39
  76.1 0.5 collective-permute-start.6
  76.6 5.8 %collective-permute-done.6 = f32[65,384]{1,0:T(8,128)S(1)} collective-permute-done((f32[65,384]{1,0:T(8,128)S(1)}, f32[65,384]{1,0:T(8,128)S(1)}, u32[]{:S(2)}, u32[]{:S(2)}) %collective-permute-start.6) | collective-permute-done | bytes 99872 | tf_op jit(solution)/shard_map/ppermute | solution.py:39
  82.5 0.7 collective-permute-start.7
  83.2 4.1 %collective-permute-done.7 = f32[65,384]{1,0:T(8,128)S(1)} collective-permute-done((f32[65,384]{1,0:T(8,128)S(1)}, f32[65,384]{1,0:T(8,128)S(1)}, u32[]{:S(2)}, u32[]{:S(2)}) %collective-permute-start.7) | collective-permute-done | bytes 99872 | tf_op jit(solution)/shard_map/ppermute | solution.py:39
  87.3 0.1 collective-permute-start.8
  87.4 0.1 slice.265
  87.5 1.2 %collective-permute-done.8 = f32[65,384]{1,0:T(8,128)S(1)} collective-permute-done((f32[65,384]{1,0:T(8,128)S(1)}, f32[65,384]{1,0:T(8,128)S(1)}, u32[]{:S(2)}, u32[]{:S(2)}) %collective-permute-start.8) | collective-permute-done | bytes 99872 | tf_op jit(solution)/shard_map/ppermute | solution.py:41
  88.7 0.6 fusion.57
  91.3 0.1 multiply_reduce_fusion.1
  91.5 2.6 %fusion.11 = f32[768,768]{1,0:T(8,128)} fusion(f32[128,768]{1,0:T(8,128)S(1)} %broadcast_multiply_fusion, f32[65,768]{1,0:T(8,128)S(1)} %maximum_select_fusion.1, bf16[128,768]{1,0:T(8,128)(2,1)S(1)} %fusion.9, f32[64]{0:T(128)S(1)} %slice.265, f32[64]{0:T(128)S(1)} %multiply_reduce_fusion.1, f32[]{:T(128)} %bitcast.39), kind=kOutput, calls=%fused_computation.24 | convolution fusion | flops 453181440 | bytes 2851844 | tf_op jit(solution)/shard_map/dk,dj->kj/dot_general | solution.py:113
  (27 shorter events, 0.3 us)
Async XLA Ops:
  0.6 50.9 %copy-start = (bf16[768,768]{1,0:T(8,128)(2,1)S(1)}, bf16[768,768]{1,0:T(8,128)(2,1)}, u32[]{:S(2)}) copy-start(bf16[768,768]{1,0:T(8,128)(2,1)} %param.11) | copy-start | bytes 3538948
  3.6 14.5 %all-to-all-start = ((s32[32,2,81]{2,1,0:T(2,128)}), s32[32,2,81]{2,1,0:T(2,128)S(1)}, u32[]{:S(2)}, u32[]{:S(2)}) async-start(s32[32,2,81]{2,1,0:T(2,128)} %broadcast_in_dim.23), calls=%async_computation | async-start | bytes 65536 | tf_op jit(solution)/shard_map/all_to_all | solution.py:60
  20.2 29.8 %copy-start.1 = (f32[5120]{0:T(1024)S(1)}, f32[5120]{0:T(1024)}, u32[]{:S(2)}) copy-start(f32[5120]{0:T(1024)} %param.13) | copy-start | bytes 61444
  20.2 1.5 %collective-permute-start = (f32[128,384]{1,0:T(8,128)S(1)}, f32[128,384]{1,0:T(8,128)S(1)}, u32[]{:S(2)}, u32[]{:S(2)}) collective-permute-start(f32[128,384]{1,0:T(8,128)S(1)} %slice_select_fusion), channel_id=1, source_target_pairs={{0,8},{1,9},{2,10},{3,11},{4,12},{5,13},{6,14},{7,15},{8,0},{9,1},... | collective-permute-start | bytes 589832 | tf_op jit(solution)/shard_map/ppermute | solution.py:15
  22.4 11.9 %all-to-all-start.1 = ((f32[8,16,384]{2,1,0:T(8,128)}), f32[8,16,384]{2,1,0:T(8,128)S(1)}, u32[]{:S(2)}, u32[]{:S(2)}) async-start(f32[8,16,384]{2,1,0:T(8,128)} %bitcast.36), calls=%async_computation.1 | async-start | bytes 393216 | tf_op jit(solution)/shard_map/all_to_all | solution.py:17
  34.3 3.9 %collective-permute-start.1 = (f32[16,384]{1,0:T(8,128)S(1)}, f32[16,384]{1,0:T(8,128)S(1)}, u32[]{:S(2)}, u32[]{:S(2)}) collective-permute-start(f32[16,384]{1,0:T(8,128)S(1)} %reduce_sum.72), channel_id=1, source_target_pairs={{0,16},{1,17},{2,18},{3,19},{4,20},{5,21},{6,22},{7,23},{8,24},{9,... | collective-permute-start | bytes 73736 | tf_op jit(solution)/shard_map/ppermute | solution.py:21
  38.9 11.1 %all-to-all-start.2 = ((f32[8,16,384]{2,1,0:T(8,128)}), f32[8,16,384]{2,1,0:T(8,128)S(1)}, u32[]{:S(2)}, u32[]{:S(2)}) async-start(f32[8,16,384]{2,1,0:T(8,128)} %broadcast_in_dim.24), calls=%async_computation.2 | async-start | bytes 393216 | tf_op jit(solution)/shard_map/all_to_all | solution.py:24
  50.0 1.4 %collective-permute-start.2 = (f32[128,384]{1,0:T(8,128)S(1)}, f32[128,384]{1,0:T(8,128)S(1)}, u32[]{:S(2)}, u32[]{:S(2)}) collective-permute-start(f32[128,384]{1,0:T(8,128)S(1)} %bitcast.85), channel_id=1, source_target_pairs={{0,8},{1,9},{2,10},{3,11},{4,12},{5,13},{6,14},{7,15},{8,0},{9,1},... | collective-permute-start | bytes 589832 | tf_op jit(solution)/shard_map/ppermute | solution.py:25
  51.9 9.9 %slice-start = ((s8[7864320]{0:T(1024)(128)(4,1)}), s8[4194304]{0:T(1024)(128)(4,1)S(1)}, s32[]{:S(2)}) async-start(s8[7864320]{0:T(1024)(128)(4,1)} %bitcast.80), calls=%async_computation.3 | async-start | bytes 8388608
  52.0 9.8 %slice-start.1 = ((s8[7864320]{0:T(1024)(128)(4,1)}), s8[3670016]{0:T(1024)(128)(4,1)S(1)}, s32[]{:S(2)}) async-start(s8[7864320]{0:T(1024)(128)(4,1)} %bitcast.80), calls=%async_computation.4 | async-start | bytes 7340032
  64.7 1.4 %collective-permute-start.3 = (f32[65,384]{1,0:T(8,128)S(1)}, f32[65,384]{1,0:T(8,128)S(1)}, u32[]{:S(2)}, u32[]{:S(2)}) collective-permute-start(f32[65,384]{1,0:T(8,128)S(1)} %broadcast_select_fusion), channel_id=1, source_target_pairs={{0,8},{1,9},{2,10},{3,11},{4,12},{5,13},{6,14},{7,15},{8,0},{9,1},... | collective-permute-start | bytes 299528 | tf_op jit(solution)/shard_map/ppermute | solution.py:35
  66.1 5.2 %collective-permute-start.4 = (f32[65,384]{1,0:T(8,128)S(1)}, f32[65,384]{1,0:T(8,128)S(1)}, u32[]{:S(2)}, u32[]{:S(2)}) collective-permute-start(f32[65,384]{1,0:T(8,128)S(1)} %select_add_fusion.1), channel_id=1, source_target_pairs={{0,1},{1,0},{2,3},{3,2},{4,5},{5,4},{6,7},{7,6},{8,9},{9,8},{10,11... | collective-permute-start | bytes 299528 | tf_op jit(solution)/shard_map/ppermute | solution.py:39
  71.3 4.8 %collective-permute-start.5 = (f32[65,384]{1,0:T(8,128)S(1)}, f32[65,384]{1,0:T(8,128)S(1)}, u32[]{:S(2)}, u32[]{:S(2)}) collective-permute-start(f32[65,384]{1,0:T(8,128)S(1)} %add.208), channel_id=1, source_target_pairs={{0,2},{1,3},{2,0},{3,1},{4,6},{5,7},{6,4},{7,5},{8,10},{9,11},{10,... | collective-permute-start | bytes 299528 | tf_op jit(solution)/shard_map/ppermute | solution.py:39
  76.1 6.3 %collective-permute-start.6 = (f32[65,384]{1,0:T(8,128)S(1)}, f32[65,384]{1,0:T(8,128)S(1)}, u32[]{:S(2)}, u32[]{:S(2)}) collective-permute-start(f32[65,384]{1,0:T(8,128)S(1)} %add.209), channel_id=1, source_target_pairs={{0,4},{1,5},{2,6},{3,7},{4,0},{5,1},{6,2},{7,3},{8,12},{9,13},{10,... | collective-permute-start | bytes 299528 | tf_op jit(solution)/shard_map/ppermute | solution.py:39
  82.5 4.8 %collective-permute-start.7 = (f32[65,384]{1,0:T(8,128)S(1)}, f32[65,384]{1,0:T(8,128)S(1)}, u32[]{:S(2)}, u32[]{:S(2)}) collective-permute-start(f32[65,384]{1,0:T(8,128)S(1)} %add.210), channel_id=1, source_target_pairs={{0,16},{1,17},{2,18},{3,19},{4,20},{5,21},{6,22},{7,23},{8,24},{9,... | collective-permute-start | bytes 299528 | tf_op jit(solution)/shard_map/ppermute | solution.py:39
  87.3 1.4 %collective-permute-start.8 = (f32[65,384]{1,0:T(8,128)S(1)}, f32[65,384]{1,0:T(8,128)S(1)}, u32[]{:S(2)}, u32[]{:S(2)}) collective-permute-start(f32[65,384]{1,0:T(8,128)S(1)} %add.211), channel_id=1, source_target_pairs={{0,8},{1,9},{2,10},{3,11},{4,12},{5,13},{6,14},{7,15},{8,0},{9,1},... | collective-permute-start | bytes 299528 | tf_op jit(solution)/shard_map/ppermute | solution.py:41

commit v5 on v4

--- a/solution.py
+++ b/solution.py
@@ -1,6 +1,8 @@
 import jax
 import jax.numpy as jnp
 from jax import lax
+from jax.experimental import pallas as pl
+from jax.experimental.pallas import tpu as pltpu
 from jax.sharding import PartitionSpec as P
 
 AXES = ("dp", "label")
@@ -42,6 +44,71 @@
     return jnp.where(upper, jnp.concatenate([other, x], 1), jnp.concatenate([x, other], 1))
 
 
+def label_kernel(emb_ref, lab_ref, rate_ref, pos_ref, flag_ref, grad_ref, cols_ref):
+    tile = pl.program_id(0)
+    docs = pos_ref.shape[0]
+    width = lab_ref.shape[0]
+    lab = lab_ref[...]
+    scores = (
+        lax.dot_general(emb_ref[...], lab, (((1,), (1,)), ((), ())), preferred_element_type=jnp.float32)
+        * 16.0
+        - 6.0
+    )
+    weak = scores[:docs]
+    strong = scores[docs:]
+    teacher = jax.nn.sigmoid(weak)
+    mean_teacher = jnp.sum(teacher, axis=0, keepdims=True) / docs
+    codes = tile * width + lax.broadcasted_iota(jnp.int32, (1, width), 1)
+    pos = pos_ref[...]
+    hit = pos[:, 0:1] == codes
+    for column in range(1, pos.shape[1]):
+        hit = hit | (pos[:, column : column + 1] == codes)
+    hit = hit.astype(jnp.float32)
+    flag = flag_ref[...]
+    target = jnp.where(flag > 0.5, hit, teacher * rate_ref[...] / mean_teacher)
+    softplus = jnp.maximum(strong, 0.0) + jnp.log1p(jnp.exp(-jnp.abs(strong)))
+    slope = (jax.nn.sigmoid(strong) - target).astype(jnp.bfloat16)
+    cols_ref[0:1, :] = jnp.sum(target, axis=0, keepdims=True)
+    cols_ref[1:2, :] = jnp.sum(softplus - target * strong, axis=0, keepdims=True)
+    cols_ref[2:3, :] = jnp.sum(flag * hit, axis=0, keepdims=True)
+    part = jnp.dot(slope, lab, preferred_element_type=jnp.float32)
+
+    @pl.when(tile == 0)
+    def _():
+        grad_ref[...] = part
+
+    @pl.when(tile > 0)
+    def _():
+        grad_ref[...] += part
+
+
+def label_pass(emb, label_matrix, rates, positives, flag):
+    rows, depth = emb.shape
+    docs, n_pos = positives.shape
+    labels = label_matrix.shape[0]
+    width = 1024 if labels % 1024 == 0 else labels
+    return pl.pallas_call(
+        label_kernel,
+        grid=(labels // width,),
+        in_specs=[
+            pl.BlockSpec((rows, depth), lambda i: (0, 0)),
+            pl.BlockSpec((width, depth), lambda i: (i, 0)),
+            pl.BlockSpec((1, width), lambda i: (0, i)),
+            pl.BlockSpec((docs, n_pos), lambda i: (0, 0)),
+            pl.BlockSpec((docs, 1), lambda i: (0, 0)),
+        ],
+        out_specs=[
+            pl.BlockSpec((docs, depth), lambda i: (0, 0)),
+            pl.BlockSpec((3, width), lambda i: (0, i)),
+        ],
+        out_shape=[
+            jax.ShapeDtypeStruct((docs, depth), jnp.float32),
+            jax.ShapeDtypeStruct((3, labels), jnp.float32),
+        ],
+        compiler_params=pltpu.CompilerParams(dimension_semantics=("arbitrary",)),
+    )(emb, label_matrix, rates, positives, flag)
+
+
 def make_shards(n, n_label):
     def shards(
         token_ids, labeled, positive_ids, vocab_table, enc_weight, label_matrix, label_log_rates
@@ -75,31 +142,17 @@
         unit = pre * inv_norm
         emb = unit.astype(jnp.bfloat16)
 
-        scores = (
-            jnp.einsum("rk,lk->rl", emb, label_matrix, preferred_element_type=jnp.float32) * 16.0
-            - 6.0
+        rates = jnp.exp(label_log_rates)
+        flag = (all_labeled == 1).astype(jnp.float32)[:, None]
+        grad_local, cols = label_pass(
+            emb, label_matrix, rates[None, :], all_positives - me * label_rows, flag
         )
-        weak = scores[:docs]
-        strong = scores[docs:]
-        teacher = jax.nn.sigmoid(weak)
-        mean_teacher = jnp.mean(teacher, axis=0)
-        label_codes = me * label_rows + jnp.arange(label_rows, dtype=jnp.int32)
-        hit = jnp.zeros((docs, label_rows), dtype=bool)
-        for column in range(n_pos):
-            hit = hit | (all_positives[:, column : column + 1] == label_codes[None, :])
-        flag = (all_labeled == 1)[:, None]
-        rates = jnp.exp(label_log_rates)
-        target = jnp.where(
-            flag, hit.astype(jnp.float32), teacher * rates[None, :] / mean_teacher[None, :]
-        )
-        total_local = jnp.sum(target)
-        loss_local = jnp.sum(jax.nn.softplus(strong) - target * strong)
-        slope = (jax.nn.sigmoid(strong) - target).astype(jnp.bfloat16)
+        total_local = jnp.sum(cols[0])
+        loss_local = jnp.sum(cols[1])
         labeled_count = jnp.sum(all_labeled).astype(jnp.float32)
-        batch_rate = jnp.sum((flag & hit).astype(jnp.float32), axis=0) / labeled_count
+        batch_rate = cols[2] / labeled_count
         new_log_rates = jnp.log(0.9 * rates + 0.1 * batch_rate)
 
-        grad_local = jnp.dot(slope, label_matrix, preferred_element_type=jnp.float32)
         lane = jnp.arange(width, dtype=jnp.int32)[None, :]
         extra = jnp.where(lane == 0, total_local, jnp.where(lane == 1, loss_local, 0.0))
         summed = butterfly_sum(jnp.concatenate([grad_local, extra], axis=0), n, n_label)

time: 95.6 us -> 95.5 us (level)
  blocking collectives: 0 us -> 10.9 us
  Pallas kernels: 0 us -> 8.35 us
  matrix products: 12.2 us -> 4.72 us
  waiting for transfers between devices: 46.4 us -> 39.1 us
  starting transfers between devices: 16.6 us -> 13.2 us
  other arithmetic: 11.4 us -> 9.49 us
    all_to_all x0 -> x1, blocking collectives: none -> 10.9 us  [tree_sum(): lax.all_to_all(x.reshape(n_label, rows // n_label, half), 'label', 0, 0,...]
    pallas_call x0 -> x1, Pallas kernels: none -> 8.35 us  [label_pass(): pl.pallas_call(label_kernel, grid=(labels // width,), in_specs=[pl.BlockS...]
    all_to_all x1 -> x0, waiting for transfers between devices: 7.62 us -> none  [tree_sum(): lax.all_to_all(x.reshape(n_label, rows // n_label, half), 'label', 0, 0,...]
    dot_general x2 -> x0, matrix products: 7.51 us -> none  [the longest x1 6.01 us: shards(): jnp.einsum('rk,lk->rl', emb, label_matrix, preferred_element_type=jnp.flo...]
    reduce_sum x3 -> x1, other arithmetic: 6.52 us -> 1.7 us  [shards(): total_local = jnp.sum(cols[0])]
    all_to_all x1 -> x0, starting transfers between devices: 3.39 us -> none  [tree_sum(): lax.all_to_all(x.reshape(n_label, rows // n_label, half), 'label', 0, 0,...]
    convert_element_type x0 -> x2, other arithmetic: none -> 1.48 us  [the longest x1 0.8 us: shards(): emb = unit.astype(jnp.bfloat16)]
  transfers between devices with their start and end apart: 12 -> 11, of which waited for: 12 -> 11; matrix products, arithmetic and copies ran while one was open for 5% -> 4% of each run, Pallas kernels for 0% -> 0%
where the time goes in v5:
time: 95.5 us; the launch traced here: 94.8 us
  waiting for transfers between devices  39.1 us (41%)
  starting transfers between devices  13.2 us (14%)
  blocking collectives  10.9 us (11%)
  other arithmetic  9.49 us (10%)
  Pallas kernels  8.35 us (9%)
  matrix products  4.72 us (5%)
  between operations  4.63 us (5%)
  local copies, waits for them, and re-layouts  4.42 us (5%)
    ppermute x4, waiting for transfers between devices, butterfly_sum(): x = x + lax.ppermute(x, AXES, [(i, i ^ step) for i in range(n)])  19.8 us
    all_to_all x1, blocking collectives, tree_sum(): lax.all_to_all(x.reshape(n_label, rows // n_label, half), 'label', 0, 0,...  10.9 us
    pallas_call x1, Pallas kernels, label_pass(): pl.pallas_call(label_kernel, grid=(labels // width,), in_specs=[pl.BlockS...  8.35 us
    all_to_all x1, starting transfers between devices, shards(): lax.all_to_all(spread, AXES, 0, 0, tiled=False)  7.33 us
    all_to_all x1, waiting for transfers between devices, shards(): lax.all_to_all(spread, AXES, 0, 0, tiled=False)  7.15 us
    all_to_all x1, waiting for transfers between devices, tree_sum(): x = lax.all_to_all(every, 'label', 0, 0, tiled=False).reshape(rows, half)  5.05 us
    all_to_all x1, starting transfers between devices, tree_sum(): x = lax.all_to_all(every, 'label', 0, 0, tiled=False).reshape(rows, half)  3.39 us
    ppermute x1, waiting for transfers between devices, tree_sum(): part = part + lax.ppermute(part, AXES, [(i, i ^ step) for i in range(n)])  3.2 us
  transfers between devices with their start and end apart: 11, of which 11 were waited for; matrix products, arithmetic and copies ran while one was open for 4% of the time, Pallas kernels for 0%

profile of v5, /device:TPU:0, one launch (start us, length us, event | category | flops | bytes accessed | tf_op | source)
XLA Modules:
  0.0 94.8 jit_solution(11037427313186930781)
XLA Ops:
  0.6 0.0 copy-start
  0.6 0.9 reshape.75
  1.5 0.7 copy.14
  2.2 0.8 pad_add_fusion
  3.0 0.6 broadcast_in_dim.18
  3.6 7.3 %all-to-all-start = ((s32[32,2,81]{2,1,0:T(2,128)}), s32[32,2,81]{2,1,0:T(2,128)S(1)}, u32[]{:S(2)}, u32[]{:S(2)}) async-start(s32[32,2,81]{2,1,0:T(2,128)} %broadcast_in_dim.18), calls=%async_computation | async-start | bytes 65536 | tf_op jit(solution)/shard_map/all_to_all | solution.py:127
  11.0 7.2 %all-to-all-done = s32[32,2,81]{2,1,0:T(2,128)S(1)} async-done(((s32[32,2,81]{2,1,0:T(2,128)}), s32[32,2,81]{2,1,0:T(2,128)S(1)}, u32[]{:S(2)}, u32[]{:S(2)}) %all-to-all-start) | async-done | bytes 20768 | tf_op jit(solution)/shard_map/all_to_all | solution.py:127
  18.2 0.1 copy.15
  18.3 0.1 sub.34
  18.4 1.7 %fusion.12 = f32[128,768]{1,0:T(8,128)S(1)} fusion(bf16[128,768]{1,0:T(8,128)(2,1)} %param.10, s32[128]{0:T(128)S(1)} %get-tuple-element.15, s32[128]{0:T(128)S(1)} %get-tuple-element.16, s32[128]{0:T(128)S(1)} %get-tuple-element.17, s32[128]{0:T(128)S(1)} %get-tuple-element.18, s32[128]{0:T(128)S(1)} %get-tuple-element.19, s32[128]{0:T(128)S(1)} %get-tuple-element.20, ...), kind=kOutput, calls=%fused_computation.58 | convolution fusion | flops 26738688 | bytes 606208 | tf_op jit(solution)/shard_map/dot_general | solution.py:137
  20.2 0.0 copy-start.1
  20.2 0.2 collective-permute-start
  20.4 1.3 %collective-permute-done = f32[128,384]{1,0:T(8,128)S(1)} collective-permute-done((f32[128,384]{1,0:T(8,128)S(1)}, f32[128,384]{1,0:T(8,128)S(1)}, u32[]{:S(2)}, u32[]{:S(2)}) %collective-permute-start) | collective-permute-done | bytes 196640 | tf_op jit(solution)/shard_map/ppermute | solution.py:17
  21.7 10.9 %all_to_all.15 = f32[8,16,384]{2,1,0:T(8,128)S(1)} all-to-all(f32[8,16,384]{2,1,0:T(8,128)S(1)} %bitcast.86), channel_id=1, replica_groups=mesh['dp'=4,'label'=8] {'label'}, dimensions={0} | all-to-all | bytes 393216 | tf_op jit(solution)/shard_map/all_to_all | solution.py:19
  32.7 0.7 collective-permute-start.1
  33.4 3.2 %collective-permute-done.1 = f32[16,384]{1,0:T(8,128)S(1)} collective-permute-done((f32[16,384]{1,0:T(8,128)S(1)}, f32[16,384]{1,0:T(8,128)S(1)}, u32[]{:S(2)}, u32[]{:S(2)}) %collective-permute-start.1) | collective-permute-done | bytes 24608 | tf_op jit(solution)/shard_map/ppermute | solution.py:23
  36.6 0.7 broadcast_in_dim.19
  37.3 3.4 %all-to-all-start.2 = ((f32[8,16,384]{2,1,0:T(8,128)}), f32[8,16,384]{2,1,0:T(8,128)S(1)}, u32[]{:S(2)}, u32[]{:S(2)}) async-start(f32[8,16,384]{2,1,0:T(8,128)} %broadcast_in_dim.19), calls=%async_computation.2 | async-start | bytes 393216 | tf_op jit(solution)/shard_map/all_to_all | solution.py:26
  40.7 0.6 exp.3
  41.3 0.7 slice_reduce_fusion
  42.7 0.7 compare_convert_fusion.flag_ref
  43.3 5.1 %all-to-all-done.2 = f32[8,16,384]{2,1,0:T(8,128)S(1)} async-done(((f32[8,16,384]{2,1,0:T(8,128)}), f32[8,16,384]{2,1,0:T(8,128)S(1)}, u32[]{:S(2)}, u32[]{:S(2)}) %all-to-all-start.2) | async-done | bytes 196640 | tf_op jit(solution)/shard_map/all_to_all | solution.py:26
  48.4 0.7 slice_subtract_fusion.pos_ref
  49.1 0.8 collective-permute-done.2
  49.9 0.4 multiply_reduce_fusion
  50.3 0.8 fusion.45
  51.1 8.4 %shard_map.94 = (f32[64,768]{1,0:T(8,128)}, f32[3,5120]{1,0:T(4,128)}) custom-call(bf16[128,768]{1,0:T(8,128)(2,1)} %get-tuple-element.9.emb_ref, bf16[5120,768]{1,0:T(8,128)(2,1)} %lab_ref.1, f32[1,5120]{1,0:T(1,128)} %bitcast.88, s32[64,16]{1,0:T(8,128)} %slice_subtract_fusion.pos_ref, f32[64,1]{1,0:T(8,128)} %compare_convert_fusion.flag_ref), custom_call_target="tpu_custom_call" | custom-call | tf_op jit(solution)/shard_map/pallas_call | solution.py:90
  59.5 1.7 %slice_reduce_fusion.2 = (f32[]{:T(128)}, f32[]{:T(128)}, f32[1,5120]{1,0:T(1,128)S(1)}) fusion(f32[3,5120]{1,0:T(4,128)} %get-tuple-element.6, f32[]{:T(128)S(6)} %convert_element_type.149), kind=kLoop, calls=%fused_computation.98 | loop fusion | flops 20478 | bytes 81932 | tf_op jit(solution)/shard_map/reduce_sum | solution.py:150
  61.2 1.3 %compare_select_fusion.1 = f32[1,768]{1,0:T(1,128)S(1)} fusion(f32[]{:T(128)} %get-tuple-element.8, f32[]{:T(128)} %get-tuple-element.7), kind=kLoop, calls=%fused_computation.100 | loop fusion | flops 3072 | bytes 3080 | tf_op jit(solution)/shard_map/jit(_where)/select_n | solution.py:157
  62.5 1.0 %broadcast_select_fusion = f32[65,384]{1,0:T(8,128)S(1)} fusion(pred[]{:T(512)S(6)} %eq.522, f32[1,768]{1,0:T(1,128)S(1)} %compare_select_fusion.1, f32[64,768]{1,0:T(8,128)} %get-tuple-element.5), kind=kLoop, calls=%fused_computation.57 | loop fusion | flops 74880 | bytes 299521 | tf_op jit(solution)/shard_map/jit(_where)/select_n | solution.py:37
  63.4 0.2 collective-permute-start.3
  63.6 1.2 %collective-permute-done.3 = f32[65,384]{1,0:T(8,128)S(1)} collective-permute-done((f32[65,384]{1,0:T(8,128)S(1)}, f32[65,384]{1,0:T(8,128)S(1)}, u32[]{:S(2)}, u32[]{:S(2)}) %collective-permute-start.3) | collective-permute-done | bytes 99872 | tf_op jit(solution)/shard_map/ppermute | solution.py:37
  64.8 1.0 %select_add_fusion.1 = f32[65,384]{1,0:T(8,128)S(1)} fusion(f32[65,384]{1,0:T(8,128)S(1)} %collective-permute-done.3, pred[]{:T(512)S(6)} %eq.522, f32[1,768]{1,0:T(1,128)S(1)} %compare_select_fusion.1, f32[64,768]{1,0:T(8,128)} %get-tuple-element.5), kind=kLoop, calls=%fused_computation.19 | loop fusion | flops 99840 | bytes 399361 | tf_op jit(solution)/shard_map/add | solution.py:37
  65.8 0.1 collective-permute-start.4
  65.9 5.1 %collective-permute-done.4 = f32[65,384]{1,0:T(8,128)S(1)} collective-permute-done((f32[65,384]{1,0:T(8,128)S(1)}, f32[65,384]{1,0:T(8,128)S(1)}, u32[]{:S(2)}, u32[]{:S(2)}) %collective-permute-start.4) | collective-permute-done | bytes 99872 | tf_op jit(solution)/shard_map/ppermute | solution.py:41
  71.0 0.1 collective-permute-start.5
  71.1 4.7 %collective-permute-done.5 = f32[65,384]{1,0:T(8,128)S(1)} collective-permute-done((f32[65,384]{1,0:T(8,128)S(1)}, f32[65,384]{1,0:T(8,128)S(1)}, u32[]{:S(2)}, u32[]{:S(2)}) %collective-permute-start.5) | collective-permute-done | bytes 99872 | tf_op jit(solution)/shard_map/ppermute | solution.py:41
  75.8 0.5 collective-permute-start.6
  76.3 5.9 %collective-permute-done.6 = f32[65,384]{1,0:T(8,128)S(1)} collective-permute-done((f32[65,384]{1,0:T(8,128)S(1)}, f32[65,384]{1,0:T(8,128)S(1)}, u32[]{:S(2)}, u32[]{:S(2)}) %collective-permute-start.6) | collective-permute-done | bytes 99872 | tf_op jit(solution)/shard_map/ppermute | solution.py:41
  82.2 0.7 collective-permute-start.7
  82.9 4.1 %collective-permute-done.7 = f32[65,384]{1,0:T(8,128)S(1)} collective-permute-done((f32[65,384]{1,0:T(8,128)S(1)}, f32[65,384]{1,0:T(8,128)S(1)}, u32[]{:S(2)}, u32[]{:S(2)}) %collective-permute-start.7) | collective-permute-done | bytes 99872 | tf_op jit(solution)/shard_map/ppermute | solution.py:41
  87.0 0.1 collective-permute-start.8
  87.1 0.6 add_log_fusion
  87.7 0.1 slice.191
  87.8 0.6 collective-permute-done.8
  88.4 0.6 fusion.46
  91.0 0.1 multiply_reduce_fusion.1
  91.1 2.6 %fusion.2 = f32[768,768]{1,0:T(8,128)} fusion(f32[128,768]{1,0:T(8,128)S(1)} %get-tuple-element.10, f32[65,768]{1,0:T(8,128)S(1)} %maximum_select_fusion.1, bf16[128,768]{1,0:T(8,128)(2,1)S(1)} %fusion.1, f32[64]{0:T(128)S(1)} %slice.191, f32[64]{0:T(128)S(1)} %multiply_reduce_fusion.1, f32[]{:T(128)} %bitcast.40), kind=kOutput, calls=%fused_computation.8 | convolution fusion | flops 453181440 | bytes 2851844 | tf_op jit(solution)/shard_map/dk,dj->kj/dot_general | solution.py:166
  (18 shorter events, 0.3 us)
Async XLA Ops:
  0.6 49.2 %copy-start = (bf16[768,768]{1,0:T(8,128)(2,1)S(1)}, bf16[768,768]{1,0:T(8,128)(2,1)}, u32[]{:S(2)}) copy-start(bf16[768,768]{1,0:T(8,128)(2,1)} %param.11) | copy-start | bytes 3538948
  3.6 14.5 %all-to-all-start = ((s32[32,2,81]{2,1,0:T(2,128)}), s32[32,2,81]{2,1,0:T(2,128)S(1)}, u32[]{:S(2)}, u32[]{:S(2)}) async-start(s32[32,2,81]{2,1,0:T(2,128)} %broadcast_in_dim.18), calls=%async_computation | async-start | bytes 65536 | tf_op jit(solution)/shard_map/all_to_all | solution.py:127
  20.2 20.5 %copy-start.1 = (f32[5120]{0:T(1024)S(1)}, f32[5120]{0:T(1024)}, u32[]{:S(2)}) copy-start(f32[5120]{0:T(1024)} %param.13) | copy-start | bytes 61444
  20.2 1.5 %collective-permute-start = (f32[128,384]{1,0:T(8,128)S(1)}, f32[128,384]{1,0:T(8,128)S(1)}, u32[]{:S(2)}, u32[]{:S(2)}) collective-permute-start(f32[128,384]{1,0:T(8,128)S(1)} %slice_select_fusion), channel_id=1, source_target_pairs={{0,8},{1,9},{2,10},{3,11},{4,12},{5,13},{6,14},{7,15},{8,0},{9,1},... | collective-permute-start | bytes 589832 | tf_op jit(solution)/shard_map/ppermute | solution.py:17
  32.7 3.9 %collective-permute-start.1 = (f32[16,384]{1,0:T(8,128)S(1)}, f32[16,384]{1,0:T(8,128)S(1)}, u32[]{:S(2)}, u32[]{:S(2)}) collective-permute-start(f32[16,384]{1,0:T(8,128)S(1)} %reduce_sum.54), channel_id=1, source_target_pairs={{0,16},{1,17},{2,18},{3,19},{4,20},{5,21},{6,22},{7,23},{8,24},{9,... | collective-permute-start | bytes 73736 | tf_op jit(solution)/shard_map/ppermute | solution.py:23
  37.3 11.1 %all-to-all-start.2 = ((f32[8,16,384]{2,1,0:T(8,128)}), f32[8,16,384]{2,1,0:T(8,128)S(1)}, u32[]{:S(2)}, u32[]{:S(2)}) async-start(f32[8,16,384]{2,1,0:T(8,128)} %broadcast_in_dim.19), calls=%async_computation.2 | async-start | bytes 393216 | tf_op jit(solution)/shard_map/all_to_all | solution.py:26
  48.4 1.4 %collective-permute-start.2 = (f32[128,384]{1,0:T(8,128)S(1)}, f32[128,384]{1,0:T(8,128)S(1)}, u32[]{:S(2)}, u32[]{:S(2)}) collective-permute-start(f32[128,384]{1,0:T(8,128)S(1)} %bitcast.84), channel_id=1, source_target_pairs={{0,8},{1,9},{2,10},{3,11},{4,12},{5,13},{6,14},{7,15},{8,0},{9,1},... | collective-permute-start | bytes 589832 | tf_op jit(solution)/shard_map/ppermute | solution.py:27
  63.4 1.4 %collective-permute-start.3 = (f32[65,384]{1,0:T(8,128)S(1)}, f32[65,384]{1,0:T(8,128)S(1)}, u32[]{:S(2)}, u32[]{:S(2)}) collective-permute-start(f32[65,384]{1,0:T(8,128)S(1)} %broadcast_select_fusion), channel_id=1, source_target_pairs={{0,8},{1,9},{2,10},{3,11},{4,12},{5,13},{6,14},{7,15},{8,0},{9,1},... | collective-permute-start | bytes 299528 | tf_op jit(solution)/shard_map/ppermute | solution.py:37
  65.8 5.2 %collective-permute-start.4 = (f32[65,384]{1,0:T(8,128)S(1)}, f32[65,384]{1,0:T(8,128)S(1)}, u32[]{:S(2)}, u32[]{:S(2)}) collective-permute-start(f32[65,384]{1,0:T(8,128)S(1)} %select_add_fusion.1), channel_id=1, source_target_pairs={{0,1},{1,0},{2,3},{3,2},{4,5},{5,4},{6,7},{7,6},{8,9},{9,8},{10,11... | collective-permute-start | bytes 299528 | tf_op jit(solution)/shard_map/ppermute | solution.py:41
  71.0 4.8 %collective-permute-start.5 = (f32[65,384]{1,0:T(8,128)S(1)}, f32[65,384]{1,0:T(8,128)S(1)}, u32[]{:S(2)}, u32[]{:S(2)}) collective-permute-start(f32[65,384]{1,0:T(8,128)S(1)} %add.182), channel_id=1, source_target_pairs={{0,2},{1,3},{2,0},{3,1},{4,6},{5,7},{6,4},{7,5},{8,10},{9,11},{10,... | collective-permute-start | bytes 299528 | tf_op jit(solution)/shard_map/ppermute | solution.py:41
  75.8 6.3 %collective-permute-start.6 = (f32[65,384]{1,0:T(8,128)S(1)}, f32[65,384]{1,0:T(8,128)S(1)}, u32[]{:S(2)}, u32[]{:S(2)}) collective-permute-start(f32[65,384]{1,0:T(8,128)S(1)} %add.183), channel_id=1, source_target_pairs={{0,4},{1,5},{2,6},{3,7},{4,0},{5,1},{6,2},{7,3},{8,12},{9,13},{10,... | collective-permute-start | bytes 299528 | tf_op jit(solution)/shard_map/ppermute | solution.py:41
  82.2 4.8 %collective-permute-start.7 = (f32[65,384]{1,0:T(8,128)S(1)}, f32[65,384]{1,0:T(8,128)S(1)}, u32[]{:S(2)}, u32[]{:S(2)}) collective-permute-start(f32[65,384]{1,0:T(8,128)S(1)} %add.184), channel_id=1, source_target_pairs={{0,16},{1,17},{2,18},{3,19},{4,20},{5,21},{6,22},{7,23},{8,24},{9,... | collective-permute-start | bytes 299528 | tf_op jit(solution)/shard_map/ppermute | solution.py:41
  87.0 1.4 %collective-permute-start.8 = (f32[65,384]{1,0:T(8,128)S(1)}, f32[65,384]{1,0:T(8,128)S(1)}, u32[]{:S(2)}, u32[]{:S(2)}) collective-permute-start(f32[65,384]{1,0:T(8,128)S(1)} %add.185), channel_id=1, source_target_pairs={{0,8},{1,9},{2,10},{3,11},{4,12},{5,13},{6,14},{7,15},{8,0},{9,1},... | collective-permute-start | bytes 299528 | tf_op jit(solution)/shard_map/ppermute | solution.py:43

commit v6 on v4

--- a/solution.py
+++ b/solution.py
@@ -1,6 +1,8 @@
 import jax
 import jax.numpy as jnp
 from jax import lax
+from jax.experimental import pallas as pl
+from jax.experimental.pallas import tpu as pltpu
 from jax.sharding import PartitionSpec as P
 
 AXES = ("dp", "label")
@@ -26,13 +28,92 @@
     return jnp.where(upper, jnp.concatenate([other, x], 1), jnp.concatenate([x, other], 1))
 
 
-def butterfly_sum(x, n, pair_step):
+def label_kernel(place_ref, emb_ref, lab_ref, rate_ref, ints_ref, keep_ref, send_ref, rate_out_ref):
+    tile = pl.program_id(0)
+    upper = place_ref[0] == 1
+    base = place_ref[1]
+    docs, half = send_ref.shape[0] - 8, send_ref.shape[1]
+    width = lab_ref.shape[0]
+    n_pos = ints_ref.shape[1] - 1
+    lab = lab_ref[...]
+    scores = (
+        lax.dot_general(emb_ref[...], lab, (((1,), (1,)), ((), ())), preferred_element_type=jnp.float32)
+        * 16.0
+        - 6.0
+    )
+    weak = scores[:docs]
+    strong = scores[docs:]
+    teacher = jax.nn.sigmoid(weak)
+    mean_teacher = jnp.sum(teacher, axis=0, keepdims=True) / docs
+    codes = base + tile * width + lax.broadcasted_iota(jnp.int32, (1, width), 1)
+    ints = ints_ref[...]
+    hit = ints[:, 0:1] == codes
+    for column in range(1, n_pos):
+        hit = hit | (ints[:, column : column + 1] == codes)
+    hit = hit.astype(jnp.float32)
+    flag = (ints[:, n_pos : n_pos + 1] == 1).astype(jnp.float32)
+    target = jnp.where(flag > 0.5, hit, teacher * rate_ref[...] / mean_teacher)
+    softplus = jnp.maximum(strong, 0.0) + jnp.log1p(jnp.exp(-jnp.abs(strong)))
+    slope = (jax.nn.sigmoid(strong) - target).astype(jnp.bfloat16)
+    rate_out_ref[...] = jnp.sum(flag * hit, axis=0, keepdims=True)
+    part = jnp.dot(slope, lab, preferred_element_type=jnp.float32)
+    low, high = part[:, :half], part[:, half:]
+    lane = lax.broadcasted_iota(jnp.int32, (8, half), 1)
+    row = lax.broadcasted_iota(jnp.int32, (8, half), 0)
+    total = jnp.sum(target)
+    loss = jnp.sum(softplus - target * strong)
+    extra = jnp.where(row == 0, jnp.where(lane == 0, total, jnp.where(lane == 1, loss, 0.0)), 0.0)
+    keep = jnp.concatenate([jnp.where(upper, high, low), jnp.where(upper, 0.0, extra)], axis=0)
+    send = jnp.concatenate([jnp.where(upper, low, high), jnp.where(upper, extra, 0.0)], axis=0)
+
+    @pl.when(tile == 0)
+    def _():
+        keep_ref[...] = keep
+        send_ref[...] = send
+
+    @pl.when(tile > 0)
+    def _():
+        keep_ref[...] += keep
+        send_ref[...] += send
+
+
+def label_pass(place, emb, label_matrix, rates, ints):
+    rows, depth = emb.shape
+    docs = ints.shape[0]
+    labels = label_matrix.shape[0]
+    width = 1024 if labels % 1024 == 0 else labels
+    half = depth // 2
+    return pl.pallas_call(
+        label_kernel,
+        grid_spec=pltpu.PrefetchScalarGridSpec(
+            num_scalar_prefetch=1,
+            grid=(labels // width,),
+            in_specs=[
+                pl.BlockSpec((rows, depth), lambda i, p: (0, 0)),
+                pl.BlockSpec((width, depth), lambda i, p: (i, 0)),
+                pl.BlockSpec((1, width), lambda i, p: (0, i)),
+                pl.BlockSpec(ints.shape, lambda i, p: (0, 0)),
+            ],
+            out_specs=[
+                pl.BlockSpec((docs + 8, half), lambda i, p: (0, 0)),
+                pl.BlockSpec((docs + 8, half), lambda i, p: (0, 0)),
+                pl.BlockSpec((1, width), lambda i, p: (0, i)),
+            ],
+        ),
+        out_shape=[
+            jax.ShapeDtypeStruct((docs + 8, half), jnp.float32),
+            jax.ShapeDtypeStruct((docs + 8, half), jnp.float32),
+            jax.ShapeDtypeStruct((1, labels), jnp.float32),
+        ],
+        compiler_params=pltpu.CompilerParams(dimension_semantics=("arbitrary",)),
+    )(place, emb, label_matrix, rates, ints)
+
+
+def split_sum(keep, send, n, pair_step):
     me = lax.axis_index(AXES)
     upper = (me // pair_step) % 2 == 1
-    half = x.shape[1] // 2
-    low, high = x[:, :half], x[:, half:]
     swap = [(i, i ^ pair_step) for i in range(n)]
-    x = jnp.where(upper, high, low) + lax.ppermute(jnp.where(upper, low, high), AXES, swap)
+    x = keep + lax.ppermute(send, AXES, swap)
     step = 1
     while step < n:
         if step != pair_step:
@@ -59,7 +140,6 @@
         spread = jnp.broadcast_to(packed[None], (n,) + packed.shape)
         every = lax.all_to_all(spread, AXES, 0, 0, tiled=False).reshape(docs, packed.shape[1])
         all_tokens = every[:, : views * title].reshape(docs, views, title)
-        all_positives = every[:, views * title : views * title + n_pos]
         all_labeled = every[:, views * title + n_pos]
 
         rows = jnp.transpose(all_tokens, (1, 0, 2)).reshape(views * docs, title) - me * vocab_rows
@@ -75,34 +155,17 @@
         unit = pre * inv_norm
         emb = unit.astype(jnp.bfloat16)
 
-        scores = (
-            jnp.einsum("rk,lk->rl", emb, label_matrix, preferred_element_type=jnp.float32) * 16.0
-            - 6.0
+        rates = jnp.exp(label_log_rates)
+        upper = (me // n_label) % 2
+        place = jnp.stack([upper, me * label_rows]).astype(jnp.int32)
+        keep, send, hits = label_pass(
+            place, emb, label_matrix, rates[None, :], every[:, views * title :]
         )
-        weak = scores[:docs]
-        strong = scores[docs:]
-        teacher = jax.nn.sigmoid(weak)
-        mean_teacher = jnp.mean(teacher, axis=0)
-        label_codes = me * label_rows + jnp.arange(label_rows, dtype=jnp.int32)
-        hit = jnp.zeros((docs, label_rows), dtype=bool)
-        for column in range(n_pos):
-            hit = hit | (all_positives[:, column : column + 1] == label_codes[None, :])
-        flag = (all_labeled == 1)[:, None]
-        rates = jnp.exp(label_log_rates)
-        target = jnp.where(
-            flag, hit.astype(jnp.float32), teacher * rates[None, :] / mean_teacher[None, :]
-        )
-        total_local = jnp.sum(target)
-        loss_local = jnp.sum(jax.nn.softplus(strong) - target * strong)
-        slope = (jax.nn.sigmoid(strong) - target).astype(jnp.bfloat16)
         labeled_count = jnp.sum(all_labeled).astype(jnp.float32)
-        batch_rate = jnp.sum((flag & hit).astype(jnp.float32), axis=0) / labeled_count
+        batch_rate = hits[0] / labeled_count
         new_log_rates = jnp.log(0.9 * rates + 0.1 * batch_rate)
 
-        grad_local = jnp.dot(slope, label_matrix, preferred_element_type=jnp.float32)
-        lane = jnp.arange(width, dtype=jnp.int32)[None, :]
-        extra = jnp.where(lane == 0, total_local, jnp.where(lane == 1, loss_local, 0.0))
-        summed = butterfly_sum(jnp.concatenate([grad_local, extra], axis=0), n, n_label)
+        summed = split_sum(keep, send, n, n_label)
         total = summed[docs, 0]
         loss_sum = summed[docs, 1]
         grad_emb = summed[:docs] * (16.0 / total)

time: 95.6 us -> 92 us (0.962)
  blocking collectives: 0 us -> 21.7 us
  waiting for transfers between devices: 46.4 us -> 32.1 us
  Pallas kernels: 0 us -> 9.11 us
  matrix products: 12.2 us -> 4.71 us
  other arithmetic: 11.4 us -> 4.73 us
  starting transfers between devices: 16.6 us -> 10.2 us
    all_to_all x0 -> x2, blocking collectives: none -> 21.7 us  [the longest x1 10.9 us: tree_sum(): lax.all_to_all(x.reshape(n_label, rows // n_label, half), 'label', 0, 0,...]
    all_to_all x2 -> x0, waiting for transfers between devices: 12.6 us -> none  [the longest x1 7.62 us: tree_sum(): lax.all_to_all(x.reshape(n_label, rows // n_label, half), 'label', 0, 0,...]
    pallas_call x0 -> x1, Pallas kernels: none -> 9.11 us  [label_pass(): pl.pallas_call(label_kernel, grid_spec=pltpu.PrefetchScalarGridSpec(num_s...]
    dot_general x2 -> x0, matrix products: 7.51 us -> none  [the longest x1 6.01 us: shards(): jnp.einsum('rk,lk->rl', emb, label_matrix, preferred_element_type=jnp.flo...]
    all_to_all x2 -> x0, starting transfers between devices: 6.78 us -> none  [the longest x1 3.39 us: tree_sum(): lax.all_to_all(x.reshape(n_label, rows // n_label, half), 'label', 0, 0,...]
    reduce_sum x3 -> x0, other arithmetic: 6.52 us -> none  [the longest x1 3.38 us: shards(): total_local = jnp.sum(target)]
    ppermute x6, waiting for transfers between devices: 22.2 us -> 20.4 us  [the longest x4 18.6 us: split_sum(): x = x + lax.ppermute(x, AXES, [(i, i ^ step) for i in range(n)])]
    select_n x3 -> x1, other arithmetic: 1.33 us -> 0.02 us  [split_sum(): jnp.where(upper, jnp.concatenate([other, x], 1), jnp.concatenate([x, othe...]
  transfers between devices with their start and end apart: 12 -> 10, of which waited for: 12 -> 9; matrix products, arithmetic and copies ran while one was open for 5% -> 4% of each run, Pallas kernels for 0% -> 0%
where the time goes in v6:
time: 92 us; the launch traced here: 91.6 us
  waiting for transfers between devices  32.1 us (35%)
  blocking collectives  21.7 us (24%)
  starting transfers between devices  10.2 us (11%)
  Pallas kernels  9.11 us (10%)
  other arithmetic  4.73 us (5%)
  matrix products  4.71 us (5%)
  between operations  4.62 us (5%)
  local copies, waits for them, and re-layouts  4.43 us (5%)
    ppermute x4, waiting for transfers between devices, split_sum(): x = x + lax.ppermute(x, AXES, [(i, i ^ step) for i in range(n)])  18.6 us
    all_to_all x1, blocking collectives, tree_sum(): lax.all_to_all(x.reshape(n_label, rows // n_label, half), 'label', 0, 0,...  10.9 us
    all_to_all x1, blocking collectives, tree_sum(): x = lax.all_to_all(every, 'label', 0, 0, tiled=False).reshape(rows, half)  10.7 us
    pallas_call x1, Pallas kernels, label_pass(): pl.pallas_call(label_kernel, grid_spec=pltpu.PrefetchScalarGridSpec(num_s...  9.11 us
    all_to_all x1, starting transfers between devices, shards(): lax.all_to_all(spread, AXES, 0, 0, tiled=False)  7.33 us
    all_to_all x1, waiting for transfers between devices, shards(): lax.all_to_all(spread, AXES, 0, 0, tiled=False)  7.15 us
    ppermute x1, waiting for transfers between devices, tree_sum(): part = part + lax.ppermute(part, AXES, [(i, i ^ step) for i in range(n)])  3.2 us
    dot_general x1, matrix products, shards(): jnp.einsum('dk,dj->kj', pooled[docs:].astype(jnp.float32), grad_pre, prec...  2.56 us
  transfers between devices with their start and end apart: 10, of which 9 were waited for; matrix products, arithmetic and copies ran while one was open for 4% of the time, Pallas kernels for 0%

profile of v6, /device:TPU:0, one launch (start us, length us, event | category | flops | bytes accessed | tf_op | source)
XLA Modules:
  0.0 91.6 jit_solution(4941194224464339267)
XLA Ops:
  0.6 0.0 copy-start
  0.6 0.9 reshape.51
  1.5 0.7 copy.14
  2.2 0.8 pad_add_fusion
  3.0 0.6 broadcast_in_dim.9
  3.6 7.3 %all-to-all-start = ((s32[32,2,81]{2,1,0:T(2,128)}), s32[32,2,81]{2,1,0:T(2,128)S(1)}, u32[]{:S(2)}, u32[]{:S(2)}) async-start(s32[32,2,81]{2,1,0:T(2,128)} %broadcast_in_dim.9), calls=%async_computation | async-start | bytes 65536 | tf_op jit(solution)/shard_map/all_to_all | solution.py:141
  11.0 7.2 %all-to-all-done = s32[32,2,81]{2,1,0:T(2,128)S(1)} async-done(((s32[32,2,81]{2,1,0:T(2,128)}), s32[32,2,81]{2,1,0:T(2,128)S(1)}, u32[]{:S(2)}, u32[]{:S(2)}) %all-to-all-start) | async-done | bytes 20768 | tf_op jit(solution)/shard_map/all_to_all | solution.py:141
  18.2 0.1 copy.15
  18.3 0.1 sub.29
  18.4 1.7 %fusion.11 = f32[128,768]{1,0:T(8,128)S(1)} fusion(bf16[128,768]{1,0:T(8,128)(2,1)} %param.10, s32[128]{0:T(128)S(1)} %get-tuple-element.14, s32[128]{0:T(128)S(1)} %get-tuple-element.15, s32[128]{0:T(128)S(1)} %get-tuple-element.16, s32[128]{0:T(128)S(1)} %get-tuple-element.17, s32[128]{0:T(128)S(1)} %get-tuple-element.18, s32[128]{0:T(128)S(1)} %get-tuple-element.19, ...), kind=kOutput, calls=%fused_computation.52 | convolution fusion | flops 26738688 | bytes 606208 | tf_op jit(solution)/shard_map/dot_general | solution.py:150
  20.2 0.0 copy-start.1
  20.2 0.2 collective-permute-start
  20.4 1.3 %collective-permute-done = f32[128,384]{1,0:T(8,128)S(1)} collective-permute-done((f32[128,384]{1,0:T(8,128)S(1)}, f32[128,384]{1,0:T(8,128)S(1)}, u32[]{:S(2)}, u32[]{:S(2)}) %collective-permute-start) | collective-permute-done | bytes 196640 | tf_op jit(solution)/shard_map/ppermute | solution.py:17
  21.7 10.9 %all_to_all.15 = f32[8,16,384]{2,1,0:T(8,128)S(1)} all-to-all(f32[8,16,384]{2,1,0:T(8,128)S(1)} %bitcast.84), channel_id=1, replica_groups=mesh['dp'=4,'label'=8] {'label'}, dimensions={0} | all-to-all | bytes 393216 | tf_op jit(solution)/shard_map/all_to_all | solution.py:19
  32.7 0.7 collective-permute-start.1
  33.4 3.2 %collective-permute-done.1 = f32[16,384]{1,0:T(8,128)S(1)} collective-permute-done((f32[16,384]{1,0:T(8,128)S(1)}, f32[16,384]{1,0:T(8,128)S(1)}, u32[]{:S(2)}, u32[]{:S(2)}) %collective-permute-start.1) | collective-permute-done | bytes 24608 | tf_op jit(solution)/shard_map/ppermute | solution.py:23
  36.6 10.7 %all_to_all.16 = f32[8,16,384]{2,1,0:T(8,128)S(1)} all-to-all(f32[8,16,384]{2,1,0:T(8,128)S(1)} %broadcast_in_dim.10), channel_id=1, replica_groups=mesh['dp'=4,'label'=8] {'label'}, dimensions={0} | all-to-all | bytes 393216 | tf_op jit(solution)/shard_map/all_to_all | solution.py:26
  47.3 0.0 collective-permute-start.2
  47.3 0.0 copy-done.1
  47.3 0.6 exp.3
  47.9 0.6 pad_add_fusion.1.place_ref
  48.5 0.7 slice.208.ints_ref
  49.2 0.0 collective-permute-done.2
  49.2 0.0 copy-done
  49.3 0.4 multiply_reduce_fusion
  49.7 0.8 fusion.44
  50.5 9.1 %shard_map.94 = (f32[72,384]{1,0:T(8,128)}, f32[72,384]{1,0:T(8,128)}, f32[1,5120]{1,0:T(1,128)}) custom-call(s32[2]{0:T(128)} %pad_add_fusion.1.place_ref, bf16[128,768]{1,0:T(8,128)(2,1)} %get-tuple-element.9.emb_ref, bf16[5120,768]{1,0:T(8,128)(2,1)} %lab_ref.1, f32[1,5120]{1,0:T(1,128)} %bitcast.89, s32[64,17]{1,0:T(8,128)} %slice.208.ints_ref), custom_call_target="tpu_custom_call" | custom-call | tf_op jit(solution)/shard_map/pallas_call | solution.py:86
  59.6 0.0 copy-start.2
  59.6 0.6 collective-permute-start.3
  60.2 1.2 %collective-permute-done.3 = f32[72,384]{1,0:T(8,128)S(1)} collective-permute-done((f32[72,384]{1,0:T(8,128)}, f32[72,384]{1,0:T(8,128)S(1)}, u32[]{:S(2)}, u32[]{:S(2)}) %collective-permute-start.3) | collective-permute-done | bytes 110624 | tf_op jit(solution)/shard_map/ppermute | solution.py:116
  61.3 0.9 add.182
  62.3 0.1 collective-permute-start.4
  62.4 5.3 %collective-permute-done.4 = f32[72,384]{1,0:T(8,128)S(1)} collective-permute-done((f32[72,384]{1,0:T(8,128)S(1)}, f32[72,384]{1,0:T(8,128)S(1)}, u32[]{:S(2)}, u32[]{:S(2)}) %collective-permute-start.4) | collective-permute-done | bytes 110624 | tf_op jit(solution)/shard_map/ppermute | solution.py:120
  67.7 0.1 collective-permute-start.5
  67.7 4.7 %collective-permute-done.5 = f32[72,384]{1,0:T(8,128)S(1)} collective-permute-done((f32[72,384]{1,0:T(8,128)S(1)}, f32[72,384]{1,0:T(8,128)S(1)}, u32[]{:S(2)}, u32[]{:S(2)}) %collective-permute-start.5) | collective-permute-done | bytes 110624 | tf_op jit(solution)/shard_map/ppermute | solution.py:120
  72.5 0.5 collective-permute-start.6
  73.0 0.7 slice_reduce_fusion
  74.4 4.5 %collective-permute-done.6 = f32[72,384]{1,0:T(8,128)S(1)} collective-permute-done((f32[72,384]{1,0:T(8,128)S(1)}, f32[72,384]{1,0:T(8,128)S(1)}, u32[]{:S(2)}, u32[]{:S(2)}) %collective-permute-start.6) | collective-permute-done | bytes 110624 | tf_op jit(solution)/shard_map/ppermute | solution.py:120
  78.9 0.7 collective-permute-start.7
  79.6 0.0 copy-done.2
  79.6 4.1 %collective-permute-done.7 = f32[72,384]{1,0:T(8,128)S(1)} collective-permute-done((f32[72,384]{1,0:T(8,128)S(1)}, f32[72,384]{1,0:T(8,128)S(1)}, u32[]{:S(2)}, u32[]{:S(2)}) %collective-permute-start.7) | collective-permute-done | bytes 110624 | tf_op jit(solution)/shard_map/ppermute | solution.py:120
  83.7 0.1 collective-permute-start.8
  83.8 0.6 add_log_fusion
  84.4 0.1 slice.171
  84.5 0.6 collective-permute-done.8
  85.1 0.6 fusion.45
  87.7 0.1 multiply_reduce_fusion.1
  87.9 2.6 %fusion.2 = f32[768,768]{1,0:T(8,128)} fusion(f32[128,768]{1,0:T(8,128)S(1)} %get-tuple-element.10, f32[72,768]{1,0:T(8,128)S(1)} %maximum_select_fusion.1, bf16[128,768]{1,0:T(8,128)(2,1)S(1)} %fusion.1, f32[64]{0:T(128)S(1)} %slice.171, f32[64]{0:T(128)S(1)} %multiply_reduce_fusion.1, f32[]{:T(128)} %bitcast.42), kind=kOutput, calls=%fused_computation.6 | convolution fusion | flops 453181440 | bytes 2851844 | tf_op jit(solution)/shard_map/dk,dj->kj/dot_general | solution.py:176
  (17 shorter events, 0.3 us)
Async XLA Ops:
  0.6 48.6 %copy-start = (bf16[768,768]{1,0:T(8,128)(2,1)S(1)}, bf16[768,768]{1,0:T(8,128)(2,1)}, u32[]{:S(2)}) copy-start(bf16[768,768]{1,0:T(8,128)(2,1)} %param.11) | copy-start | bytes 3538948
  3.6 14.5 %all-to-all-start = ((s32[32,2,81]{2,1,0:T(2,128)}), s32[32,2,81]{2,1,0:T(2,128)S(1)}, u32[]{:S(2)}, u32[]{:S(2)}) async-start(s32[32,2,81]{2,1,0:T(2,128)} %broadcast_in_dim.9), calls=%async_computation | async-start | bytes 65536 | tf_op jit(solution)/shard_map/all_to_all | solution.py:141
  20.2 27.2 %copy-start.1 = (f32[5120]{0:T(1024)S(1)}, f32[5120]{0:T(1024)}, u32[]{:S(2)}) copy-start(f32[5120]{0:T(1024)} %param.13) | copy-start | bytes 61444
  20.2 1.5 %collective-permute-start = (f32[128,384]{1,0:T(8,128)S(1)}, f32[128,384]{1,0:T(8,128)S(1)}, u32[]{:S(2)}, u32[]{:S(2)}) collective-permute-start(f32[128,384]{1,0:T(8,128)S(1)} %slice_select_fusion), channel_id=1, source_target_pairs={{0,8},{1,9},{2,10},{3,11},{4,12},{5,13},{6,14},{7,15},{8,0},{9,1},... | collective-permute-start | bytes 589832 | tf_op jit(solution)/shard_map/ppermute | solution.py:17
  32.7 3.9 %collective-permute-start.1 = (f32[16,384]{1,0:T(8,128)S(1)}, f32[16,384]{1,0:T(8,128)S(1)}, u32[]{:S(2)}, u32[]{:S(2)}) collective-permute-start(f32[16,384]{1,0:T(8,128)S(1)} %reduce_sum.36), channel_id=1, source_target_pairs={{0,16},{1,17},{2,18},{3,19},{4,20},{5,21},{6,22},{7,23},{8,24},{9,... | collective-permute-start | bytes 73736 | tf_op jit(solution)/shard_map/ppermute | solution.py:23
  47.3 1.9 %collective-permute-start.2 = (f32[128,384]{1,0:T(8,128)S(1)}, f32[128,384]{1,0:T(8,128)S(1)}, u32[]{:S(2)}, u32[]{:S(2)}) collective-permute-start(f32[128,384]{1,0:T(8,128)S(1)} %bitcast.82), channel_id=1, source_target_pairs={{0,8},{1,9},{2,10},{3,11},{4,12},{5,13},{6,14},{7,15},{8,0},{9,1},... | collective-permute-start | bytes 589832 | tf_op jit(solution)/shard_map/ppermute | solution.py:27
  59.6 20.0 %copy-start.2 = (f32[1,5120]{1,0:T(1,128)S(1)}, f32[1,5120]{1,0:T(1,128)}, u32[]{:S(2)}) copy-start(f32[1,5120]{1,0:T(1,128)} %get-tuple-element.8) | copy-start | bytes 61444
  59.6 1.7 %collective-permute-start.3 = (f32[72,384]{1,0:T(8,128)}, f32[72,384]{1,0:T(8,128)S(1)}, u32[]{:S(2)}, u32[]{:S(2)}) collective-permute-start(f32[72,384]{1,0:T(8,128)} %get-tuple-element.7), channel_id=1, source_target_pairs={{0,8},{1,9},{2,10},{3,11},{4,12},{5,13},{6,14},{7,15},{8,0},{9,1},... | collective-permute-start | bytes 331784 | tf_op jit(solution)/shard_map/ppermute | solution.py:116
  62.3 5.4 %collective-permute-start.4 = (f32[72,384]{1,0:T(8,128)S(1)}, f32[72,384]{1,0:T(8,128)S(1)}, u32[]{:S(2)}, u32[]{:S(2)}) collective-permute-start(f32[72,384]{1,0:T(8,128)S(1)} %add.182), channel_id=1, source_target_pairs={{0,1},{1,0},{2,3},{3,2},{4,5},{5,4},{6,7},{7,6},{8,9},{9,8},{10,11... | collective-permute-start | bytes 331784 | tf_op jit(solution)/shard_map/ppermute | solution.py:120
  67.7 4.8 %collective-permute-start.5 = (f32[72,384]{1,0:T(8,128)S(1)}, f32[72,384]{1,0:T(8,128)S(1)}, u32[]{:S(2)}, u32[]{:S(2)}) collective-permute-start(f32[72,384]{1,0:T(8,128)S(1)} %add.183), channel_id=1, source_target_pairs={{0,2},{1,3},{2,0},{3,1},{4,6},{5,7},{6,4},{7,5},{8,10},{9,11},{10,... | collective-permute-start | bytes 331784 | tf_op jit(solution)/shard_map/ppermute | solution.py:120
  72.5 6.4 %collective-permute-start.6 = (f32[72,384]{1,0:T(8,128)S(1)}, f32[72,384]{1,0:T(8,128)S(1)}, u32[]{:S(2)}, u32[]{:S(2)}) collective-permute-start(f32[72,384]{1,0:T(8,128)S(1)} %add.184), channel_id=1, source_target_pairs={{0,4},{1,5},{2,6},{3,7},{4,0},{5,1},{6,2},{7,3},{8,12},{9,13},{10,... | collective-permute-start | bytes 331784 | tf_op jit(solution)/shard_map/ppermute | solution.py:120
  78.9 4.8 %collective-permute-start.7 = (f32[72,384]{1,0:T(8,128)S(1)}, f32[72,384]{1,0:T(8,128)S(1)}, u32[]{:S(2)}, u32[]{:S(2)}) collective-permute-start(f32[72,384]{1,0:T(8,128)S(1)} %add.185), channel_id=1, source_target_pairs={{0,16},{1,17},{2,18},{3,19},{4,20},{5,21},{6,22},{7,23},{8,24},{9,... | collective-permute-start | bytes 331784 | tf_op jit(solution)/shard_map/ppermute | solution.py:120
  83.7 1.4 %collective-permute-start.8 = (f32[72,384]{1,0:T(8,128)S(1)}, f32[72,384]{1,0:T(8,128)S(1)}, u32[]{:S(2)}, u32[]{:S(2)}) collective-permute-start(f32[72,384]{1,0:T(8,128)S(1)} %add.186), channel_id=1, source_target_pairs={{0,8},{1,9},{2,10},{3,11},{4,12},{5,13},{6,14},{7,15},{8,0},{9,1},... | collective-permute-start | bytes 331784 | tf_op jit(solution)/shard_map/ppermute | solution.py:122

commit v7 on v6

--- a/solution.py
+++ b/solution.py
@@ -1,3 +1,5 @@
+import functools
+
 import jax
 import jax.numpy as jnp
 from jax import lax
@@ -28,13 +30,13 @@
     return jnp.where(upper, jnp.concatenate([other, x], 1), jnp.concatenate([x, other], 1))
 
 
-def label_kernel(place_ref, emb_ref, lab_ref, rate_ref, ints_ref, keep_ref, send_ref, rate_out_ref):
+def label_kernel(first, place_ref, emb_ref, lab_ref, rate_ref, ints_ref, keep_ref, send_ref, rate_out_ref):
     tile = pl.program_id(0)
     upper = place_ref[0] == 1
     base = place_ref[1]
     docs, half = send_ref.shape[0] - 8, send_ref.shape[1]
     width = lab_ref.shape[0]
-    n_pos = ints_ref.shape[1] - 1
+    n_pos = ints_ref.shape[1] - 1 - first
     lab = lab_ref[...]
     scores = (
         lax.dot_general(emb_ref[...], lab, (((1,), (1,)), ((), ())), preferred_element_type=jnp.float32)
@@ -47,12 +49,12 @@
     mean_teacher = jnp.sum(teacher, axis=0, keepdims=True) / docs
     codes = base + tile * width + lax.broadcasted_iota(jnp.int32, (1, width), 1)
     ints = ints_ref[...]
-    hit = ints[:, 0:1] == codes
-    for column in range(1, n_pos):
+    hit = ints[:, first : first + 1] == codes
+    for column in range(first + 1, first + n_pos):
         hit = hit | (ints[:, column : column + 1] == codes)
     hit = hit.astype(jnp.float32)
-    flag = (ints[:, n_pos : n_pos + 1] == 1).astype(jnp.float32)
-    target = jnp.where(flag > 0.5, hit, teacher * rate_ref[...] / mean_teacher)
+    flag = (ints[:, first + n_pos : first + n_pos + 1] == 1).astype(jnp.float32)
+    target = jnp.where(flag > 0.5, hit, teacher * jnp.exp(rate_ref[...]) / mean_teacher)
     softplus = jnp.maximum(strong, 0.0) + jnp.log1p(jnp.exp(-jnp.abs(strong)))
     slope = (jax.nn.sigmoid(strong) - target).astype(jnp.bfloat16)
     rate_out_ref[...] = jnp.sum(flag * hit, axis=0, keepdims=True)
@@ -77,14 +79,14 @@
         send_ref[...] += send
 
 
-def label_pass(place, emb, label_matrix, rates, ints):
+def label_pass(place, emb, label_matrix, log_rates, ints, first):
     rows, depth = emb.shape
     docs = ints.shape[0]
     labels = label_matrix.shape[0]
     width = 1024 if labels % 1024 == 0 else labels
     half = depth // 2
     return pl.pallas_call(
-        label_kernel,
+        functools.partial(label_kernel, first),
         grid_spec=pltpu.PrefetchScalarGridSpec(
             num_scalar_prefetch=1,
             grid=(labels // width,),
@@ -106,7 +108,7 @@
             jax.ShapeDtypeStruct((1, labels), jnp.float32),
         ],
         compiler_params=pltpu.CompilerParams(dimension_semantics=("arbitrary",)),
-    )(place, emb, label_matrix, rates, ints)
+    )(place, emb, label_matrix, log_rates, ints)
 
 
 def split_sum(keep, send, n, pair_step):
@@ -155,26 +157,32 @@
         unit = pre * inv_norm
         emb = unit.astype(jnp.bfloat16)
 
-        rates = jnp.exp(label_log_rates)
         upper = (me // n_label) % 2
         place = jnp.stack([upper, me * label_rows]).astype(jnp.int32)
         keep, send, hits = label_pass(
-            place, emb, label_matrix, rates[None, :], every[:, views * title :]
+            place, emb, label_matrix, label_log_rates[None, :], every, views * title
         )
         labeled_count = jnp.sum(all_labeled).astype(jnp.float32)
         batch_rate = hits[0] / labeled_count
-        new_log_rates = jnp.log(0.9 * rates + 0.1 * batch_rate)
+        new_log_rates = jnp.log(0.9 * jnp.exp(label_log_rates) + 0.1 * batch_rate)
 
         summed = split_sum(keep, send, n, n_label)
         total = summed[docs, 0]
         loss_sum = summed[docs, 1]
-        grad_emb = summed[:docs] * (16.0 / total)
+        grad_emb = summed[:docs] * 16.0 / total
         unit_strong = unit[docs:]
         grad_pre = (
             grad_emb - unit_strong * jnp.sum(unit_strong * grad_emb, axis=-1, keepdims=True)
         ) * inv_norm[docs:]
+        first_piece = lax.reduce_precision(grad_pre, exponent_bits=8, mantissa_bits=7)
+        rest = grad_pre - first_piece
+        second_piece = lax.reduce_precision(rest, exponent_bits=8, mantissa_bits=7)
+        third_piece = rest - second_piece
+        pieces = jnp.concatenate([first_piece, second_piece, third_piece], axis=0)
+        pieces = pieces.astype(jnp.bfloat16)
+        strong_pooled = jnp.concatenate([pooled[docs:]] * 3, axis=0)
         grad_weight = jnp.einsum(
-            "dk,dj->kj", pooled[docs:].astype(jnp.float32), grad_pre, precision=lax.Precision.HIGHEST
+            "dk,dj->kj", strong_pooled, pieces, preferred_element_type=jnp.float32
         )
         loss = loss_sum / total
         return (loss, grad_weight, new_log_rates)

time: 92 us -> 91.6 us (level)
  other arithmetic: 4.73 us -> 6.2 us
  local copies, waits for them, and re-layouts: 4.43 us -> 3.15 us
  transfers between devices with their start and end apart: 10 -> 10, of which waited for: 9 -> 10; matrix products, arithmetic and copies ran while one was open for 4% -> 2% of each run, Pallas kernels for 0% -> 0%
where the time goes in v7:
time: 91.6 us; the launch traced here: 91 us
  waiting for transfers between devices  32.8 us (36%)
  blocking collectives  21.7 us (24%)
  starting transfers between devices  9.86 us (11%)
  Pallas kernels  9.27 us (10%)
  other arithmetic  6.2 us (7%)
  matrix products  4.08 us (4%)
  between operations  3.98 us (4%)
  local copies, waits for them, and re-layouts  3.15 us (3%)
    ppermute x4, waiting for transfers between devices, split_sum(): x = x + lax.ppermute(x, AXES, [(i, i ^ step) for i in range(n)])  18.4 us
    all_to_all x1, blocking collectives, tree_sum(): lax.all_to_all(x.reshape(n_label, rows // n_label, half), 'label', 0, 0,...  10.9 us
    all_to_all x1, blocking collectives, tree_sum(): x = lax.all_to_all(every, 'label', 0, 0, tiled=False).reshape(rows, half)  10.7 us
    pallas_call x1, Pallas kernels, label_pass(): pl.pallas_call(functools.partial(label_kernel, first), grid_spec=pltpu.Pr...  9.27 us
    all_to_all x1, starting transfers between devices, shards(): lax.all_to_all(spread, AXES, 0, 0, tiled=False)  7.33 us
    all_to_all x1, waiting for transfers between devices, shards(): lax.all_to_all(spread, AXES, 0, 0, tiled=False)  7.15 us
    ppermute x1, waiting for transfers between devices, tree_sum(): part = part + lax.ppermute(part, AXES, [(i, i ^ step) for i in range(n)])  3.2 us
    dot_general x1, matrix products, shards(): jnp.einsum('dk,dj->kj', strong_pooled, pieces, preferred_element_type=jnp...  1.93 us
  transfers between devices with their start and end apart: 10, of which 10 were waited for; matrix products, arithmetic and copies ran while one was open for 2% of the time, Pallas kernels for 0%

profile of v7, /device:TPU:0, one launch (start us, length us, event | category | flops | bytes accessed | tf_op | source)
XLA Modules:
  0.0 91.0 jit_solution(3662228097676875257)
XLA Ops:
  0.6 0.0 copy-start
  0.6 0.9 reshape.48
  1.5 0.7 copy.14
  2.2 0.8 pad_add_fusion
  3.0 0.6 broadcast_in_dim.9
  3.6 7.3 %all-to-all-start = ((s32[32,2,81]{2,1,0:T(2,128)}), s32[32,2,81]{2,1,0:T(2,128)S(1)}, u32[]{:S(2)}, u32[]{:S(2)}) async-start(s32[32,2,81]{2,1,0:T(2,128)} %broadcast_in_dim.9), calls=%async_computation | async-start | bytes 65536 | tf_op jit(solution)/shard_map/all_to_all | solution.py:143
  11.0 7.2 %all-to-all-done = s32[32,2,81]{2,1,0:T(2,128)S(1)} async-done(((s32[32,2,81]{2,1,0:T(2,128)}), s32[32,2,81]{2,1,0:T(2,128)S(1)}, u32[]{:S(2)}, u32[]{:S(2)}) %all-to-all-start) | async-done | bytes 20768 | tf_op jit(solution)/shard_map/all_to_all | solution.py:143
  18.2 0.1 copy.15
  18.3 0.1 sub.35
  18.4 1.7 %fusion.15 = f32[128,768]{1,0:T(8,128)S(1)} fusion(bf16[128,768]{1,0:T(8,128)(2,1)} %param.10, s32[128]{0:T(128)S(1)} %get-tuple-element.18, s32[128]{0:T(128)S(1)} %get-tuple-element.19, s32[128]{0:T(128)S(1)} %get-tuple-element.20, s32[128]{0:T(128)S(1)} %get-tuple-element.21, s32[128]{0:T(128)S(1)} %get-tuple-element.22, s32[128]{0:T(128)S(1)} %get-tuple-element.23, ...), kind=kOutput, calls=%fused_computation.61 | convolution fusion | flops 26738688 | bytes 606208 | tf_op jit(solution)/shard_map/dot_general | solution.py:152
  20.2 0.0 copy-done.2
  20.2 0.2 collective-permute-start
  20.4 1.3 %collective-permute-done = f32[128,384]{1,0:T(8,128)S(1)} collective-permute-done((f32[128,384]{1,0:T(8,128)S(1)}, f32[128,384]{1,0:T(8,128)S(1)}, u32[]{:S(2)}, u32[]{:S(2)}) %collective-permute-start) | collective-permute-done | bytes 196640 | tf_op jit(solution)/shard_map/ppermute | solution.py:19
  21.7 10.9 %all_to_all.15 = f32[8,16,384]{2,1,0:T(8,128)S(1)} all-to-all(f32[8,16,384]{2,1,0:T(8,128)S(1)} %bitcast.84), channel_id=1, replica_groups=mesh['dp'=4,'label'=8] {'label'}, dimensions={0} | all-to-all | bytes 393216 | tf_op jit(solution)/shard_map/all_to_all | solution.py:21
  32.7 0.7 collective-permute-start.1
  33.4 3.2 %collective-permute-done.1 = f32[16,384]{1,0:T(8,128)S(1)} collective-permute-done((f32[16,384]{1,0:T(8,128)S(1)}, f32[16,384]{1,0:T(8,128)S(1)}, u32[]{:S(2)}, u32[]{:S(2)}) %collective-permute-start.1) | collective-permute-done | bytes 24608 | tf_op jit(solution)/shard_map/ppermute | solution.py:25
  36.6 10.7 %all_to_all.16 = f32[8,16,384]{2,1,0:T(8,128)S(1)} all-to-all(f32[8,16,384]{2,1,0:T(8,128)S(1)} %broadcast_in_dim.10), channel_id=1, replica_groups=mesh['dp'=4,'label'=8] {'label'}, dimensions={0} | all-to-all | bytes 393216 | tf_op jit(solution)/shard_map/all_to_all | solution.py:28
  47.3 0.0 collective-permute-start.2
  47.3 0.6 pad_add_fusion.1.place_ref
  47.9 0.8 collective-permute-done.2
  48.8 0.0 copy-done
  48.8 0.0 copy-start.1
  48.8 0.4 multiply_reduce_fusion
  49.2 0.8 fusion.49
  50.0 9.3 %shard_map.94 = (f32[72,384]{1,0:T(8,128)}, f32[72,384]{1,0:T(8,128)}, f32[1,5120]{1,0:T(1,128)}) custom-call(s32[2]{0:T(128)} %pad_add_fusion.1.place_ref, bf16[128,768]{1,0:T(8,128)(2,1)} %get-tuple-element.11.emb_ref, bf16[5120,768]{1,0:T(8,128)(2,1)} %lab_ref.1, f32[1,5120]{1,0:T(1,128)} %bitcast.89, s32[64,81]{1,0:T(8,128)} %bitcast.86), custom_call_target="tpu_custom_call" | custom-call | tf_op jit(solution)/shard_map/pallas_call | solution.py:88
  59.3 0.0 copy-start.4
  59.3 0.2 collective-permute-start.3
  59.5 1.4 %collective-permute-done.3 = f32[72,384]{1,0:T(8,128)S(1)} collective-permute-done((f32[72,384]{1,0:T(8,128)}, f32[72,384]{1,0:T(8,128)S(1)}, u32[]{:S(2)}, u32[]{:S(2)}) %collective-permute-start.3) | collective-permute-done | bytes 110624 | tf_op jit(solution)/shard_map/ppermute | solution.py:118
  60.9 0.9 add.182
  61.8 0.1 collective-permute-start.4
  61.9 5.1 %collective-permute-done.4 = f32[72,384]{1,0:T(8,128)S(1)} collective-permute-done((f32[72,384]{1,0:T(8,128)S(1)}, f32[72,384]{1,0:T(8,128)S(1)}, u32[]{:S(2)}, u32[]{:S(2)}) %collective-permute-start.4) | collective-permute-done | bytes 110624 | tf_op jit(solution)/shard_map/ppermute | solution.py:122
  67.0 0.1 collective-permute-start.5
  67.1 4.7 %collective-permute-done.5 = f32[72,384]{1,0:T(8,128)S(1)} collective-permute-done((f32[72,384]{1,0:T(8,128)S(1)}, f32[72,384]{1,0:T(8,128)S(1)}, u32[]{:S(2)}, u32[]{:S(2)}) %collective-permute-start.5) | collective-permute-done | bytes 110624 | tf_op jit(solution)/shard_map/ppermute | solution.py:122
  71.9 0.5 collective-permute-start.6
  72.4 0.0 copy-done.3
  72.4 0.7 slice_reduce_fusion
  73.8 4.5 %collective-permute-done.6 = f32[72,384]{1,0:T(8,128)S(1)} collective-permute-done((f32[72,384]{1,0:T(8,128)S(1)}, f32[72,384]{1,0:T(8,128)S(1)}, u32[]{:S(2)}, u32[]{:S(2)}) %collective-permute-start.6) | collective-permute-done | bytes 110624 | tf_op jit(solution)/shard_map/ppermute | solution.py:122
  78.2 0.7 collective-permute-start.7
  78.9 0.0 copy-done.5
  79.0 4.1 %collective-permute-done.7 = f32[72,384]{1,0:T(8,128)S(1)} collective-permute-done((f32[72,384]{1,0:T(8,128)S(1)}, f32[72,384]{1,0:T(8,128)S(1)}, u32[]{:S(2)}, u32[]{:S(2)}) %collective-permute-start.7) | collective-permute-done | bytes 110624 | tf_op jit(solution)/shard_map/ppermute | solution.py:122
  83.1 0.1 collective-permute-start.8
  83.2 0.6 add_log_fusion
  83.8 0.1 slice.167
  83.9 0.6 collective-permute-done.8
  84.5 0.6 fusion.50
  86.4 0.8 multiply_reduce_fusion.1
  87.2 0.7 reduce-precision_convert_fusion.1
  88.0 1.9 %fusion.2 = f32[768,768]{1,0:T(8,128)} fusion(bf16[64,768]{1,0:T(8,128)(2,1)S(1)} %slice-done, bf16[64,768]{1,0:T(8,128)(2,1)S(1)} %get-tuple-element.16, bf16[64,768]{1,0:T(8,128)(2,1)S(1)} %get-tuple-element.15, bf16[64,768]{1,0:T(8,128)(2,1)S(1)} %get-tuple-element.9), kind=kOutput, calls=%fused_computation.4 | convolution fusion | flops 228261888 | bytes 2752512 | tf_op jit(solution)/shard_map/dk,dj->kj/dot_general | solution.py:184
  (25 shorter events, 0.3 us)
Async XLA Ops:
  0.6 48.2 %copy-start = (bf16[768,768]{1,0:T(8,128)(2,1)S(1)}, bf16[768,768]{1,0:T(8,128)(2,1)}, u32[]{:S(2)}) copy-start(bf16[768,768]{1,0:T(8,128)(2,1)} %param.11) | copy-start | bytes 3538948
  3.6 14.5 %all-to-all-start = ((s32[32,2,81]{2,1,0:T(2,128)}), s32[32,2,81]{2,1,0:T(2,128)S(1)}, u32[]{:S(2)}, u32[]{:S(2)}) async-start(s32[32,2,81]{2,1,0:T(2,128)} %broadcast_in_dim.9), calls=%async_computation | async-start | bytes 65536 | tf_op jit(solution)/shard_map/all_to_all | solution.py:143
  18.1 2.0 %copy-start.2 = (s32[32,2,81]{2,1,0:T(2,128)}, s32[32,2,81]{2,1,0:T(2,128)S(1)}, u32[]{:S(2)}) copy-start(s32[32,2,81]{2,1,0:T(2,128)S(1)} %all-to-all-done) | copy-start | bytes 62212
  20.2 1.5 %collective-permute-start = (f32[128,384]{1,0:T(8,128)S(1)}, f32[128,384]{1,0:T(8,128)S(1)}, u32[]{:S(2)}, u32[]{:S(2)}) collective-permute-start(f32[128,384]{1,0:T(8,128)S(1)} %slice_select_fusion), channel_id=1, source_target_pairs={{0,8},{1,9},{2,10},{3,11},{4,12},{5,13},{6,14},{7,15},{8,0},{9,1},... | collective-permute-start | bytes 589832 | tf_op jit(solution)/shard_map/ppermute | solution.py:19
  32.7 3.9 %collective-permute-start.1 = (f32[16,384]{1,0:T(8,128)S(1)}, f32[16,384]{1,0:T(8,128)S(1)}, u32[]{:S(2)}, u32[]{:S(2)}) collective-permute-start(f32[16,384]{1,0:T(8,128)S(1)} %reduce_sum.36), channel_id=1, source_target_pairs={{0,16},{1,17},{2,18},{3,19},{4,20},{5,21},{6,22},{7,23},{8,24},{9,... | collective-permute-start | bytes 73736 | tf_op jit(solution)/shard_map/ppermute | solution.py:25
  47.3 1.4 %collective-permute-start.2 = (f32[128,384]{1,0:T(8,128)S(1)}, f32[128,384]{1,0:T(8,128)S(1)}, u32[]{:S(2)}, u32[]{:S(2)}) collective-permute-start(f32[128,384]{1,0:T(8,128)S(1)} %bitcast.82), channel_id=1, source_target_pairs={{0,8},{1,9},{2,10},{3,11},{4,12},{5,13},{6,14},{7,15},{8,0},{9,1},... | collective-permute-start | bytes 589832 | tf_op jit(solution)/shard_map/ppermute | solution.py:29
  48.8 35.0 %copy-start.1 = (bf16[128,768]{1,0:T(8,128)(2,1)}, bf16[128,768]{1,0:T(8,128)(2,1)S(1)}, u32[]{:S(2)}) copy-start(bf16[128,768]{1,0:T(8,128)(2,1)S(1)} %fusion.1) | copy-start | bytes 589828
  50.0 22.3 %copy-start.3 = (s32[32,2,81]{2,1,0:T(2,128)S(1)}, s32[32,2,81]{2,1,0:T(2,128)}, u32[]{:S(2)}) copy-start(s32[32,2,81]{2,1,0:T(2,128)} %copy-done.2) | copy-start | bytes 62212
  59.3 19.6 %copy-start.5 = (f32[1,5120]{1,0:T(1,128)S(1)}, f32[1,5120]{1,0:T(1,128)}, u32[]{:S(2)}) copy-start(f32[1,5120]{1,0:T(1,128)} %get-tuple-element.8) | copy-start | bytes 61444
  59.3 23.8 %copy-start.4 = (f32[5120]{0:T(1024)S(1)}, f32[5120]{0:T(1024)}, u32[]{:S(2)}) copy-start(f32[5120]{0:T(1024)} %param.13) | copy-start | bytes 61444
  59.3 1.6 %collective-permute-start.3 = (f32[72,384]{1,0:T(8,128)}, f32[72,384]{1,0:T(8,128)S(1)}, u32[]{:S(2)}, u32[]{:S(2)}) collective-permute-start(f32[72,384]{1,0:T(8,128)} %get-tuple-element.7), channel_id=1, source_target_pairs={{0,8},{1,9},{2,10},{3,11},{4,12},{5,13},{6,14},{7,15},{8,0},{9,1},... | collective-permute-start | bytes 331784 | tf_op jit(solution)/shard_map/ppermute | solution.py:118
  61.8 5.2 %collective-permute-start.4 = (f32[72,384]{1,0:T(8,128)S(1)}, f32[72,384]{1,0:T(8,128)S(1)}, u32[]{:S(2)}, u32[]{:S(2)}) collective-permute-start(f32[72,384]{1,0:T(8,128)S(1)} %add.182), channel_id=1, source_target_pairs={{0,1},{1,0},{2,3},{3,2},{4,5},{5,4},{6,7},{7,6},{8,9},{9,8},{10,11... | collective-permute-start | bytes 331784 | tf_op jit(solution)/shard_map/ppermute | solution.py:122
  67.0 4.8 %collective-permute-start.5 = (f32[72,384]{1,0:T(8,128)S(1)}, f32[72,384]{1,0:T(8,128)S(1)}, u32[]{:S(2)}, u32[]{:S(2)}) collective-permute-start(f32[72,384]{1,0:T(8,128)S(1)} %add.183), channel_id=1, source_target_pairs={{0,2},{1,3},{2,0},{3,1},{4,6},{5,7},{6,4},{7,5},{8,10},{9,11},{10,... | collective-permute-start | bytes 331784 | tf_op jit(solution)/shard_map/ppermute | solution.py:122
  71.9 6.3 %collective-permute-start.6 = (f32[72,384]{1,0:T(8,128)S(1)}, f32[72,384]{1,0:T(8,128)S(1)}, u32[]{:S(2)}, u32[]{:S(2)}) collective-permute-start(f32[72,384]{1,0:T(8,128)S(1)} %add.184), channel_id=1, source_target_pairs={{0,4},{1,5},{2,6},{3,7},{4,0},{5,1},{6,2},{7,3},{8,12},{9,13},{10,... | collective-permute-start | bytes 331784 | tf_op jit(solution)/shard_map/ppermute | solution.py:122
  78.2 4.8 %collective-permute-start.7 = (f32[72,384]{1,0:T(8,128)S(1)}, f32[72,384]{1,0:T(8,128)S(1)}, u32[]{:S(2)}, u32[]{:S(2)}) collective-permute-start(f32[72,384]{1,0:T(8,128)S(1)} %add.185), channel_id=1, source_target_pairs={{0,16},{1,17},{2,18},{3,19},{4,20},{5,21},{6,22},{7,23},{8,24},{9,... | collective-permute-start | bytes 331784 | tf_op jit(solution)/shard_map/ppermute | solution.py:122
  83.1 1.4 %collective-permute-start.8 = (f32[72,384]{1,0:T(8,128)S(1)}, f32[72,384]{1,0:T(8,128)S(1)}, u32[]{:S(2)}, u32[]{:S(2)}) collective-permute-start(f32[72,384]{1,0:T(8,128)S(1)} %add.186), channel_id=1, source_target_pairs={{0,8},{1,9},{2,10},{3,11},{4,12},{5,13},{6,14},{7,15},{8,0},{9,1},... | collective-permute-start | bytes 331784 | tf_op jit(solution)/shard_map/ppermute | solution.py:124
  83.8 4.2 %slice-start = ((bf16[128,768]{1,0:T(8,128)(2,1)}), bf16[64,768]{1,0:T(8,128)(2,1)S(1)}, s32[]{:S(2)}) async-start(bf16[128,768]{1,0:T(8,128)(2,1)} %copy-done.1), calls=%async_computation.3 | async-start | bytes 196608 | tf_op jit(solution)/shard_map/slice | solution.py:183

commit v8 on v7

--- a/solution.py
+++ b/solution.py
@@ -30,13 +30,12 @@
     return jnp.where(upper, jnp.concatenate([other, x], 1), jnp.concatenate([x, other], 1))
 
 
-def label_kernel(first, place_ref, emb_ref, lab_ref, rate_ref, ints_ref, keep_ref, send_ref, rate_out_ref):
+def label_kernel(first, n_pos, place_ref, emb_ref, lab_ref, rate_ref, ints_ref, keep_ref, send_ref, rate_out_ref):
     tile = pl.program_id(0)
     upper = place_ref[0] == 1
     base = place_ref[1]
     docs, half = send_ref.shape[0] - 8, send_ref.shape[1]
     width = lab_ref.shape[0]
-    n_pos = ints_ref.shape[1] - 1 - first
     lab = lab_ref[...]
     scores = (
         lax.dot_general(emb_ref[...], lab, (((1,), (1,)), ((), ())), preferred_element_type=jnp.float32)
@@ -79,14 +78,14 @@
         send_ref[...] += send
 
 
-def label_pass(place, emb, label_matrix, log_rates, ints, first):
+def label_pass(place, emb, label_matrix, log_rates, ints, first, n_pos):
     rows, depth = emb.shape
     docs = ints.shape[0]
     labels = label_matrix.shape[0]
     width = 1024 if labels % 1024 == 0 else labels
     half = depth // 2
     return pl.pallas_call(
-        functools.partial(label_kernel, first),
+        functools.partial(label_kernel, first, n_pos),
         grid_spec=pltpu.PrefetchScalarGridSpec(
             num_scalar_prefetch=1,
             grid=(labels // width,),
@@ -136,13 +135,15 @@
         me = lax.axis_index(AXES)
         docs = own_docs * n
 
-        packed = jnp.concatenate(
-            [token_ids.reshape(own_docs, views * title), positive_ids, labeled[:, None]], axis=1
+        side = jnp.concatenate(
+            [positive_ids, labeled[:, None], jnp.zeros((own_docs, title - n_pos - 1), jnp.int32)], axis=1
         )
+        packed = jnp.concatenate([token_ids, side[:, None, :]], axis=1)
         spread = jnp.broadcast_to(packed[None], (n,) + packed.shape)
-        every = lax.all_to_all(spread, AXES, 0, 0, tiled=False).reshape(docs, packed.shape[1])
-        all_tokens = every[:, : views * title].reshape(docs, views, title)
-        all_labeled = every[:, views * title + n_pos]
+        every = lax.all_to_all(spread, AXES, 0, 0, tiled=False).reshape(docs, views + 1, title)
+        all_tokens = every[:, :views]
+        side_all = every[:, views]
+        all_labeled = side_all[:, n_pos]
 
         rows = jnp.transpose(all_tokens, (1, 0, 2)).reshape(views * docs, title) - me * vocab_rows
         codes = jnp.arange(vocab_rows, dtype=jnp.int32)
@@ -160,7 +161,7 @@
         upper = (me // n_label) % 2
         place = jnp.stack([upper, me * label_rows]).astype(jnp.int32)
         keep, send, hits = label_pass(
-            place, emb, label_matrix, label_log_rates[None, :], every, views * title
+            place, emb, label_matrix, label_log_rates[None, :], side_all, 0, n_pos
         )
         labeled_count = jnp.sum(all_labeled).astype(jnp.float32)
         batch_rate = hits[0] / labeled_count
@@ -168,7 +169,6 @@
 
         summed = split_sum(keep, send, n, n_label)
         total = summed[docs, 0]
-        loss_sum = summed[docs, 1]
         grad_emb = summed[:docs] * 16.0 / total
         unit_strong = unit[docs:]
         grad_pre = (
@@ -184,7 +184,7 @@
         grad_weight = jnp.einsum(
             "dk,dj->kj", strong_pooled, pieces, preferred_element_type=jnp.float32
         )
-        loss = loss_sum / total
+        loss = jnp.reshape(summed[docs : docs + 1, 1:2] / summed[docs : docs + 1, 0:1], ())
         return (loss, grad_weight, new_log_rates)
 
     return shards

time: 91.6 us -> 96.3 us (1.051)
  blocking collectives: 21.7 us -> 10.9 us
  waiting for transfers between devices: 32.8 us -> 40 us
  local copies, waits for them, and re-layouts: 3.15 us -> 7.56 us
  starting transfers between devices: 9.86 us -> 13.2 us
  other arithmetic: 6.2 us -> 7.61 us
    all_to_all x1 -> x0, blocking collectives: 10.7 us -> none  [tree_sum(): x = lax.all_to_all(every, 'label', 0, 0, tiled=False).reshape(rows, half)]
    all_to_all x0 -> x1, waiting for transfers between devices: none -> 7.12 us  [tree_sum(): x = lax.all_to_all(every, 'label', 0, 0, tiled=False).reshape(rows, half)]
    unnamed x12 -> x47, local copies, waits for them, and re-layouts: 0.03 us -> 3.48 us
    all_to_all x0 -> x1, starting transfers between devices: none -> 3.39 us  [tree_sum(): x = lax.all_to_all(every, 'label', 0, 0, tiled=False).reshape(rows, half)]
  transfers between devices with their start and end apart: 10 -> 11, of which waited for: 10 -> 11; matrix products, arithmetic and copies ran while one was open for 2% -> 3% of each run, Pallas kernels for 0% -> 0%
where the time goes in v8:
time: 96.3 us; the launch traced here: 95.7 us
  waiting for transfers between devices  40 us (42%)
  starting transfers between devices  13.2 us (14%)
  blocking collectives  10.9 us (11%)
  Pallas kernels  9.26 us (10%)
  other arithmetic  7.61 us (8%)
  local copies, waits for them, and re-layouts  7.56 us (8%)
  between operations  4.03 us (4%)
  matrix products  3.13 us (3%)
    ppermute x4, waiting for transfers between devices, split_sum(): x = x + lax.ppermute(x, AXES, [(i, i ^ step) for i in range(n)])  18.4 us
    all_to_all x1, blocking collectives, tree_sum(): lax.all_to_all(x.reshape(n_label, rows // n_label, half), 'label', 0, 0,...  10.9 us
    pallas_call x1, Pallas kernels, label_pass(): pl.pallas_call(functools.partial(label_kernel, first, n_pos), grid_spec=p...  9.26 us
    all_to_all x1, starting transfers between devices, shards(): lax.all_to_all(spread, AXES, 0, 0, tiled=False)  7.33 us
    all_to_all x1, waiting for transfers between devices, shards(): lax.all_to_all(spread, AXES, 0, 0, tiled=False)  7.15 us
    all_to_all x1, waiting for transfers between devices, tree_sum(): x = lax.all_to_all(every, 'label', 0, 0, tiled=False).reshape(rows, half)  7.12 us
    unnamed x47, local copies, waits for them, and re-layouts  3.48 us
    all_to_all x1, starting transfers between devices, tree_sum(): x = lax.all_to_all(every, 'label', 0, 0, tiled=False).reshape(rows, half)  3.39 us
  transfers between devices with their start and end apart: 11, of which 11 were waited for; matrix products, arithmetic and copies ran while one was open for 3% of the time, Pallas kernels for 0%

profile of v8, /device:TPU:0, one launch (start us, length us, event | category | flops | bytes accessed | tf_op | source)
XLA Modules:
  0.0 95.7 jit_solution(3087885197926639126)
XLA Ops:
  0.7 0.8 copy.45
  1.6 0.8 add_add_fusion
  2.3 0.7 pad_add_fusion
  3.0 0.8 reshape.49
  3.8 7.3 %all-to-all-start = ((s32[32,1,192]{2,1,0:T(1,128)}), s32[32,1,192]{2,1,0:T(1,128)S(1)}, u32[]{:S(2)}, u32[]{:S(2)}) async-start(s32[32,1,192]{2,1,0:T(1,128)} %reshape.49), calls=%async_computation | async-start | bytes 65536 | tf_op jit(solution)/shard_map/all_to_all | solution.py:143
  11.2 7.2 %all-to-all-done = s32[32,1,192]{2,1,0:T(1,128)S(1)} async-done(((s32[32,1,192]{2,1,0:T(1,128)}), s32[32,1,192]{2,1,0:T(1,128)S(1)}, u32[]{:S(2)}, u32[]{:S(2)}) %all-to-all-start) | async-done | bytes 24608 | tf_op jit(solution)/shard_map/all_to_all | solution.py:143
  18.3 0.5 broadcast.32
  18.8 0.7 reduce.1
  19.5 0.1 reshape.50
  19.7 0.3 fusion.52
  20.0 0.4 fusion.51
  20.8 0.1 copy.89
  21.0 0.1 copy.86
  21.2 0.1 copy.84
  21.4 0.1 copy.81
  21.7 0.1 copy.109
  23.0 0.8 fusion.15
  23.8 0.2 collective-permute-start
  24.0 1.3 %collective-permute-done = f32[128,384]{1,0:T(8,128)S(1)} collective-permute-done((f32[128,384]{1,0:T(8,128)S(1)}, f32[128,384]{1,0:T(8,128)S(1)}, u32[]{:S(2)}, u32[]{:S(2)}) %collective-permute-start) | collective-permute-done | bytes 196640 | tf_op jit(solution)/shard_map/ppermute | solution.py:19
  25.4 10.9 %all_to_all.15 = f32[8,16,384]{2,1,0:T(8,128)S(1)} all-to-all(f32[8,16,384]{2,1,0:T(8,128)S(1)} %bitcast.60), channel_id=1, replica_groups=mesh['dp'=4,'label'=8] {'label'}, dimensions={0} | all-to-all | bytes 393216 | tf_op jit(solution)/shard_map/all_to_all | solution.py:21
  36.3 0.7 collective-permute-start.1
  37.0 3.2 %collective-permute-done.1 = f32[16,384]{1,0:T(8,128)S(1)} collective-permute-done((f32[16,384]{1,0:T(8,128)S(1)}, f32[16,384]{1,0:T(8,128)S(1)}, u32[]{:S(2)}, u32[]{:S(2)}) %collective-permute-start.1) | collective-permute-done | bytes 24608 | tf_op jit(solution)/shard_map/ppermute | solution.py:25
  40.2 0.7 broadcast_in_dim.13
  40.9 3.4 %all-to-all-start.2 = ((f32[8,16,384]{2,1,0:T(8,128)}), f32[8,16,384]{2,1,0:T(8,128)S(1)}, u32[]{:S(2)}, u32[]{:S(2)}) async-start(f32[8,16,384]{2,1,0:T(8,128)} %broadcast_in_dim.13), calls=%async_computation.2 | async-start | bytes 393216 | tf_op jit(solution)/shard_map/all_to_all | solution.py:28
  44.3 0.6 pad_add_fusion.1.place_ref
  44.9 7.1 %all-to-all-done.2 = f32[8,16,384]{2,1,0:T(8,128)S(1)} async-done(((f32[8,16,384]{2,1,0:T(8,128)}), f32[8,16,384]{2,1,0:T(8,128)S(1)}, u32[]{:S(2)}, u32[]{:S(2)}) %all-to-all-start.2) | async-done | bytes 196640 | tf_op jit(solution)/shard_map/all_to_all | solution.py:28
  52.0 0.6 slice_bitcast_fusion.ints_ref
  52.6 0.8 collective-permute-done.2
  53.5 0.4 multiply_reduce_fusion
  54.0 0.8 fusion.49
  54.8 9.3 %shard_map.94 = (f32[72,384]{1,0:T(8,128)}, f32[72,384]{1,0:T(8,128)}, f32[1,5120]{1,0:T(1,128)}) custom-call(s32[2]{0:T(128)} %pad_add_fusion.1.place_ref, bf16[128,768]{1,0:T(8,128)(2,1)} %get-tuple-element.11.emb_ref, bf16[5120,768]{1,0:T(8,128)(2,1)} %lab_ref.1, f32[1,5120]{1,0:T(1,128)} %bitcast.64, s32[64,32]{1,0:T(8,128)} %slice_bitcast_fusion.ints_ref), custom_call_target="tpu_custom_call" | custom-call | tf_op jit(solution)/shard_map/pallas_call | solution.py:87
  64.0 0.2 collective-permute-start.3
  64.3 1.4 %collective-permute-done.3 = f32[72,384]{1,0:T(8,128)S(1)} collective-permute-done((f32[72,384]{1,0:T(8,128)}, f32[72,384]{1,0:T(8,128)S(1)}, u32[]{:S(2)}, u32[]{:S(2)}) %collective-permute-start.3) | collective-permute-done | bytes 110624 | tf_op jit(solution)/shard_map/ppermute | solution.py:117
  65.6 0.9 add.182
  66.6 0.1 collective-permute-start.4
  66.7 5.1 %collective-permute-done.4 = f32[72,384]{1,0:T(8,128)S(1)} collective-permute-done((f32[72,384]{1,0:T(8,128)S(1)}, f32[72,384]{1,0:T(8,128)S(1)}, u32[]{:S(2)}, u32[]{:S(2)}) %collective-permute-start.4) | collective-permute-done | bytes 110624 | tf_op jit(solution)/shard_map/ppermute | solution.py:121
  71.8 4.7 %collective-permute-done.5 = f32[72,384]{1,0:T(8,128)S(1)} collective-permute-done((f32[72,384]{1,0:T(8,128)S(1)}, f32[72,384]{1,0:T(8,128)S(1)}, u32[]{:S(2)}, u32[]{:S(2)}) %collective-permute-start.5) | collective-permute-done | bytes 110624 | tf_op jit(solution)/shard_map/ppermute | solution.py:121
  76.6 0.5 collective-permute-start.6
  77.1 0.7 slice_reduce_fusion
  78.4 4.5 %collective-permute-done.6 = f32[72,384]{1,0:T(8,128)S(1)} collective-permute-done((f32[72,384]{1,0:T(8,128)S(1)}, f32[72,384]{1,0:T(8,128)S(1)}, u32[]{:S(2)}, u32[]{:S(2)}) %collective-permute-start.6) | collective-permute-done | bytes 110624 | tf_op jit(solution)/shard_map/ppermute | solution.py:121
  82.9 0.7 collective-permute-start.7
  83.7 4.1 %collective-permute-done.7 = f32[72,384]{1,0:T(8,128)S(1)} collective-permute-done((f32[72,384]{1,0:T(8,128)S(1)}, f32[72,384]{1,0:T(8,128)S(1)}, u32[]{:S(2)}, u32[]{:S(2)}) %collective-permute-start.7) | collective-permute-done | bytes 110624 | tf_op jit(solution)/shard_map/ppermute | solution.py:121
  87.9 0.6 add_log_fusion
  88.6 0.6 collective-permute-done.8
  89.2 0.6 fusion.50
  91.1 0.8 multiply_reduce_fusion.1
  91.9 0.7 reduce-precision_convert_fusion.1
  92.7 1.9 %fusion.2 = f32[768,768]{1,0:T(8,128)} fusion(bf16[64,768]{1,0:T(8,128)(2,1)S(1)} %slice-done, bf16[64,768]{1,0:T(8,128)(2,1)S(1)} %get-tuple-element.16, bf16[64,768]{1,0:T(8,128)(2,1)S(1)} %get-tuple-element.15, bf16[64,768]{1,0:T(8,128)(2,1)S(1)} %get-tuple-element.9), kind=kOutput, calls=%fused_computation.4 | convolution fusion | flops 228261888 | bytes 2752512 | tf_op jit(solution)/shard_map/dk,dj->kj/dot_general | solution.py:184
  (64 shorter events, 2.8 us)
Async XLA Ops:
  0.6 52.9 %copy-start = (bf16[768,768]{1,0:T(8,128)(2,1)S(1)}, bf16[768,768]{1,0:T(8,128)(2,1)}, u32[]{:S(2)}) copy-start(bf16[768,768]{1,0:T(8,128)(2,1)} %param.11) | copy-start | bytes 3538948
  3.8 14.5 %all-to-all-start = ((s32[32,1,192]{2,1,0:T(1,128)}), s32[32,1,192]{2,1,0:T(1,128)S(1)}, u32[]{:S(2)}, u32[]{:S(2)}) async-start(s32[32,1,192]{2,1,0:T(1,128)} %reshape.49), calls=%async_computation | async-start | bytes 65536 | tf_op jit(solution)/shard_map/all_to_all | solution.py:143
  20.7 2.3 %copy-start.5 = (bf16[128,768]{1,0:T(8,128)(2,1)S(1)}, bf16[128,768]{1,0:T(8,128)(2,1)}, u32[]{:S(2)}) copy-start(bf16[128,768]{1,0:T(8,128)(2,1)} %param.10) | copy-start | bytes 589828
  23.8 1.5 %collective-permute-start = (f32[128,384]{1,0:T(8,128)S(1)}, f32[128,384]{1,0:T(8,128)S(1)}, u32[]{:S(2)}, u32[]{:S(2)}) collective-permute-start(f32[128,384]{1,0:T(8,128)S(1)} %slice_select_fusion), channel_id=1, source_target_pairs={{0,8},{1,9},{2,10},{3,11},{4,12},{5,13},{6,14},{7,15},{8,0},{9,1},... | collective-permute-start | bytes 589832 | tf_op jit(solution)/shard_map/ppermute | solution.py:19
  36.3 3.9 %collective-permute-start.1 = (f32[16,384]{1,0:T(8,128)S(1)}, f32[16,384]{1,0:T(8,128)S(1)}, u32[]{:S(2)}, u32[]{:S(2)}) collective-permute-start(f32[16,384]{1,0:T(8,128)S(1)} %reduce_sum.36), channel_id=1, source_target_pairs={{0,16},{1,17},{2,18},{3,19},{4,20},{5,21},{6,22},{7,23},{8,24},{9,... | collective-permute-start | bytes 73736 | tf_op jit(solution)/shard_map/ppermute | solution.py:25
  40.9 11.1 %all-to-all-start.2 = ((f32[8,16,384]{2,1,0:T(8,128)}), f32[8,16,384]{2,1,0:T(8,128)S(1)}, u32[]{:S(2)}, u32[]{:S(2)}) async-start(f32[8,16,384]{2,1,0:T(8,128)} %broadcast_in_dim.13), calls=%async_computation.2 | async-start | bytes 393216 | tf_op jit(solution)/shard_map/all_to_all | solution.py:28
  52.0 1.4 %collective-permute-start.2 = (f32[128,384]{1,0:T(8,128)S(1)}, f32[128,384]{1,0:T(8,128)S(1)}, u32[]{:S(2)}, u32[]{:S(2)}) collective-permute-start(f32[128,384]{1,0:T(8,128)S(1)} %bitcast.58), channel_id=1, source_target_pairs={{0,8},{1,9},{2,10},{3,11},{4,12},{5,13},{6,14},{7,15},{8,0},{9,1},... | collective-permute-start | bytes 589832 | tf_op jit(solution)/shard_map/ppermute | solution.py:29
  53.5 35.0 %copy-start.1 = (bf16[128,768]{1,0:T(8,128)(2,1)}, bf16[128,768]{1,0:T(8,128)(2,1)S(1)}, u32[]{:S(2)}) copy-start(bf16[128,768]{1,0:T(8,128)(2,1)S(1)} %fusion.1) | copy-start | bytes 589828
  54.8 22.3 %copy-start.2 = (s32[64,32]{1,0:T(8,128)S(1)}, s32[64,32]{1,0:T(8,128)}, u32[]{:S(2)}) copy-start(s32[64,32]{1,0:T(8,128)} %slice_bitcast_fusion.ints_ref) | copy-start | bytes 24580
  64.0 19.6 %copy-start.4 = (f32[1,5120]{1,0:T(1,128)S(1)}, f32[1,5120]{1,0:T(1,128)}, u32[]{:S(2)}) copy-start(f32[1,5120]{1,0:T(1,128)} %get-tuple-element.8) | copy-start | bytes 61444
  64.0 23.8 %copy-start.3 = (f32[5120]{0:T(1024)S(1)}, f32[5120]{0:T(1024)}, u32[]{:S(2)}) copy-start(f32[5120]{0:T(1024)} %param.13) | copy-start | bytes 61444
  64.0 1.6 %collective-permute-start.3 = (f32[72,384]{1,0:T(8,128)}, f32[72,384]{1,0:T(8,128)S(1)}, u32[]{:S(2)}, u32[]{:S(2)}) collective-permute-start(f32[72,384]{1,0:T(8,128)} %get-tuple-element.7), channel_id=1, source_target_pairs={{0,8},{1,9},{2,10},{3,11},{4,12},{5,13},{6,14},{7,15},{8,0},{9,1},... | collective-permute-start | bytes 331784 | tf_op jit(solution)/shard_map/ppermute | solution.py:117
  66.6 5.2 %collective-permute-start.4 = (f32[72,384]{1,0:T(8,128)S(1)}, f32[72,384]{1,0:T(8,128)S(1)}, u32[]{:S(2)}, u32[]{:S(2)}) collective-permute-start(f32[72,384]{1,0:T(8,128)S(1)} %add.182), channel_id=1, source_target_pairs={{0,1},{1,0},{2,3},{3,2},{4,5},{5,4},{6,7},{7,6},{8,9},{9,8},{10,11... | collective-permute-start | bytes 331784 | tf_op jit(solution)/shard_map/ppermute | solution.py:121
  71.8 4.8 %collective-permute-start.5 = (f32[72,384]{1,0:T(8,128)S(1)}, f32[72,384]{1,0:T(8,128)S(1)}, u32[]{:S(2)}, u32[]{:S(2)}) collective-permute-start(f32[72,384]{1,0:T(8,128)S(1)} %add.183), channel_id=1, source_target_pairs={{0,2},{1,3},{2,0},{3,1},{4,6},{5,7},{6,4},{7,5},{8,10},{9,11},{10,... | collective-permute-start | bytes 331784 | tf_op jit(solution)/shard_map/ppermute | solution.py:121
  76.6 6.3 %collective-permute-start.6 = (f32[72,384]{1,0:T(8,128)S(1)}, f32[72,384]{1,0:T(8,128)S(1)}, u32[]{:S(2)}, u32[]{:S(2)}) collective-permute-start(f32[72,384]{1,0:T(8,128)S(1)} %add.184), channel_id=1, source_target_pairs={{0,4},{1,5},{2,6},{3,7},{4,0},{5,1},{6,2},{7,3},{8,12},{9,13},{10,... | collective-permute-start | bytes 331784 | tf_op jit(solution)/shard_map/ppermute | solution.py:121
  82.9 4.8 %collective-permute-start.7 = (f32[72,384]{1,0:T(8,128)S(1)}, f32[72,384]{1,0:T(8,128)S(1)}, u32[]{:S(2)}, u32[]{:S(2)}) collective-permute-start(f32[72,384]{1,0:T(8,128)S(1)} %add.185), channel_id=1, source_target_pairs={{0,16},{1,17},{2,18},{3,19},{4,20},{5,21},{6,22},{7,23},{8,24},{9,... | collective-permute-start | bytes 331784 | tf_op jit(solution)/shard_map/ppermute | solution.py:121
  87.8 1.4 %collective-permute-start.8 = (f32[72,384]{1,0:T(8,128)S(1)}, f32[72,384]{1,0:T(8,128)S(1)}, u32[]{:S(2)}, u32[]{:S(2)}) collective-permute-start(f32[72,384]{1,0:T(8,128)S(1)} %add.186), channel_id=1, source_target_pairs={{0,8},{1,9},{2,10},{3,11},{4,12},{5,13},{6,14},{7,15},{8,0},{9,1},... | collective-permute-start | bytes 331784 | tf_op jit(solution)/shard_map/ppermute | solution.py:123
  88.5 4.2 %slice-start = ((bf16[128,768]{1,0:T(8,128)(2,1)}), bf16[64,768]{1,0:T(8,128)(2,1)S(1)}, s32[]{:S(2)}) async-start(bf16[128,768]{1,0:T(8,128)(2,1)} %copy-done.1), calls=%async_computation.3 | async-start | bytes 196608 | tf_op jit(solution)/shard_map/slice | solution.py:183

commit v9 on v7

--- a/solution.py
+++ b/solution.py
@@ -111,9 +111,51 @@
     )(place, emb, label_matrix, log_rates, ints)
 
 
+def tail_kernel(upper_ref, mine_ref, other_ref, unit_ref, inv_ref, pooled_t_ref, weight_ref, loss_ref):
+    upper = upper_ref[0] == 1
+    docs = unit_ref.shape[0]
+    half = mine_ref.shape[1]
+    mine = mine_ref[...]
+    other = other_ref[...]
+    low = jnp.where(upper, other, mine)
+    high = jnp.where(upper, mine, other)
+    total = low[docs : docs + 1, 0:1]
+    loss_ref[...] = low[docs : docs + 1, 1:2] / total
+    unit = unit_ref[...]
+    grad_low = low[:docs] * 16.0 / total
+    grad_high = high[:docs] * 16.0 / total
+    along = jnp.sum(unit[:, :half] * grad_low, axis=1, keepdims=True) + jnp.sum(
+        unit[:, half:] * grad_high, axis=1, keepdims=True
+    )
+    inv = inv_ref[...]
+    pooled_t = pooled_t_ref[...]
+    for index, grad in enumerate((grad_low, grad_high)):
+        pre = (grad - unit[:, index * half : (index + 1) * half] * along) * inv
+        first = pre.astype(jnp.bfloat16)
+        rest = pre - first.astype(jnp.float32)
+        second = rest.astype(jnp.bfloat16)
+        third = (rest - second.astype(jnp.float32)).astype(jnp.bfloat16)
+        acc = jnp.dot(pooled_t, first, preferred_element_type=jnp.float32)
+        acc = acc + jnp.dot(pooled_t, second, preferred_element_type=jnp.float32)
+        acc = acc + jnp.dot(pooled_t, third, preferred_element_type=jnp.float32)
+        weight_ref[:, index * half : (index + 1) * half] = acc
+
+
+def tail_pass(upper, mine, other, unit, inv, pooled_t):
+    depth = pooled_t.shape[0]
+    vmem = pltpu.MemorySpace.VMEM
+    return pl.pallas_call(
+        tail_kernel,
+        in_specs=[pl.BlockSpec(memory_space=pltpu.MemorySpace.SMEM)] + [pl.BlockSpec(memory_space=vmem)] * 5,
+        out_specs=[pl.BlockSpec(memory_space=vmem), pl.BlockSpec(memory_space=vmem)],
+        out_shape=[
+            jax.ShapeDtypeStruct((depth, depth), jnp.float32),
+            jax.ShapeDtypeStruct((1, 1), jnp.float32),
+        ],
+    )(upper, mine, other, unit, inv, pooled_t)
+
+
 def split_sum(keep, send, n, pair_step):
-    me = lax.axis_index(AXES)
-    upper = (me // pair_step) % 2 == 1
     swap = [(i, i ^ pair_step) for i in range(n)]
     x = keep + lax.ppermute(send, AXES, swap)
     step = 1
@@ -121,8 +163,7 @@
         if step != pair_step:
             x = x + lax.ppermute(x, AXES, [(i, i ^ step) for i in range(n)])
         step *= 2
-    other = lax.ppermute(x, AXES, swap)
-    return jnp.where(upper, jnp.concatenate([other, x], 1), jnp.concatenate([x, other], 1))
+    return x, lax.ppermute(x, AXES, swap)
 
 
 def make_shards(n, n_label):
@@ -166,25 +207,11 @@
         batch_rate = hits[0] / labeled_count
         new_log_rates = jnp.log(0.9 * jnp.exp(label_log_rates) + 0.1 * batch_rate)
 
-        summed = split_sum(keep, send, n, n_label)
-        total = summed[docs, 0]
-        loss_sum = summed[docs, 1]
-        grad_emb = summed[:docs] * 16.0 / total
-        unit_strong = unit[docs:]
-        grad_pre = (
-            grad_emb - unit_strong * jnp.sum(unit_strong * grad_emb, axis=-1, keepdims=True)
-        ) * inv_norm[docs:]
-        first_piece = lax.reduce_precision(grad_pre, exponent_bits=8, mantissa_bits=7)
-        rest = grad_pre - first_piece
-        second_piece = lax.reduce_precision(rest, exponent_bits=8, mantissa_bits=7)
-        third_piece = rest - second_piece
-        pieces = jnp.concatenate([first_piece, second_piece, third_piece], axis=0)
-        pieces = pieces.astype(jnp.bfloat16)
-        strong_pooled = jnp.concatenate([pooled[docs:]] * 3, axis=0)
-        grad_weight = jnp.einsum(
-            "dk,dj->kj", strong_pooled, pieces, preferred_element_type=jnp.float32
+        mine, other = split_sum(keep, send, n, n_label)
+        grad_weight, loss = tail_pass(
+            upper.astype(jnp.int32)[None], mine, other, unit[docs:], inv_norm[docs:], pooled[docs:].T
         )
-        loss = loss_sum / total
+        loss = loss.reshape(())
         return (loss, grad_weight, new_log_rates)
 
     return shards

time: 91.6 us -> 89.8 us (0.980)
  Pallas kernels: 9.27 us -> 13.1 us
  waiting for transfers between devices: 32.8 us -> 30.1 us
  between operations: 3.98 us -> 1.49 us
  local copies, waits for them, and re-layouts: 3.15 us -> 5.53 us
  matrix products: 4.08 us -> 2.17 us
    pallas_call x0 -> x1, Pallas kernels: none -> 3.79 us  [tail_pass(): pl.pallas_call(tail_kernel, in_specs=[pl.BlockSpec(memory_space=pltpu.Mem...]
    ppermute x4, waiting for transfers between devices: 18.4 us -> 16.2 us  [split_sum(): x = x + lax.ppermute(x, AXES, [(i, i ^ step) for i in range(n)])]
    dot_general x1 -> x0, matrix products: 1.93 us -> none  [shards(): jnp.einsum('dk,dj->kj', strong_pooled, pieces, preferred_element_type=jnp...]
  transfers between devices with their start and end apart: 10 -> 10, of which waited for: 10 -> 9; matrix products, arithmetic and copies ran while one was open for 2% -> 6% of each run, Pallas kernels for 0% -> 0%
where the time goes in v9:
time: 89.8 us; the launch traced here: 89.3 us
  waiting for transfers between devices  30.1 us (34%)
  blocking collectives  21.7 us (24%)
  Pallas kernels  13.1 us (15%)
  starting transfers between devices  9.93 us (11%)
  local copies, waits for them, and re-layouts  5.53 us (6%)
  other arithmetic  5.37 us (6%)
  matrix products  2.17 us (2%)
  between operations  1.49 us (2%)
    ppermute x4, waiting for transfers between devices, split_sum(): x = x + lax.ppermute(x, AXES, [(i, i ^ step) for i in range(n)])  16.2 us
    all_to_all x1, blocking collectives, tree_sum(): lax.all_to_all(x.reshape(n_label, rows // n_label, half), 'label', 0, 0,...  10.9 us
    all_to_all x1, blocking collectives, tree_sum(): x = lax.all_to_all(every, 'label', 0, 0, tiled=False).reshape(rows, half)  10.7 us
    pallas_call x1, Pallas kernels, label_pass(): pl.pallas_call(functools.partial(label_kernel, first), grid_spec=pltpu.Pr...  9.27 us
    all_to_all x1, starting transfers between devices, shards(): lax.all_to_all(spread, AXES, 0, 0, tiled=False)  7.33 us
    all_to_all x1, waiting for transfers between devices, shards(): lax.all_to_all(spread, AXES, 0, 0, tiled=False)  7.15 us
    pallas_call x1, Pallas kernels, tail_pass(): pl.pallas_call(tail_kernel, in_specs=[pl.BlockSpec(memory_space=pltpu.Mem...  3.79 us
    ppermute x1, waiting for transfers between devices, tree_sum(): part = part + lax.ppermute(part, AXES, [(i, i ^ step) for i in range(n)])  3.2 us
  transfers between devices with their start and end apart: 10, of which 9 were waited for; matrix products, arithmetic and copies ran while one was open for 6% of the time, Pallas kernels for 0%

profile of v9, /device:TPU:0, one launch (start us, length us, event | category | flops | bytes accessed | tf_op | source)
XLA Modules:
  0.0 89.3 jit_solution(16428534546585540326)
XLA Ops:
  0.6 0.0 copy-start
  0.6 0.9 reshape.49
  1.5 0.7 copy.19
  2.2 0.8 pad_add_fusion
  3.0 0.6 broadcast_in_dim.12
  3.6 7.3 %all-to-all-start = ((s32[32,2,81]{2,1,0:T(2,128)}), s32[32,2,81]{2,1,0:T(2,128)S(1)}, u32[]{:S(2)}, u32[]{:S(2)}) async-start(s32[32,2,81]{2,1,0:T(2,128)} %broadcast_in_dim.12), calls=%async_computation | async-start | bytes 65536 | tf_op jit(solution)/shard_map/all_to_all | solution.py:184
  11.0 7.2 %all-to-all-done = s32[32,2,81]{2,1,0:T(2,128)S(1)} async-done(((s32[32,2,81]{2,1,0:T(2,128)}), s32[32,2,81]{2,1,0:T(2,128)S(1)}, u32[]{:S(2)}, u32[]{:S(2)}) %all-to-all-start) | async-done | bytes 20768 | tf_op jit(solution)/shard_map/all_to_all | solution.py:184
  18.2 0.1 copy.20
  18.3 0.1 sub.25
  18.4 1.7 %fusion.2 = f32[128,768]{1,0:T(8,128)S(1)} fusion(bf16[128,768]{1,0:T(8,128)(2,1)} %param.10, s32[128]{0:T(128)S(1)} %get-tuple-element.16, s32[128]{0:T(128)S(1)} %get-tuple-element.17, s32[128]{0:T(128)S(1)} %get-tuple-element.18, s32[128]{0:T(128)S(1)} %get-tuple-element.19, s32[128]{0:T(128)S(1)} %get-tuple-element.20, s32[128]{0:T(128)S(1)} %get-tuple-element.21, ...), kind=kOutput, calls=%fused_computation.41 | convolution fusion | flops 26738688 | bytes 606208 | tf_op jit(solution)/shard_map/dot_general | solution.py:193
  20.2 0.2 collective-permute-start
  20.4 1.3 %collective-permute-done = f32[128,384]{1,0:T(8,128)S(1)} collective-permute-done((f32[128,384]{1,0:T(8,128)S(1)}, f32[128,384]{1,0:T(8,128)S(1)}, u32[]{:S(2)}, u32[]{:S(2)}) %collective-permute-start) | collective-permute-done | bytes 196640 | tf_op jit(solution)/shard_map/ppermute | solution.py:19
  21.7 10.9 %all_to_all.15 = f32[8,16,384]{2,1,0:T(8,128)S(1)} all-to-all(f32[8,16,384]{2,1,0:T(8,128)S(1)} %bitcast.86), channel_id=1, replica_groups=mesh['dp'=4,'label'=8] {'label'}, dimensions={0} | all-to-all | bytes 393216 | tf_op jit(solution)/shard_map/all_to_all | solution.py:21
  32.7 0.7 collective-permute-start.1
  33.4 3.2 %collective-permute-done.1 = f32[16,384]{1,0:T(8,128)S(1)} collective-permute-done((f32[16,384]{1,0:T(8,128)S(1)}, f32[16,384]{1,0:T(8,128)S(1)}, u32[]{:S(2)}, u32[]{:S(2)}) %collective-permute-start.1) | collective-permute-done | bytes 24608 | tf_op jit(solution)/shard_map/ppermute | solution.py:25
  36.6 10.7 %all_to_all.16 = f32[8,16,384]{2,1,0:T(8,128)S(1)} all-to-all(f32[8,16,384]{2,1,0:T(8,128)S(1)} %broadcast_in_dim.13), channel_id=1, replica_groups=mesh['dp'=4,'label'=8] {'label'}, dimensions={0} | all-to-all | bytes 393216 | tf_op jit(solution)/shard_map/all_to_all | solution.py:28
  47.3 0.1 copy.22
  47.4 0.1 collective-permute-start.2
  47.5 0.6 pad_add_fusion.1.place_ref
  48.1 0.8 collective-permute-done.2
  48.9 0.1 fusion.1
  49.0 0.4 multiply_reduce_fusion
  49.5 0.8 fusion.35
  50.3 9.3 %shard_map.94 = (f32[72,384]{1,0:T(8,128)}, f32[72,384]{1,0:T(8,128)}, f32[1,5120]{1,0:T(1,128)}) custom-call(s32[2]{0:T(128)} %pad_add_fusion.1.place_ref, bf16[128,768]{1,0:T(8,128)(2,1)} %get-tuple-element.13.emb_ref, bf16[5120,768]{1,0:T(8,128)(2,1)} %lab_ref.1, f32[1,5120]{1,0:T(1,128)} %bitcast.91, s32[64,81]{1,0:T(8,128)} %bitcast.88), custom_call_target="tpu_custom_call" | custom-call | tf_op jit(solution)/shard_map/pallas_call | solution.py:88
  59.5 0.2 collective-permute-start.3
  59.7 1.4 %collective-permute-done.3 = f32[72,384]{1,0:T(8,128)S(1)} collective-permute-done((f32[72,384]{1,0:T(8,128)}, f32[72,384]{1,0:T(8,128)S(1)}, u32[]{:S(2)}, u32[]{:S(2)}) %collective-permute-start.3) | collective-permute-done | bytes 110624 | tf_op jit(solution)/shard_map/ppermute | solution.py:160
  61.1 0.9 %add.180 = f32[72,384]{1,0:T(8,128)S(1)} add(f32[72,384]{1,0:T(8,128)} %get-tuple-element.8, f32[72,384]{1,0:T(8,128)S(1)} %collective-permute-done.3) | non-fusion elementwise | flops 27648 | bytes 331776 | tf_op jit(solution)/shard_map/add | solution.py:160
  62.0 0.1 collective-permute-start.4
  62.1 0.0 copy-done.2
  62.1 0.7 slice_reduce_fusion
  63.5 3.7 %collective-permute-done.4 = f32[72,384]{1,0:T(8,128)S(1)} collective-permute-done((f32[72,384]{1,0:T(8,128)S(1)}, f32[72,384]{1,0:T(8,128)S(1)}, u32[]{:S(2)}, u32[]{:S(2)}) %collective-permute-start.4) | collective-permute-done | bytes 110624 | tf_op jit(solution)/shard_map/ppermute | solution.py:164
  67.2 0.1 collective-permute-start.5
  67.3 0.8 divide_multiply_fusion
  68.1 4.0 %collective-permute-done.5 = f32[72,384]{1,0:T(8,128)S(1)} collective-permute-done((f32[72,384]{1,0:T(8,128)S(1)}, f32[72,384]{1,0:T(8,128)S(1)}, u32[]{:S(2)}, u32[]{:S(2)}) %collective-permute-start.5) | collective-permute-done | bytes 110624 | tf_op jit(solution)/shard_map/ppermute | solution.py:164
  72.1 0.5 collective-permute-start.6
  72.6 0.8 slice_bitcast_fusion.pooled_t_ref
  73.4 5.0 %collective-permute-done.6 = f32[72,384]{1,0:T(8,128)S(1)} collective-permute-done((f32[72,384]{1,0:T(8,128)S(1)}, f32[72,384]{1,0:T(8,128)S(1)}, u32[]{:S(2)}, u32[]{:S(2)}) %collective-permute-start.6) | collective-permute-done | bytes 110624 | tf_op jit(solution)/shard_map/ppermute | solution.py:164
  78.4 0.7 collective-permute-start.7
  79.1 0.0 copy-done.5
  79.1 0.6 add_log_fusion
  79.8 3.5 %collective-permute-done.7 = f32[72,384]{1,0:T(8,128)S(1)} collective-permute-done((f32[72,384]{1,0:T(8,128)S(1)}, f32[72,384]{1,0:T(8,128)S(1)}, u32[]{:S(2)}, u32[]{:S(2)}) %collective-permute-start.7) | collective-permute-done | bytes 110624 | tf_op jit(solution)/shard_map/ppermute | solution.py:164
  83.3 0.1 collective-permute-start.8
  83.4 0.1 slice_bitcast_fusion.33
  83.4 0.7 copy.25.inv_ref
  84.1 0.7 slice.195.unit_ref
  84.8 0.0 collective-permute-done.8.other_ref
  84.8 0.6 copy-done.4
  85.5 3.8 %shard_map.95 = (f32[768,768]{1,0:T(8,128)}, f32[1,1]{1,0:T(1,128)}) custom-call(s32[1]{0:T(128)} %bitcast.upper_ref, f32[72,384]{1,0:T(8,128)} %copy-done.3, f32[72,384]{1,0:T(8,128)} %copy-done.4, f32[64,768]{1,0:T(8,128)} %slice.195.unit_ref, f32[64,1]{1,0:T(8,128)} %copy.25.inv_ref, bf16[768,64]{1,0:T(8,128)(2,1)} %slice_bitcast_fusion.pooled_t_ref), custom_call_target="tpu_custom_call" | custom-call | tf_op jit(solution)/shard_map/pallas_call | solution.py:147
  (22 shorter events, 0.2 us)
Async XLA Ops:
  0.6 48.4 %copy-start = (bf16[768,768]{1,0:T(8,128)(2,1)S(1)}, bf16[768,768]{1,0:T(8,128)(2,1)}, u32[]{:S(2)}) copy-start(bf16[768,768]{1,0:T(8,128)(2,1)} %param.11) | copy-start | bytes 3538948
  3.6 14.5 %all-to-all-start = ((s32[32,2,81]{2,1,0:T(2,128)}), s32[32,2,81]{2,1,0:T(2,128)S(1)}, u32[]{:S(2)}, u32[]{:S(2)}) async-start(s32[32,2,81]{2,1,0:T(2,128)} %broadcast_in_dim.12), calls=%async_computation | async-start | bytes 65536 | tf_op jit(solution)/shard_map/all_to_all | solution.py:184
  18.1 2.0 %copy-start.1 = (s32[32,2,81]{2,1,0:T(2,128)}, s32[32,2,81]{2,1,0:T(2,128)S(1)}, u32[]{:S(2)}) copy-start(s32[32,2,81]{2,1,0:T(2,128)S(1)} %all-to-all-done) | copy-start | bytes 62212
  20.2 1.5 %collective-permute-start = (f32[128,384]{1,0:T(8,128)S(1)}, f32[128,384]{1,0:T(8,128)S(1)}, u32[]{:S(2)}, u32[]{:S(2)}) collective-permute-start(f32[128,384]{1,0:T(8,128)S(1)} %slice_select_fusion), channel_id=1, source_target_pairs={{0,8},{1,9},{2,10},{3,11},{4,12},{5,13},{6,14},{7,15},{8,0},{9,1},... | collective-permute-start | bytes 589832 | tf_op jit(solution)/shard_map/ppermute | solution.py:19
  32.7 3.9 %collective-permute-start.1 = (f32[16,384]{1,0:T(8,128)S(1)}, f32[16,384]{1,0:T(8,128)S(1)}, u32[]{:S(2)}, u32[]{:S(2)}) collective-permute-start(f32[16,384]{1,0:T(8,128)S(1)} %reduce_sum.27), channel_id=1, source_target_pairs={{0,16},{1,17},{2,18},{3,19},{4,20},{5,21},{6,22},{7,23},{8,24},{9,... | collective-permute-start | bytes 73736 | tf_op jit(solution)/shard_map/ppermute | solution.py:25
  47.4 1.5 %collective-permute-start.2 = (f32[128,384]{0,1:T(8,128)S(1)}, f32[128,384]{0,1:T(8,128)S(1)}, u32[]{:S(2)}, u32[]{:S(2)}) collective-permute-start(f32[128,384]{0,1:T(8,128)S(1)} %copy.22), channel_id=1, source_target_pairs={{0,8},{1,9},{2,10},{3,11},{4,12},{5,13},{6,14},{7,15},{8,0},{9,1},... | collective-permute-start | bytes 589832 | tf_op jit(solution)/shard_map/ppermute | solution.py:29
  50.3 11.9 %copy-start.2 = (s32[32,2,81]{2,1,0:T(2,128)S(1)}, s32[32,2,81]{2,1,0:T(2,128)}, u32[]{:S(2)}) copy-start(s32[32,2,81]{2,1,0:T(2,128)} %copy-done.1) | copy-start | bytes 62212
  59.5 19.6 %copy-start.5 = (f32[5120]{0:T(1024)S(1)}, f32[5120]{0:T(1024)}, u32[]{:S(2)}) copy-start(f32[5120]{0:T(1024)} %param.13) | copy-start | bytes 61444
  59.5 1.6 %collective-permute-start.3 = (f32[72,384]{1,0:T(8,128)}, f32[72,384]{1,0:T(8,128)S(1)}, u32[]{:S(2)}, u32[]{:S(2)}) collective-permute-start(f32[72,384]{1,0:T(8,128)} %get-tuple-element.9), channel_id=1, source_target_pairs={{0,8},{1,9},{2,10},{3,11},{4,12},{5,13},{6,14},{7,15},{8,0},{9,1},... | collective-permute-start | bytes 331784 | tf_op jit(solution)/shard_map/ppermute | solution.py:160
  62.0 5.2 %collective-permute-start.4 = (f32[72,384]{1,0:T(8,128)S(1)}, f32[72,384]{1,0:T(8,128)S(1)}, u32[]{:S(2)}, u32[]{:S(2)}) collective-permute-start(f32[72,384]{1,0:T(8,128)S(1)} %add.180), channel_id=1, source_target_pairs={{0,1},{1,0},{2,3},{3,2},{4,5},{5,4},{6,7},{7,6},{8,9},{9,8},{10,11... | collective-permute-start | bytes 331784 | tf_op jit(solution)/shard_map/ppermute | solution.py:164
  67.2 4.8 %collective-permute-start.5 = (f32[72,384]{1,0:T(8,128)S(1)}, f32[72,384]{1,0:T(8,128)S(1)}, u32[]{:S(2)}, u32[]{:S(2)}) collective-permute-start(f32[72,384]{1,0:T(8,128)S(1)} %add.181), channel_id=1, source_target_pairs={{0,2},{1,3},{2,0},{3,1},{4,6},{5,7},{6,4},{7,5},{8,10},{9,11},{10,... | collective-permute-start | bytes 331784 | tf_op jit(solution)/shard_map/ppermute | solution.py:164
  72.1 6.3 %collective-permute-start.6 = (f32[72,384]{1,0:T(8,128)S(1)}, f32[72,384]{1,0:T(8,128)S(1)}, u32[]{:S(2)}, u32[]{:S(2)}) collective-permute-start(f32[72,384]{1,0:T(8,128)S(1)} %add.182), channel_id=1, source_target_pairs={{0,4},{1,5},{2,6},{3,7},{4,0},{5,1},{6,2},{7,3},{8,12},{9,13},{10,... | collective-permute-start | bytes 331784 | tf_op jit(solution)/shard_map/ppermute | solution.py:164
  78.4 4.8 %collective-permute-start.7 = (f32[72,384]{1,0:T(8,128)S(1)}, f32[72,384]{1,0:T(8,128)S(1)}, u32[]{:S(2)}, u32[]{:S(2)}) collective-permute-start(f32[72,384]{1,0:T(8,128)S(1)} %add.183), channel_id=1, source_target_pairs={{0,16},{1,17},{2,18},{3,19},{4,20},{5,21},{6,22},{7,23},{8,24},{9,... | collective-permute-start | bytes 331784 | tf_op jit(solution)/shard_map/ppermute | solution.py:164
  83.3 1.6 %copy-start.3 = (f32[72,384]{1,0:T(8,128)}, f32[72,384]{1,0:T(8,128)S(1)}, u32[]{:S(2)}) copy-start(f32[72,384]{1,0:T(8,128)S(1)} %add.184.mine_ref) | copy-start | bytes 331780
  83.3 1.6 %collective-permute-start.8 = (f32[72,384]{1,0:T(8,128)S(1)}, f32[72,384]{1,0:T(8,128)S(1)}, u32[]{:S(2)}, u32[]{:S(2)}) collective-permute-start(f32[72,384]{1,0:T(8,128)S(1)} %add.184.mine_ref), channel_id=1, source_target_pairs={{0,8},{1,9},{2,10},{3,11},{4,12},{5,13},{6,14},{7,15},{8,0},{9,1},... | collective-permute-start | bytes 331784 | tf_op jit(solution)/shard_map/ppermute | solution.py:166
  84.8 0.6 copy-start.4

commit v10 on v9

--- a/solution.py
+++ b/solution.py
@@ -113,7 +113,7 @@
 
 def tail_kernel(upper_ref, mine_ref, other_ref, unit_ref, inv_ref, pooled_t_ref, weight_ref, loss_ref):
     upper = upper_ref[0] == 1
-    docs = unit_ref.shape[0]
+    docs = pooled_t_ref.shape[1]
     half = mine_ref.shape[1]
     mine = mine_ref[...]
     other = other_ref[...]
@@ -121,13 +121,13 @@
     high = jnp.where(upper, mine, other)
     total = low[docs : docs + 1, 0:1]
     loss_ref[...] = low[docs : docs + 1, 1:2] / total
-    unit = unit_ref[...]
+    unit = unit_ref[docs:, :]
     grad_low = low[:docs] * 16.0 / total
     grad_high = high[:docs] * 16.0 / total
     along = jnp.sum(unit[:, :half] * grad_low, axis=1, keepdims=True) + jnp.sum(
         unit[:, half:] * grad_high, axis=1, keepdims=True
     )
-    inv = inv_ref[...]
+    inv = inv_ref[docs:, :]
     pooled_t = pooled_t_ref[...]
     for index, grad in enumerate((grad_low, grad_high)):
         pre = (grad - unit[:, index * half : (index + 1) * half] * along) * inv
@@ -209,7 +209,7 @@
 
         mine, other = split_sum(keep, send, n, n_label)
         grad_weight, loss = tail_pass(
-            upper.astype(jnp.int32)[None], mine, other, unit[docs:], inv_norm[docs:], pooled[docs:].T
+            upper.astype(jnp.int32)[None], mine, other, unit, inv_norm, pooled[docs:].T
         )
         loss = loss.reshape(())
         return (loss, grad_weight, new_log_rates)

time: 89.8 us -> 89.9 us (level)
    slice x3 -> x0, local copies, waits for them, and re-layouts: 1.48 us -> none  [the longest x2 0.78 us: shards(): inv_norm[docs:]]
  transfers between devices with their start and end apart: 10 -> 10, of which waited for: 9 -> 9; matrix products, arithmetic and copies ran while one was open for 6% -> 5% of each run, Pallas kernels for 0% -> 0%
where the time goes in v10:
time: 89.9 us; the launch traced here: 89.3 us
  waiting for transfers between devices  30.7 us (34%)
  blocking collectives  21.7 us (24%)
  Pallas kernels  13.1 us (15%)
  starting transfers between devices  9.92 us (11%)
  other arithmetic  5.49 us (6%)
  local copies, waits for them, and re-layouts  4.78 us (5%)
  matrix products  2.17 us (2%)
  between operations  1.5 us (2%)
    ppermute x4, waiting for transfers between devices, split_sum(): x = x + lax.ppermute(x, AXES, [(i, i ^ step) for i in range(n)])  16.8 us
    all_to_all x1, blocking collectives, tree_sum(): lax.all_to_all(x.reshape(n_label, rows // n_label, half), 'label', 0, 0,...  10.9 us
    all_to_all x1, blocking collectives, tree_sum(): x = lax.all_to_all(every, 'label', 0, 0, tiled=False).reshape(rows, half)  10.7 us
    pallas_call x1, Pallas kernels, label_pass(): pl.pallas_call(functools.partial(label_kernel, first), grid_spec=pltpu.Pr...  9.26 us
    all_to_all x1, starting transfers between devices, shards(): lax.all_to_all(spread, AXES, 0, 0, tiled=False)  7.33 us
    all_to_all x1, waiting for transfers between devices, shards(): lax.all_to_all(spread, AXES, 0, 0, tiled=False)  7.15 us
    pallas_call x1, Pallas kernels, tail_pass(): pl.pallas_call(tail_kernel, in_specs=[pl.BlockSpec(memory_space=pltpu.Mem...  3.83 us
    ppermute x1, waiting for transfers between devices, tree_sum(): part = part + lax.ppermute(part, AXES, [(i, i ^ step) for i in range(n)])  3.2 us
  transfers between devices with their start and end apart: 10, of which 9 were waited for; matrix products, arithmetic and copies ran while one was open for 5% of the time, Pallas kernels for 0%

profile of v10, /device:TPU:0, one launch (start us, length us, event | category | flops | bytes accessed | tf_op | source)
XLA Modules:
  0.0 89.3 jit_solution(4929674956574690381)
XLA Ops:
  0.6 0.0 copy-start
  0.6 0.9 reshape.48
  1.5 0.7 copy.19
  2.2 0.8 pad_add_fusion
  3.0 0.6 broadcast_in_dim.12
  3.6 7.3 %all-to-all-start = ((s32[32,2,81]{2,1,0:T(2,128)}), s32[32,2,81]{2,1,0:T(2,128)S(1)}, u32[]{:S(2)}, u32[]{:S(2)}) async-start(s32[32,2,81]{2,1,0:T(2,128)} %broadcast_in_dim.12), calls=%async_computation | async-start | bytes 65536 | tf_op jit(solution)/shard_map/all_to_all | solution.py:184
  11.0 7.2 %all-to-all-done = s32[32,2,81]{2,1,0:T(2,128)S(1)} async-done(((s32[32,2,81]{2,1,0:T(2,128)}), s32[32,2,81]{2,1,0:T(2,128)S(1)}, u32[]{:S(2)}, u32[]{:S(2)}) %all-to-all-start) | async-done | bytes 20768 | tf_op jit(solution)/shard_map/all_to_all | solution.py:184
  18.2 0.1 copy.20
  18.3 0.1 sub.25
  18.4 1.7 %fusion.2 = f32[128,768]{1,0:T(8,128)S(1)} fusion(bf16[128,768]{1,0:T(8,128)(2,1)} %param.10, s32[128]{0:T(128)S(1)} %get-tuple-element.16, s32[128]{0:T(128)S(1)} %get-tuple-element.17, s32[128]{0:T(128)S(1)} %get-tuple-element.18, s32[128]{0:T(128)S(1)} %get-tuple-element.19, s32[128]{0:T(128)S(1)} %get-tuple-element.20, s32[128]{0:T(128)S(1)} %get-tuple-element.21, ...), kind=kOutput, calls=%fused_computation.41 | convolution fusion | flops 26738688 | bytes 606208 | tf_op jit(solution)/shard_map/dot_general | solution.py:193
  20.2 0.0 copy-done.1
  20.2 0.2 collective-permute-start
  20.4 1.3 %collective-permute-done = f32[128,384]{1,0:T(8,128)S(1)} collective-permute-done((f32[128,384]{1,0:T(8,128)S(1)}, f32[128,384]{1,0:T(8,128)S(1)}, u32[]{:S(2)}, u32[]{:S(2)}) %collective-permute-start) | collective-permute-done | bytes 196640 | tf_op jit(solution)/shard_map/ppermute | solution.py:19
  21.7 10.9 %all_to_all.15 = f32[8,16,384]{2,1,0:T(8,128)S(1)} all-to-all(f32[8,16,384]{2,1,0:T(8,128)S(1)} %bitcast.86), channel_id=1, replica_groups=mesh['dp'=4,'label'=8] {'label'}, dimensions={0} | all-to-all | bytes 393216 | tf_op jit(solution)/shard_map/all_to_all | solution.py:21
  32.7 0.7 collective-permute-start.1
  33.4 3.2 %collective-permute-done.1 = f32[16,384]{1,0:T(8,128)S(1)} collective-permute-done((f32[16,384]{1,0:T(8,128)S(1)}, f32[16,384]{1,0:T(8,128)S(1)}, u32[]{:S(2)}, u32[]{:S(2)}) %collective-permute-start.1) | collective-permute-done | bytes 24608 | tf_op jit(solution)/shard_map/ppermute | solution.py:25
  36.6 10.7 %all_to_all.16 = f32[8,16,384]{2,1,0:T(8,128)S(1)} all-to-all(f32[8,16,384]{2,1,0:T(8,128)S(1)} %broadcast_in_dim.13), channel_id=1, replica_groups=mesh['dp'=4,'label'=8] {'label'}, dimensions={0} | all-to-all | bytes 393216 | tf_op jit(solution)/shard_map/all_to_all | solution.py:28
  47.3 0.1 copy.22
  47.4 0.1 collective-permute-start.2
  47.5 0.6 pad_add_fusion.1.place_ref
  48.1 0.8 collective-permute-done.2
  48.9 0.1 fusion.1
  49.0 0.0 copy-done
  49.0 0.4 multiply_reduce_fusion
  49.5 0.9 %fusion.36 = (bf16[128,768]{1,0:T(8,128)(2,1)}, f32[128,768]{1,0:T(8,128)}) fusion(f32[128,768]{1,0:T(8,128)S(1)} %get-tuple-element.50, f32[128]{0:T(128)S(1)} %get-tuple-element.48), kind=kLoop, calls=%fused_computation.114 | loop fusion | flops 196608 | bytes 983552 | tf_op jit(solution)/shard_map/convert_element_type | solution.py:199
  50.4 9.3 %shard_map.94 = (f32[72,384]{1,0:T(8,128)}, f32[72,384]{1,0:T(8,128)}, f32[1,5120]{1,0:T(1,128)}) custom-call(s32[2]{0:T(128)} %pad_add_fusion.1.place_ref, bf16[128,768]{1,0:T(8,128)(2,1)} %get-tuple-element.13.emb_ref, bf16[5120,768]{1,0:T(8,128)(2,1)} %lab_ref.1, f32[1,5120]{1,0:T(1,128)} %bitcast.91, s32[64,81]{1,0:T(8,128)} %bitcast.88), custom_call_target="tpu_custom_call" | custom-call | tf_op jit(solution)/shard_map/pallas_call | solution.py:88
  59.7 0.2 collective-permute-start.3
  59.9 1.4 %collective-permute-done.3 = f32[72,384]{1,0:T(8,128)S(1)} collective-permute-done((f32[72,384]{1,0:T(8,128)}, f32[72,384]{1,0:T(8,128)S(1)}, u32[]{:S(2)}, u32[]{:S(2)}) %collective-permute-start.3) | collective-permute-done | bytes 110624 | tf_op jit(solution)/shard_map/ppermute | solution.py:160
  61.2 0.9 %add.180 = f32[72,384]{1,0:T(8,128)S(1)} add(f32[72,384]{1,0:T(8,128)} %get-tuple-element.8, f32[72,384]{1,0:T(8,128)S(1)} %collective-permute-done.3) | non-fusion elementwise | flops 27648 | bytes 331776 | tf_op jit(solution)/shard_map/add | solution.py:160
  62.2 0.1 collective-permute-start.4
  62.3 5.1 %collective-permute-done.4 = f32[72,384]{1,0:T(8,128)S(1)} collective-permute-done((f32[72,384]{1,0:T(8,128)S(1)}, f32[72,384]{1,0:T(8,128)S(1)}, u32[]{:S(2)}, u32[]{:S(2)}) %collective-permute-start.4) | collective-permute-done | bytes 110624 | tf_op jit(solution)/shard_map/ppermute | solution.py:164
  67.4 0.1 collective-permute-start.5
  67.4 0.0 copy-done.2
  67.4 0.7 slice_reduce_fusion
  68.8 3.4 %collective-permute-done.5 = f32[72,384]{1,0:T(8,128)S(1)} collective-permute-done((f32[72,384]{1,0:T(8,128)S(1)}, f32[72,384]{1,0:T(8,128)S(1)}, u32[]{:S(2)}, u32[]{:S(2)}) %collective-permute-start.5) | collective-permute-done | bytes 110624 | tf_op jit(solution)/shard_map/ppermute | solution.py:164
  72.2 0.5 collective-permute-start.6
  72.7 0.8 divide_multiply_fusion
  73.5 5.1 %collective-permute-done.6 = f32[72,384]{1,0:T(8,128)S(1)} collective-permute-done((f32[72,384]{1,0:T(8,128)S(1)}, f32[72,384]{1,0:T(8,128)S(1)}, u32[]{:S(2)}, u32[]{:S(2)}) %collective-permute-start.6) | collective-permute-done | bytes 110624 | tf_op jit(solution)/shard_map/ppermute | solution.py:164
  78.5 0.7 collective-permute-start.7
  79.2 0.8 slice_bitcast_fusion.pooled_t_ref
  80.0 3.3 %collective-permute-done.7 = f32[72,384]{1,0:T(8,128)S(1)} collective-permute-done((f32[72,384]{1,0:T(8,128)S(1)}, f32[72,384]{1,0:T(8,128)S(1)}, u32[]{:S(2)}, u32[]{:S(2)}) %collective-permute-start.7) | collective-permute-done | bytes 110624 | tf_op jit(solution)/shard_map/ppermute | solution.py:164
  83.4 0.1 collective-permute-start.8
  83.5 0.0 copy-done.5
  83.5 0.6 add_log_fusion
  84.1 0.7 copy.25.inv_ref
  84.8 0.0 collective-permute-done.8.other_ref
  84.9 0.6 copy-done.4
  85.5 3.8 %shard_map.95 = (f32[768,768]{1,0:T(8,128)}, f32[1,1]{1,0:T(1,128)}) custom-call(s32[1]{0:T(128)} %bitcast.upper_ref, f32[72,384]{1,0:T(8,128)} %copy-done.3, f32[72,384]{1,0:T(8,128)} %copy-done.4, f32[128,768]{1,0:T(8,128)} %get-tuple-element.14.unit_ref, f32[128,1]{1,0:T(8,128)} %copy.25.inv_ref, bf16[768,64]{1,0:T(8,128)(2,1)} %slice_bitcast_fusion.pooled_t_ref), custom_call_target="tpu_custom_call" | custom-call | tf_op jit(solution)/shard_map/pallas_call | solution.py:147
  (20 shorter events, 0.2 us)
Async XLA Ops:
  0.6 48.4 %copy-start = (bf16[768,768]{1,0:T(8,128)(2,1)S(1)}, bf16[768,768]{1,0:T(8,128)(2,1)}, u32[]{:S(2)}) copy-start(bf16[768,768]{1,0:T(8,128)(2,1)} %param.11) | copy-start | bytes 3538948
  3.6 14.5 %all-to-all-start = ((s32[32,2,81]{2,1,0:T(2,128)}), s32[32,2,81]{2,1,0:T(2,128)S(1)}, u32[]{:S(2)}, u32[]{:S(2)}) async-start(s32[32,2,81]{2,1,0:T(2,128)} %broadcast_in_dim.12), calls=%async_computation | async-start | bytes 65536 | tf_op jit(solution)/shard_map/all_to_all | solution.py:184
  18.1 2.0 %copy-start.1 = (s32[32,2,81]{2,1,0:T(2,128)}, s32[32,2,81]{2,1,0:T(2,128)S(1)}, u32[]{:S(2)}) copy-start(s32[32,2,81]{2,1,0:T(2,128)S(1)} %all-to-all-done) | copy-start | bytes 62212
  20.2 1.5 %collective-permute-start = (f32[128,384]{1,0:T(8,128)S(1)}, f32[128,384]{1,0:T(8,128)S(1)}, u32[]{:S(2)}, u32[]{:S(2)}) collective-permute-start(f32[128,384]{1,0:T(8,128)S(1)} %slice_select_fusion), channel_id=1, source_target_pairs={{0,8},{1,9},{2,10},{3,11},{4,12},{5,13},{6,14},{7,15},{8,0},{9,1},... | collective-permute-start | bytes 589832 | tf_op jit(solution)/shard_map/ppermute | solution.py:19
  32.7 3.9 %collective-permute-start.1 = (f32[16,384]{1,0:T(8,128)S(1)}, f32[16,384]{1,0:T(8,128)S(1)}, u32[]{:S(2)}, u32[]{:S(2)}) collective-permute-start(f32[16,384]{1,0:T(8,128)S(1)} %reduce_sum.27), channel_id=1, source_target_pairs={{0,16},{1,17},{2,18},{3,19},{4,20},{5,21},{6,22},{7,23},{8,24},{9,... | collective-permute-start | bytes 73736 | tf_op jit(solution)/shard_map/ppermute | solution.py:25
  47.4 1.5 %collective-permute-start.2 = (f32[128,384]{0,1:T(8,128)S(1)}, f32[128,384]{0,1:T(8,128)S(1)}, u32[]{:S(2)}, u32[]{:S(2)}) collective-permute-start(f32[128,384]{0,1:T(8,128)S(1)} %copy.22), channel_id=1, source_target_pairs={{0,8},{1,9},{2,10},{3,11},{4,12},{5,13},{6,14},{7,15},{8,0},{9,1},... | collective-permute-start | bytes 589832 | tf_op jit(solution)/shard_map/ppermute | solution.py:29
  50.4 17.1 %copy-start.2 = (s32[32,2,81]{2,1,0:T(2,128)S(1)}, s32[32,2,81]{2,1,0:T(2,128)}, u32[]{:S(2)}) copy-start(s32[32,2,81]{2,1,0:T(2,128)} %copy-done.1) | copy-start | bytes 62212
  59.6 23.8 %copy-start.5 = (f32[5120]{0:T(1024)S(1)}, f32[5120]{0:T(1024)}, u32[]{:S(2)}) copy-start(f32[5120]{0:T(1024)} %param.13) | copy-start | bytes 61444
  59.7 1.6 %collective-permute-start.3 = (f32[72,384]{1,0:T(8,128)}, f32[72,384]{1,0:T(8,128)S(1)}, u32[]{:S(2)}, u32[]{:S(2)}) collective-permute-start(f32[72,384]{1,0:T(8,128)} %get-tuple-element.9), channel_id=1, source_target_pairs={{0,8},{1,9},{2,10},{3,11},{4,12},{5,13},{6,14},{7,15},{8,0},{9,1},... | collective-permute-start | bytes 331784 | tf_op jit(solution)/shard_map/ppermute | solution.py:160
  62.2 5.2 %collective-permute-start.4 = (f32[72,384]{1,0:T(8,128)S(1)}, f32[72,384]{1,0:T(8,128)S(1)}, u32[]{:S(2)}, u32[]{:S(2)}) collective-permute-start(f32[72,384]{1,0:T(8,128)S(1)} %add.180), channel_id=1, source_target_pairs={{0,1},{1,0},{2,3},{3,2},{4,5},{5,4},{6,7},{7,6},{8,9},{9,8},{10,11... | collective-permute-start | bytes 331784 | tf_op jit(solution)/shard_map/ppermute | solution.py:164
  67.4 4.8 %collective-permute-start.5 = (f32[72,384]{1,0:T(8,128)S(1)}, f32[72,384]{1,0:T(8,128)S(1)}, u32[]{:S(2)}, u32[]{:S(2)}) collective-permute-start(f32[72,384]{1,0:T(8,128)S(1)} %add.181), channel_id=1, source_target_pairs={{0,2},{1,3},{2,0},{3,1},{4,6},{5,7},{6,4},{7,5},{8,10},{9,11},{10,... | collective-permute-start | bytes 331784 | tf_op jit(solution)/shard_map/ppermute | solution.py:164
  72.2 6.3 %collective-permute-start.6 = (f32[72,384]{1,0:T(8,128)S(1)}, f32[72,384]{1,0:T(8,128)S(1)}, u32[]{:S(2)}, u32[]{:S(2)}) collective-permute-start(f32[72,384]{1,0:T(8,128)S(1)} %add.182), channel_id=1, source_target_pairs={{0,4},{1,5},{2,6},{3,7},{4,0},{5,1},{6,2},{7,3},{8,12},{9,13},{10,... | collective-permute-start | bytes 331784 | tf_op jit(solution)/shard_map/ppermute | solution.py:164
  78.5 4.8 %collective-permute-start.7 = (f32[72,384]{1,0:T(8,128)S(1)}, f32[72,384]{1,0:T(8,128)S(1)}, u32[]{:S(2)}, u32[]{:S(2)}) collective-permute-start(f32[72,384]{1,0:T(8,128)S(1)} %add.183), channel_id=1, source_target_pairs={{0,16},{1,17},{2,18},{3,19},{4,20},{5,21},{6,22},{7,23},{8,24},{9,... | collective-permute-start | bytes 331784 | tf_op jit(solution)/shard_map/ppermute | solution.py:164
  83.4 1.5 %copy-start.3 = (f32[72,384]{1,0:T(8,128)}, f32[72,384]{1,0:T(8,128)S(1)}, u32[]{:S(2)}) copy-start(f32[72,384]{1,0:T(8,128)S(1)} %add.184.mine_ref) | copy-start | bytes 331780
  83.4 1.5 %collective-permute-start.8 = (f32[72,384]{1,0:T(8,128)S(1)}, f32[72,384]{1,0:T(8,128)S(1)}, u32[]{:S(2)}, u32[]{:S(2)}) collective-permute-start(f32[72,384]{1,0:T(8,128)S(1)} %add.184.mine_ref), channel_id=1, source_target_pairs={{0,8},{1,9},{2,10},{3,11},{4,12},{5,13},{6,14},{7,15},{8,0},{9,1},... | collective-permute-start | bytes 331784 | tf_op jit(solution)/shard_map/ppermute | solution.py:166
  84.8 0.7 copy-start.4

commit v11 on v10

--- a/solution.py
+++ b/solution.py
@@ -57,7 +57,9 @@
     target = jnp.where(flag > 0.5, hit, teacher * jnp.exp(rate_ref[...]) / mean_teacher)
     softplus = jnp.maximum(strong, 0.0) + jnp.log1p(jnp.exp(-jnp.abs(strong)))
     slope = (jax.nn.sigmoid(strong) - target).astype(jnp.bfloat16)
-    rate_out_ref[...] = jnp.sum(flag * hit, axis=0, keepdims=True)
+    count = jnp.sum(ints[:, first + n_pos : first + n_pos + 1].astype(jnp.float32))
+    batch_rate = jnp.sum(flag * hit, axis=0, keepdims=True) / count
+    rate_out_ref[...] = jnp.log(0.9 * jnp.exp(rate_ref[...]) + 0.1 * batch_rate)
     part = jnp.dot(slope, lab, preferred_element_type=jnp.float32)
     low, high = part[:, :half], part[:, half:]
     lane = lax.broadcasted_iota(jnp.int32, (8, half), 1)
@@ -111,7 +113,7 @@
     )(place, emb, label_matrix, log_rates, ints)
 
 
-def tail_kernel(upper_ref, mine_ref, other_ref, unit_ref, inv_ref, pooled_t_ref, weight_ref, loss_ref):
+def tail_kernel(upper_ref, mine_ref, other_ref, pre_ref, pooled_t_ref, weight_ref, loss_ref):
     upper = upper_ref[0] == 1
     docs = pooled_t_ref.shape[1]
     half = mine_ref.shape[1]
@@ -121,13 +123,14 @@
     high = jnp.where(upper, mine, other)
     total = low[docs : docs + 1, 0:1]
     loss_ref[...] = low[docs : docs + 1, 1:2] / total
-    unit = unit_ref[docs:, :]
+    pre = pre_ref[docs:, :]
+    inv = lax.rsqrt(jnp.sum(pre * pre, axis=1, keepdims=True) + 1e-06)
+    unit = pre * inv
     grad_low = low[:docs] * 16.0 / total
     grad_high = high[:docs] * 16.0 / total
     along = jnp.sum(unit[:, :half] * grad_low, axis=1, keepdims=True) + jnp.sum(
         unit[:, half:] * grad_high, axis=1, keepdims=True
     )
-    inv = inv_ref[docs:, :]
     pooled_t = pooled_t_ref[...]
     for index, grad in enumerate((grad_low, grad_high)):
         pre = (grad - unit[:, index * half : (index + 1) * half] * along) * inv
@@ -141,18 +144,18 @@
         weight_ref[:, index * half : (index + 1) * half] = acc
 
 
-def tail_pass(upper, mine, other, unit, inv, pooled_t):
+def tail_pass(upper, mine, other, pre, pooled_t):
     depth = pooled_t.shape[0]
     vmem = pltpu.MemorySpace.VMEM
     return pl.pallas_call(
         tail_kernel,
-        in_specs=[pl.BlockSpec(memory_space=pltpu.MemorySpace.SMEM)] + [pl.BlockSpec(memory_space=vmem)] * 5,
+        in_specs=[pl.BlockSpec(memory_space=pltpu.MemorySpace.SMEM)] + [pl.BlockSpec(memory_space=vmem)] * 4,
         out_specs=[pl.BlockSpec(memory_space=vmem), pl.BlockSpec(memory_space=vmem)],
         out_shape=[
             jax.ShapeDtypeStruct((depth, depth), jnp.float32),
             jax.ShapeDtypeStruct((1, 1), jnp.float32),
         ],
-    )(upper, mine, other, unit, inv, pooled_t)
+    )(upper, mine, other, pre, pooled_t)
 
 
 def split_sum(keep, send, n, pair_step):
@@ -183,7 +186,6 @@
         spread = jnp.broadcast_to(packed[None], (n,) + packed.shape)
         every = lax.all_to_all(spread, AXES, 0, 0, tiled=False).reshape(docs, packed.shape[1])
         all_tokens = every[:, : views * title].reshape(docs, views, title)
-        all_labeled = every[:, views * title + n_pos]
 
         rows = jnp.transpose(all_tokens, (1, 0, 2)).reshape(views * docs, title) - me * vocab_rows
         codes = jnp.arange(vocab_rows, dtype=jnp.int32)
@@ -200,16 +202,14 @@
 
         upper = (me // n_label) % 2
         place = jnp.stack([upper, me * label_rows]).astype(jnp.int32)
-        keep, send, hits = label_pass(
+        keep, send, new_rates = label_pass(
             place, emb, label_matrix, label_log_rates[None, :], every, views * title
         )
-        labeled_count = jnp.sum(all_labeled).astype(jnp.float32)
-        batch_rate = hits[0] / labeled_count
-        new_log_rates = jnp.log(0.9 * jnp.exp(label_log_rates) + 0.1 * batch_rate)
+        new_log_rates = new_rates[0]
 
         mine, other = split_sum(keep, send, n, n_label)
         grad_weight, loss = tail_pass(
-            upper.astype(jnp.int32)[None], mine, other, unit, inv_norm, pooled[docs:].T
+            upper.astype(jnp.int32)[None], mine, other, pre, pooled[docs:].T
         )
         loss = loss.reshape(())
         return (loss, grad_weight, new_log_rates)

time: 89.9 us -> 89.4 us (level)
  waiting for transfers between devices: 30.7 us -> 34.1 us
  other arithmetic: 5.49 us -> 3.28 us
    ppermute x4, waiting for transfers between devices: 16.8 us -> 19.8 us  [split_sum(): x = x + lax.ppermute(x, AXES, [(i, i ^ step) for i in range(n)])]
  transfers between devices with their start and end apart: 10 -> 10, of which waited for: 9 -> 10; matrix products, arithmetic and copies ran while one was open for 5% -> 2% of each run, Pallas kernels for 0% -> 0%
where the time goes in v11:
time: 89.4 us; the launch traced here: 88.9 us
  waiting for transfers between devices  34.1 us (38%)
  blocking collectives  21.7 us (24%)
  Pallas kernels  12.9 us (14%)
  starting transfers between devices  9.93 us (11%)
  local copies, waits for them, and re-layouts  4.04 us (5%)
  other arithmetic  3.28 us (4%)
  matrix products  2.17 us (2%)
    ppermute x4, waiting for transfers between devices, split_sum(): x = x + lax.ppermute(x, AXES, [(i, i ^ step) for i in range(n)])  19.8 us
    all_to_all x1, blocking collectives, tree_sum(): lax.all_to_all(x.reshape(n_label, rows // n_label, half), 'label', 0, 0,...  10.9 us
    all_to_all x1, blocking collectives, tree_sum(): x = lax.all_to_all(every, 'label', 0, 0, tiled=False).reshape(rows, half)  10.7 us
    pallas_call x1, Pallas kernels, label_pass(): pl.pallas_call(functools.partial(label_kernel, first), grid_spec=pltpu.Pr...  9.08 us
    all_to_all x1, starting transfers between devices, shards(): lax.all_to_all(spread, AXES, 0, 0, tiled=False)  7.33 us
    all_to_all x1, waiting for transfers between devices, shards(): lax.all_to_all(spread, AXES, 0, 0, tiled=False)  7.15 us
    pallas_call x1, Pallas kernels, tail_pass(): pl.pallas_call(tail_kernel, in_specs=[pl.BlockSpec(memory_space=pltpu.Mem...  3.82 us
    ppermute x1, waiting for transfers between devices, tree_sum(): part = part + lax.ppermute(part, AXES, [(i, i ^ step) for i in range(n)])  3.2 us
  transfers between devices with their start and end apart: 10, of which 10 were waited for; matrix products, arithmetic and copies ran while one was open for 2% of the time, Pallas kernels for 0%

profile of v11, /device:TPU:0, one launch (start us, length us, event | category | flops | bytes accessed | tf_op | source)
XLA Modules:
  0.0 88.9 jit_solution(14189315445249110498)
XLA Ops:
  0.6 0.0 copy-start
  0.6 0.9 reshape.35
  1.5 0.7 copy.17
  2.2 0.8 pad_add_fusion
  3.0 0.6 broadcast_in_dim.12
  3.6 7.3 %all-to-all-start = ((s32[32,2,81]{2,1,0:T(2,128)}), s32[32,2,81]{2,1,0:T(2,128)S(1)}, u32[]{:S(2)}, u32[]{:S(2)}) async-start(s32[32,2,81]{2,1,0:T(2,128)} %broadcast_in_dim.12), calls=%async_computation | async-start | bytes 65536 | tf_op jit(solution)/shard_map/all_to_all | solution.py:187
  11.0 7.2 %all-to-all-done = s32[32,2,81]{2,1,0:T(2,128)S(1)} async-done(((s32[32,2,81]{2,1,0:T(2,128)}), s32[32,2,81]{2,1,0:T(2,128)S(1)}, u32[]{:S(2)}, u32[]{:S(2)}) %all-to-all-start) | async-done | bytes 20768 | tf_op jit(solution)/shard_map/all_to_all | solution.py:187
  18.1 0.0 copy-start.3
  18.2 0.1 copy.18
  18.3 0.1 sub.25
  18.4 1.7 %fusion.2 = f32[128,768]{1,0:T(8,128)S(1)} fusion(bf16[128,768]{1,0:T(8,128)(2,1)} %param.10, s32[128]{0:T(128)S(1)} %get-tuple-element.14, s32[128]{0:T(128)S(1)} %get-tuple-element.15, s32[128]{0:T(128)S(1)} %get-tuple-element.16, s32[128]{0:T(128)S(1)} %get-tuple-element.17, s32[128]{0:T(128)S(1)} %get-tuple-element.18, s32[128]{0:T(128)S(1)} %get-tuple-element.19, ...), kind=kOutput, calls=%fused_computation.41 | convolution fusion | flops 26738688 | bytes 606208 | tf_op jit(solution)/shard_map/dot_general | solution.py:195
  20.2 0.0 copy-done.3
  20.2 0.2 collective-permute-start
  20.4 1.3 %collective-permute-done = f32[128,384]{1,0:T(8,128)S(1)} collective-permute-done((f32[128,384]{1,0:T(8,128)S(1)}, f32[128,384]{1,0:T(8,128)S(1)}, u32[]{:S(2)}, u32[]{:S(2)}) %collective-permute-start) | collective-permute-done | bytes 196640 | tf_op jit(solution)/shard_map/ppermute | solution.py:19
  21.7 10.9 %all_to_all.15 = f32[8,16,384]{2,1,0:T(8,128)S(1)} all-to-all(f32[8,16,384]{2,1,0:T(8,128)S(1)} %bitcast.84), channel_id=1, replica_groups=mesh['dp'=4,'label'=8] {'label'}, dimensions={0} | all-to-all | bytes 393216 | tf_op jit(solution)/shard_map/all_to_all | solution.py:21
  32.7 0.7 collective-permute-start.1
  33.4 3.2 %collective-permute-done.1 = f32[16,384]{1,0:T(8,128)S(1)} collective-permute-done((f32[16,384]{1,0:T(8,128)S(1)}, f32[16,384]{1,0:T(8,128)S(1)}, u32[]{:S(2)}, u32[]{:S(2)}) %collective-permute-start.1) | collective-permute-done | bytes 24608 | tf_op jit(solution)/shard_map/ppermute | solution.py:25
  36.6 10.7 %all_to_all.16 = f32[8,16,384]{2,1,0:T(8,128)S(1)} all-to-all(f32[8,16,384]{2,1,0:T(8,128)S(1)} %broadcast_in_dim.13), channel_id=1, replica_groups=mesh['dp'=4,'label'=8] {'label'}, dimensions={0} | all-to-all | bytes 393216 | tf_op jit(solution)/shard_map/all_to_all | solution.py:28
  47.3 0.1 copy.20
  47.4 0.1 collective-permute-start.2
  47.5 0.6 pad_add_fusion.1.place_ref
  48.1 0.8 collective-permute-done.2
  48.9 0.1 fusion.1
  49.0 0.0 copy-done
  49.0 0.4 multiply_reduce_fusion
  49.5 0.0 copy-start.1
  49.5 0.8 multiply_convert_fusion.emb_ref
  50.3 9.1 %shard_map.94 = (f32[72,384]{1,0:T(8,128)}, f32[72,384]{1,0:T(8,128)}, f32[1,5120]{1,0:T(1,128)}) custom-call(s32[2]{0:T(128)} %pad_add_fusion.1.place_ref, bf16[128,768]{1,0:T(8,128)(2,1)} %multiply_convert_fusion.emb_ref, bf16[5120,768]{1,0:T(8,128)(2,1)} %lab_ref.1, f32[1,5120]{1,0:T(1,128)} %bitcast.88, s32[64,81]{1,0:T(8,128)} %bitcast.86), custom_call_target="tpu_custom_call" | custom-call | tf_op jit(solution)/shard_map/pallas_call | solution.py:90
  59.3 0.0 copy-done.1
  59.4 0.2 collective-permute-start.3
  59.6 1.4 %collective-permute-done.3 = f32[72,384]{1,0:T(8,128)S(1)} collective-permute-done((f32[72,384]{1,0:T(8,128)}, f32[72,384]{1,0:T(8,128)S(1)}, u32[]{:S(2)}, u32[]{:S(2)}) %collective-permute-start.3) | collective-permute-done | bytes 110624 | tf_op jit(solution)/shard_map/ppermute | solution.py:163
  60.9 0.9 %add.172 = f32[72,384]{1,0:T(8,128)S(1)} add(f32[72,384]{1,0:T(8,128)} %get-tuple-element.8, f32[72,384]{1,0:T(8,128)S(1)} %collective-permute-done.3) | non-fusion elementwise | flops 27648 | bytes 331776 | tf_op jit(solution)/shard_map/add | solution.py:163
  61.9 0.1 collective-permute-start.4
  62.0 5.1 %collective-permute-done.4 = f32[72,384]{1,0:T(8,128)S(1)} collective-permute-done((f32[72,384]{1,0:T(8,128)S(1)}, f32[72,384]{1,0:T(8,128)S(1)}, u32[]{:S(2)}, u32[]{:S(2)}) %collective-permute-start.4) | collective-permute-done | bytes 110624 | tf_op jit(solution)/shard_map/ppermute | solution.py:167
  67.1 0.1 collective-permute-start.5
  67.1 4.7 %collective-permute-done.5 = f32[72,384]{1,0:T(8,128)S(1)} collective-permute-done((f32[72,384]{1,0:T(8,128)S(1)}, f32[72,384]{1,0:T(8,128)S(1)}, u32[]{:S(2)}, u32[]{:S(2)}) %collective-permute-start.5) | collective-permute-done | bytes 110624 | tf_op jit(solution)/shard_map/ppermute | solution.py:167
  71.9 0.5 collective-permute-start.6
  72.4 5.8 %collective-permute-done.6 = f32[72,384]{1,0:T(8,128)S(1)} collective-permute-done((f32[72,384]{1,0:T(8,128)S(1)}, f32[72,384]{1,0:T(8,128)S(1)}, u32[]{:S(2)}, u32[]{:S(2)}) %collective-permute-start.6) | collective-permute-done | bytes 110624 | tf_op jit(solution)/shard_map/ppermute | solution.py:167
  78.2 0.7 collective-permute-start.7
  78.9 4.1 %collective-permute-done.7 = f32[72,384]{1,0:T(8,128)S(1)} collective-permute-done((f32[72,384]{1,0:T(8,128)S(1)}, f32[72,384]{1,0:T(8,128)S(1)}, u32[]{:S(2)}, u32[]{:S(2)}) %collective-permute-start.7) | collective-permute-done | bytes 110624 | tf_op jit(solution)/shard_map/ppermute | solution.py:167
  83.1 0.0 copy-start.2
  83.1 0.1 collective-permute-start.8
  83.2 0.8 slice_bitcast_fusion.pooled_t_ref
  84.0 0.5 collective-permute-done.8.other_ref
  84.5 0.0 copy-done.2
  84.5 0.0 copy-start.4
  84.5 0.6 copy-done.4
  85.1 3.8 %shard_map.95 = (f32[768,768]{1,0:T(8,128)}, f32[1,1]{1,0:T(1,128)}) custom-call(s32[1]{0:T(128)} %bitcast.upper_ref, f32[72,384]{1,0:T(8,128)} %copy-done.2, f32[72,384]{1,0:T(8,128)} %copy-done.4, f32[128,768]{1,0:T(8,128)} %copy-done.1, bf16[768,64]{1,0:T(8,128)(2,1)} %slice_bitcast_fusion.pooled_t_ref), custom_call_target="tpu_custom_call" | custom-call | tf_op jit(solution)/shard_map/pallas_call | solution.py:150
  (14 shorter events, 0.2 us)
Async XLA Ops:
  0.6 48.4 %copy-start = (bf16[768,768]{1,0:T(8,128)(2,1)S(1)}, bf16[768,768]{1,0:T(8,128)(2,1)}, u32[]{:S(2)}) copy-start(bf16[768,768]{1,0:T(8,128)(2,1)} %param.11) | copy-start | bytes 3538948
  3.6 14.5 %all-to-all-start = ((s32[32,2,81]{2,1,0:T(2,128)}), s32[32,2,81]{2,1,0:T(2,128)S(1)}, u32[]{:S(2)}, u32[]{:S(2)}) async-start(s32[32,2,81]{2,1,0:T(2,128)} %broadcast_in_dim.12), calls=%async_computation | async-start | bytes 65536 | tf_op jit(solution)/shard_map/all_to_all | solution.py:187
  18.1 2.0 %copy-start.3 = (s32[32,2,81]{2,1,0:T(2,128)}, s32[32,2,81]{2,1,0:T(2,128)S(1)}, u32[]{:S(2)}) copy-start(s32[32,2,81]{2,1,0:T(2,128)S(1)} %all-to-all-done) | copy-start | bytes 62212
  20.2 1.5 %collective-permute-start = (f32[128,384]{1,0:T(8,128)S(1)}, f32[128,384]{1,0:T(8,128)S(1)}, u32[]{:S(2)}, u32[]{:S(2)}) collective-permute-start(f32[128,384]{1,0:T(8,128)S(1)} %slice_select_fusion), channel_id=1, source_target_pairs={{0,8},{1,9},{2,10},{3,11},{4,12},{5,13},{6,14},{7,15},{8,0},{9,1},... | collective-permute-start | bytes 589832 | tf_op jit(solution)/shard_map/ppermute | solution.py:19
  32.7 3.9 %collective-permute-start.1 = (f32[16,384]{1,0:T(8,128)S(1)}, f32[16,384]{1,0:T(8,128)S(1)}, u32[]{:S(2)}, u32[]{:S(2)}) collective-permute-start(f32[16,384]{1,0:T(8,128)S(1)} %reduce_sum.18), channel_id=1, source_target_pairs={{0,16},{1,17},{2,18},{3,19},{4,20},{5,21},{6,22},{7,23},{8,24},{9,... | collective-permute-start | bytes 73736 | tf_op jit(solution)/shard_map/ppermute | solution.py:25
  47.4 1.5 %collective-permute-start.2 = (f32[128,384]{0,1:T(8,128)S(1)}, f32[128,384]{0,1:T(8,128)S(1)}, u32[]{:S(2)}, u32[]{:S(2)}) collective-permute-start(f32[128,384]{0,1:T(8,128)S(1)} %copy.20), channel_id=1, source_target_pairs={{0,8},{1,9},{2,10},{3,11},{4,12},{5,13},{6,14},{7,15},{8,0},{9,1},... | collective-permute-start | bytes 589832 | tf_op jit(solution)/shard_map/ppermute | solution.py:29
  49.5 9.9 %copy-start.1 = (f32[128,768]{1,0:T(8,128)}, f32[128,768]{1,0:T(8,128)S(1)}, u32[]{:S(2)}) copy-start(f32[128,768]{1,0:T(8,128)S(1)} %get-tuple-element.46.pre_ref) | copy-start | bytes 1179652
  59.4 1.6 %collective-permute-start.3 = (f32[72,384]{1,0:T(8,128)}, f32[72,384]{1,0:T(8,128)S(1)}, u32[]{:S(2)}, u32[]{:S(2)}) collective-permute-start(f32[72,384]{1,0:T(8,128)} %get-tuple-element.9), channel_id=1, source_target_pairs={{0,8},{1,9},{2,10},{3,11},{4,12},{5,13},{6,14},{7,15},{8,0},{9,1},... | collective-permute-start | bytes 331784 | tf_op jit(solution)/shard_map/ppermute | solution.py:163
  61.9 5.2 %collective-permute-start.4 = (f32[72,384]{1,0:T(8,128)S(1)}, f32[72,384]{1,0:T(8,128)S(1)}, u32[]{:S(2)}, u32[]{:S(2)}) collective-permute-start(f32[72,384]{1,0:T(8,128)S(1)} %add.172), channel_id=1, source_target_pairs={{0,1},{1,0},{2,3},{3,2},{4,5},{5,4},{6,7},{7,6},{8,9},{9,8},{10,11... | collective-permute-start | bytes 331784 | tf_op jit(solution)/shard_map/ppermute | solution.py:167
  67.1 4.8 %collective-permute-start.5 = (f32[72,384]{1,0:T(8,128)S(1)}, f32[72,384]{1,0:T(8,128)S(1)}, u32[]{:S(2)}, u32[]{:S(2)}) collective-permute-start(f32[72,384]{1,0:T(8,128)S(1)} %add.173), channel_id=1, source_target_pairs={{0,2},{1,3},{2,0},{3,1},{4,6},{5,7},{6,4},{7,5},{8,10},{9,11},{10,... | collective-permute-start | bytes 331784 | tf_op jit(solution)/shard_map/ppermute | solution.py:167
  71.9 6.3 %collective-permute-start.6 = (f32[72,384]{1,0:T(8,128)S(1)}, f32[72,384]{1,0:T(8,128)S(1)}, u32[]{:S(2)}, u32[]{:S(2)}) collective-permute-start(f32[72,384]{1,0:T(8,128)S(1)} %add.174), channel_id=1, source_target_pairs={{0,4},{1,5},{2,6},{3,7},{4,0},{5,1},{6,2},{7,3},{8,12},{9,13},{10,... | collective-permute-start | bytes 331784 | tf_op jit(solution)/shard_map/ppermute | solution.py:167
  78.2 4.8 %collective-permute-start.7 = (f32[72,384]{1,0:T(8,128)S(1)}, f32[72,384]{1,0:T(8,128)S(1)}, u32[]{:S(2)}, u32[]{:S(2)}) collective-permute-start(f32[72,384]{1,0:T(8,128)S(1)} %add.175), channel_id=1, source_target_pairs={{0,16},{1,17},{2,18},{3,19},{4,20},{5,21},{6,22},{7,23},{8,24},{9,... | collective-permute-start | bytes 331784 | tf_op jit(solution)/shard_map/ppermute | solution.py:167
  83.1 1.4 %copy-start.2 = (f32[72,384]{1,0:T(8,128)}, f32[72,384]{1,0:T(8,128)S(1)}, u32[]{:S(2)}) copy-start(f32[72,384]{1,0:T(8,128)S(1)} %add.176.mine_ref) | copy-start | bytes 331780
  83.1 1.4 %collective-permute-start.8 = (f32[72,384]{1,0:T(8,128)S(1)}, f32[72,384]{1,0:T(8,128)S(1)}, u32[]{:S(2)}, u32[]{:S(2)}) collective-permute-start(f32[72,384]{1,0:T(8,128)S(1)} %add.176.mine_ref), channel_id=1, source_target_pairs={{0,8},{1,9},{2,10},{3,11},{4,12},{5,13},{6,14},{7,15},{8,0},{9,1},... | collective-permute-start | bytes 331784 | tf_op jit(solution)/shard_map/ppermute | solution.py:169
  84.5 0.7 copy-start.4

commit v12 on v11

--- a/solution.py
+++ b/solution.py
@@ -30,7 +30,7 @@
     return jnp.where(upper, jnp.concatenate([other, x], 1), jnp.concatenate([x, other], 1))
 
 
-def label_kernel(first, place_ref, emb_ref, lab_ref, rate_ref, ints_ref, keep_ref, send_ref, rate_out_ref):
+def label_kernel(first, place_ref, pre_ref, lab_ref, rate_ref, ints_ref, keep_ref, send_ref, rate_out_ref, emb_ref):
     tile = pl.program_id(0)
     upper = place_ref[0] == 1
     base = place_ref[1]
@@ -38,6 +38,13 @@
     width = lab_ref.shape[0]
     n_pos = ints_ref.shape[1] - 1 - first
     lab = lab_ref[...]
+
+    @pl.when(tile == 0)
+    def _():
+        pre = pre_ref[...]
+        inv_norm = lax.rsqrt(jnp.sum(pre * pre, axis=-1, keepdims=True) + 1e-06)
+        emb_ref[...] = (pre * inv_norm).astype(jnp.bfloat16)
+
     scores = (
         lax.dot_general(emb_ref[...], lab, (((1,), (1,)), ((), ())), preferred_element_type=jnp.float32)
         * 16.0
@@ -81,8 +88,8 @@
         send_ref[...] += send
 
 
-def label_pass(place, emb, label_matrix, log_rates, ints, first):
-    rows, depth = emb.shape
+def label_pass(place, pre, label_matrix, log_rates, ints, first):
+    rows, depth = pre.shape
     docs = ints.shape[0]
     labels = label_matrix.shape[0]
     width = 1024 if labels % 1024 == 0 else labels
@@ -103,6 +110,7 @@
                 pl.BlockSpec((docs + 8, half), lambda i, p: (0, 0)),
                 pl.BlockSpec((1, width), lambda i, p: (0, i)),
             ],
+            scratch_shapes=[pltpu.VMEM((rows, depth), jnp.bfloat16)],
         ),
         out_shape=[
             jax.ShapeDtypeStruct((docs + 8, half), jnp.float32),
@@ -110,7 +118,7 @@
             jax.ShapeDtypeStruct((1, labels), jnp.float32),
         ],
         compiler_params=pltpu.CompilerParams(dimension_semantics=("arbitrary",)),
-    )(place, emb, label_matrix, log_rates, ints)
+    )(place, pre, label_matrix, log_rates, ints)
 
 
 def tail_kernel(upper_ref, mine_ref, other_ref, pre_ref, pooled_t_ref, weight_ref, loss_ref):
@@ -196,14 +204,11 @@
         pooled = (tree_sum(partial, n, n_label) * (1.0 / title)).astype(jnp.bfloat16)
 
         pre = jnp.dot(pooled, enc_weight, preferred_element_type=jnp.float32)
-        inv_norm = lax.rsqrt(jnp.sum(pre * pre, axis=-1, keepdims=True) + 1e-06)
-        unit = pre * inv_norm
-        emb = unit.astype(jnp.bfloat16)
 
         upper = (me // n_label) % 2
         place = jnp.stack([upper, me * label_rows]).astype(jnp.int32)
         keep, send, new_rates = label_pass(
-            place, emb, label_matrix, label_log_rates[None, :], every, views * title
+            place, pre, label_matrix, label_log_rates[None, :], every, views * title
         )
         new_log_rates = new_rates[0]
 

time: 89.4 us -> 89.8 us (level)
  no operation moved by 1% of the time
where the time goes in v12:
time: 89.8 us; the launch traced here: 89.4 us
  waiting for transfers between devices  34.2 us (38%)
  blocking collectives  21.7 us (24%)
  Pallas kernels  13.5 us (15%)
  starting transfers between devices  9.88 us (11%)
  local copies, waits for them, and re-layouts  4.05 us (5%)
  matrix products  2.85 us (3%)
  other arithmetic  2.47 us (3%)
    ppermute x4, waiting for transfers between devices, split_sum(): x = x + lax.ppermute(x, AXES, [(i, i ^ step) for i in range(n)])  19.8 us
    all_to_all x1, blocking collectives, tree_sum(): lax.all_to_all(x.reshape(n_label, rows // n_label, half), 'label', 0, 0,...  10.9 us
    all_to_all x1, blocking collectives, tree_sum(): x = lax.all_to_all(every, 'label', 0, 0, tiled=False).reshape(rows, half)  10.7 us
    pallas_call x1, Pallas kernels, label_pass(): pl.pallas_call(functools.partial(label_kernel, first), grid_spec=pltpu.Pr...  9.66 us
    all_to_all x1, starting transfers between devices, shards(): lax.all_to_all(spread, AXES, 0, 0, tiled=False)  7.33 us
    all_to_all x1, waiting for transfers between devices, shards(): lax.all_to_all(spread, AXES, 0, 0, tiled=False)  7.15 us
    pallas_call x1, Pallas kernels, tail_pass(): pl.pallas_call(tail_kernel, in_specs=[pl.BlockSpec(memory_space=pltpu.Mem...  3.82 us
    ppermute x1, waiting for transfers between devices, tree_sum(): part = part + lax.ppermute(part, AXES, [(i, i ^ step) for i in range(n)])  3.2 us
  transfers between devices with their start and end apart: 10, of which 10 were waited for; matrix products, arithmetic and copies ran while one was open for 2% of the time, Pallas kernels for 0%

profile of v12, /device:TPU:0, one launch (start us, length us, event | category | flops | bytes accessed | tf_op | source)
XLA Modules:
  0.0 89.4 jit_solution(4980159128222214266)
XLA Ops:
  0.6 0.0 copy-start
  0.6 0.9 reshape.29
  1.5 0.7 copy.17
  2.2 0.8 pad_add_fusion
  3.0 0.6 broadcast_in_dim.12
  3.6 7.3 %all-to-all-start = ((s32[32,2,81]{2,1,0:T(2,128)}), s32[32,2,81]{2,1,0:T(2,128)S(1)}, u32[]{:S(2)}, u32[]{:S(2)}) async-start(s32[32,2,81]{2,1,0:T(2,128)} %broadcast_in_dim.12), calls=%async_computation | async-start | bytes 65536 | tf_op jit(solution)/shard_map/all_to_all | solution.py:195
  11.0 7.2 %all-to-all-done = s32[32,2,81]{2,1,0:T(2,128)S(1)} async-done(((s32[32,2,81]{2,1,0:T(2,128)}), s32[32,2,81]{2,1,0:T(2,128)S(1)}, u32[]{:S(2)}, u32[]{:S(2)}) %all-to-all-start) | async-done | bytes 20768 | tf_op jit(solution)/shard_map/all_to_all | solution.py:195
  18.1 0.0 copy-start.2
  18.2 0.1 copy.18
  18.3 0.1 sub.25
  18.4 1.7 %fusion.2 = f32[128,768]{1,0:T(8,128)S(1)} fusion(bf16[128,768]{1,0:T(8,128)(2,1)} %param.10, s32[128]{0:T(128)S(1)} %get-tuple-element.14, s32[128]{0:T(128)S(1)} %get-tuple-element.15, s32[128]{0:T(128)S(1)} %get-tuple-element.16, s32[128]{0:T(128)S(1)} %get-tuple-element.17, s32[128]{0:T(128)S(1)} %get-tuple-element.18, s32[128]{0:T(128)S(1)} %get-tuple-element.19, ...), kind=kOutput, calls=%fused_computation.39 | convolution fusion | flops 26738688 | bytes 606208 | tf_op jit(solution)/shard_map/dot_general | solution.py:203
  20.2 0.0 copy-done.2
  20.2 0.2 collective-permute-start
  20.4 1.3 %collective-permute-done = f32[128,384]{1,0:T(8,128)S(1)} collective-permute-done((f32[128,384]{1,0:T(8,128)S(1)}, f32[128,384]{1,0:T(8,128)S(1)}, u32[]{:S(2)}, u32[]{:S(2)}) %collective-permute-start) | collective-permute-done | bytes 196640 | tf_op jit(solution)/shard_map/ppermute | solution.py:19
  21.7 10.9 %all_to_all.15 = f32[8,16,384]{2,1,0:T(8,128)S(1)} all-to-all(f32[8,16,384]{2,1,0:T(8,128)S(1)} %bitcast.84), channel_id=1, replica_groups=mesh['dp'=4,'label'=8] {'label'}, dimensions={0} | all-to-all | bytes 393216 | tf_op jit(solution)/shard_map/all_to_all | solution.py:21
  32.7 0.7 collective-permute-start.1
  33.4 3.2 %collective-permute-done.1 = f32[16,384]{1,0:T(8,128)S(1)} collective-permute-done((f32[16,384]{1,0:T(8,128)S(1)}, f32[16,384]{1,0:T(8,128)S(1)}, u32[]{:S(2)}, u32[]{:S(2)}) %collective-permute-start.1) | collective-permute-done | bytes 24608 | tf_op jit(solution)/shard_map/ppermute | solution.py:25
  36.6 10.7 %all_to_all.16 = f32[8,16,384]{2,1,0:T(8,128)S(1)} all-to-all(f32[8,16,384]{2,1,0:T(8,128)S(1)} %broadcast_in_dim.13), channel_id=1, replica_groups=mesh['dp'=4,'label'=8] {'label'}, dimensions={0} | all-to-all | bytes 393216 | tf_op jit(solution)/shard_map/all_to_all | solution.py:28
  47.3 0.1 copy.20
  47.4 0.1 collective-permute-start.2
  47.5 0.6 pad_add_fusion.1.place_ref
  48.1 0.8 collective-permute-done.2
  48.9 0.1 fusion.1
  49.0 0.0 copy-done
  49.0 1.1 %fusion.35.pre_ref = f32[128,768]{1,0:T(8,128)} fusion(bf16[128,768]{0,1:T(8,128)(2,1)S(1)} %fusion.1, bf16[768,768]{1,0:T(8,128)(2,1)S(1)} %copy-done), kind=kOutput, calls=%fused_computation.107 | convolution fusion | flops 150994944 | bytes 1769472 | tf_op jit(solution)/shard_map/dot_general | solution.py:206
  50.1 9.7 %shard_map.94 = (f32[72,384]{1,0:T(8,128)}, f32[72,384]{1,0:T(8,128)}, f32[1,5120]{1,0:T(1,128)}) custom-call(s32[2]{0:T(128)} %pad_add_fusion.1.place_ref, f32[128,768]{1,0:T(8,128)} %fusion.35.pre_ref, bf16[5120,768]{1,0:T(8,128)(2,1)} %lab_ref.1, f32[1,5120]{1,0:T(1,128)} %bitcast.88, s32[64,81]{1,0:T(8,128)} %bitcast.86), custom_call_target="tpu_custom_call" | custom-call | tf_op jit(solution)/shard_map/pallas_call | solution.py:97
  59.8 0.2 collective-permute-start.3
  60.0 1.4 %collective-permute-done.3 = f32[72,384]{1,0:T(8,128)S(1)} collective-permute-done((f32[72,384]{1,0:T(8,128)}, f32[72,384]{1,0:T(8,128)S(1)}, u32[]{:S(2)}, u32[]{:S(2)}) %collective-permute-start.3) | collective-permute-done | bytes 110624 | tf_op jit(solution)/shard_map/ppermute | solution.py:171
  61.4 0.9 %add.159 = f32[72,384]{1,0:T(8,128)S(1)} add(f32[72,384]{1,0:T(8,128)} %get-tuple-element.8, f32[72,384]{1,0:T(8,128)S(1)} %collective-permute-done.3) | non-fusion elementwise | flops 27648 | bytes 331776 | tf_op jit(solution)/shard_map/add | solution.py:171
  62.3 0.1 collective-permute-start.4
  62.4 5.1 %collective-permute-done.4 = f32[72,384]{1,0:T(8,128)S(1)} collective-permute-done((f32[72,384]{1,0:T(8,128)S(1)}, f32[72,384]{1,0:T(8,128)S(1)}, u32[]{:S(2)}, u32[]{:S(2)}) %collective-permute-start.4) | collective-permute-done | bytes 110624 | tf_op jit(solution)/shard_map/ppermute | solution.py:175
  67.5 0.1 collective-permute-start.5
  67.5 4.7 %collective-permute-done.5 = f32[72,384]{1,0:T(8,128)S(1)} collective-permute-done((f32[72,384]{1,0:T(8,128)S(1)}, f32[72,384]{1,0:T(8,128)S(1)}, u32[]{:S(2)}, u32[]{:S(2)}) %collective-permute-start.5) | collective-permute-done | bytes 110624 | tf_op jit(solution)/shard_map/ppermute | solution.py:175
  72.3 0.5 collective-permute-start.6
  72.8 5.8 %collective-permute-done.6 = f32[72,384]{1,0:T(8,128)S(1)} collective-permute-done((f32[72,384]{1,0:T(8,128)S(1)}, f32[72,384]{1,0:T(8,128)S(1)}, u32[]{:S(2)}, u32[]{:S(2)}) %collective-permute-start.6) | collective-permute-done | bytes 110624 | tf_op jit(solution)/shard_map/ppermute | solution.py:175
  78.7 0.7 collective-permute-start.7
  79.3 4.1 %collective-permute-done.7 = f32[72,384]{1,0:T(8,128)S(1)} collective-permute-done((f32[72,384]{1,0:T(8,128)S(1)}, f32[72,384]{1,0:T(8,128)S(1)}, u32[]{:S(2)}, u32[]{:S(2)}) %collective-permute-start.7) | collective-permute-done | bytes 110624 | tf_op jit(solution)/shard_map/ppermute | solution.py:175
  83.5 0.0 copy-start.1
  83.5 0.1 collective-permute-start.8
  83.6 0.8 slice_bitcast_fusion.pooled_t_ref
  84.4 0.5 collective-permute-done.8.other_ref
  84.9 0.0 copy-done.1
  84.9 0.0 copy-start.3
  84.9 0.7 copy-done.3
  85.5 3.8 %shard_map.95 = (f32[768,768]{1,0:T(8,128)}, f32[1,1]{1,0:T(1,128)}) custom-call(s32[1]{0:T(128)} %bitcast.upper_ref, f32[72,384]{1,0:T(8,128)} %copy-done.1, f32[72,384]{1,0:T(8,128)} %copy-done.3, f32[128,768]{1,0:T(8,128)} %fusion.35.pre_ref, bf16[768,64]{1,0:T(8,128)(2,1)} %slice_bitcast_fusion.pooled_t_ref), custom_call_target="tpu_custom_call" | custom-call | tf_op jit(solution)/shard_map/pallas_call | solution.py:158
  (13 shorter events, 0.2 us)
Async XLA Ops:
  0.6 48.4 %copy-start = (bf16[768,768]{1,0:T(8,128)(2,1)S(1)}, bf16[768,768]{1,0:T(8,128)(2,1)}, u32[]{:S(2)}) copy-start(bf16[768,768]{1,0:T(8,128)(2,1)} %param.11) | copy-start | bytes 3538948
  3.6 14.5 %all-to-all-start = ((s32[32,2,81]{2,1,0:T(2,128)}), s32[32,2,81]{2,1,0:T(2,128)S(1)}, u32[]{:S(2)}, u32[]{:S(2)}) async-start(s32[32,2,81]{2,1,0:T(2,128)} %broadcast_in_dim.12), calls=%async_computation | async-start | bytes 65536 | tf_op jit(solution)/shard_map/all_to_all | solution.py:195
  18.1 2.0 %copy-start.2 = (s32[32,2,81]{2,1,0:T(2,128)}, s32[32,2,81]{2,1,0:T(2,128)S(1)}, u32[]{:S(2)}) copy-start(s32[32,2,81]{2,1,0:T(2,128)S(1)} %all-to-all-done) | copy-start | bytes 62212
  20.2 1.5 %collective-permute-start = (f32[128,384]{1,0:T(8,128)S(1)}, f32[128,384]{1,0:T(8,128)S(1)}, u32[]{:S(2)}, u32[]{:S(2)}) collective-permute-start(f32[128,384]{1,0:T(8,128)S(1)} %slice_select_fusion), channel_id=1, source_target_pairs={{0,8},{1,9},{2,10},{3,11},{4,12},{5,13},{6,14},{7,15},{8,0},{9,1},... | collective-permute-start | bytes 589832 | tf_op jit(solution)/shard_map/ppermute | solution.py:19
  32.7 3.9 %collective-permute-start.1 = (f32[16,384]{1,0:T(8,128)S(1)}, f32[16,384]{1,0:T(8,128)S(1)}, u32[]{:S(2)}, u32[]{:S(2)}) collective-permute-start(f32[16,384]{1,0:T(8,128)S(1)} %reduce_sum.9), channel_id=1, source_target_pairs={{0,16},{1,17},{2,18},{3,19},{4,20},{5,21},{6,22},{7,23},{8,24},{9,... | collective-permute-start | bytes 73736 | tf_op jit(solution)/shard_map/ppermute | solution.py:25
  47.4 1.5 %collective-permute-start.2 = (f32[128,384]{0,1:T(8,128)S(1)}, f32[128,384]{0,1:T(8,128)S(1)}, u32[]{:S(2)}, u32[]{:S(2)}) collective-permute-start(f32[128,384]{0,1:T(8,128)S(1)} %copy.20), channel_id=1, source_target_pairs={{0,8},{1,9},{2,10},{3,11},{4,12},{5,13},{6,14},{7,15},{8,0},{9,1},... | collective-permute-start | bytes 589832 | tf_op jit(solution)/shard_map/ppermute | solution.py:29
  59.8 1.6 %collective-permute-start.3 = (f32[72,384]{1,0:T(8,128)}, f32[72,384]{1,0:T(8,128)S(1)}, u32[]{:S(2)}, u32[]{:S(2)}) collective-permute-start(f32[72,384]{1,0:T(8,128)} %get-tuple-element.9), channel_id=1, source_target_pairs={{0,8},{1,9},{2,10},{3,11},{4,12},{5,13},{6,14},{7,15},{8,0},{9,1},... | collective-permute-start | bytes 331784 | tf_op jit(solution)/shard_map/ppermute | solution.py:171
  62.3 5.2 %collective-permute-start.4 = (f32[72,384]{1,0:T(8,128)S(1)}, f32[72,384]{1,0:T(8,128)S(1)}, u32[]{:S(2)}, u32[]{:S(2)}) collective-permute-start(f32[72,384]{1,0:T(8,128)S(1)} %add.159), channel_id=1, source_target_pairs={{0,1},{1,0},{2,3},{3,2},{4,5},{5,4},{6,7},{7,6},{8,9},{9,8},{10,11... | collective-permute-start | bytes 331784 | tf_op jit(solution)/shard_map/ppermute | solution.py:175
  67.5 4.8 %collective-permute-start.5 = (f32[72,384]{1,0:T(8,128)S(1)}, f32[72,384]{1,0:T(8,128)S(1)}, u32[]{:S(2)}, u32[]{:S(2)}) collective-permute-start(f32[72,384]{1,0:T(8,128)S(1)} %add.160), channel_id=1, source_target_pairs={{0,2},{1,3},{2,0},{3,1},{4,6},{5,7},{6,4},{7,5},{8,10},{9,11},{10,... | collective-permute-start | bytes 331784 | tf_op jit(solution)/shard_map/ppermute | solution.py:175
  72.3 6.3 %collective-permute-start.6 = (f32[72,384]{1,0:T(8,128)S(1)}, f32[72,384]{1,0:T(8,128)S(1)}, u32[]{:S(2)}, u32[]{:S(2)}) collective-permute-start(f32[72,384]{1,0:T(8,128)S(1)} %add.161), channel_id=1, source_target_pairs={{0,4},{1,5},{2,6},{3,7},{4,0},{5,1},{6,2},{7,3},{8,12},{9,13},{10,... | collective-permute-start | bytes 331784 | tf_op jit(solution)/shard_map/ppermute | solution.py:175
  78.7 4.8 %collective-permute-start.7 = (f32[72,384]{1,0:T(8,128)S(1)}, f32[72,384]{1,0:T(8,128)S(1)}, u32[]{:S(2)}, u32[]{:S(2)}) collective-permute-start(f32[72,384]{1,0:T(8,128)S(1)} %add.162), channel_id=1, source_target_pairs={{0,16},{1,17},{2,18},{3,19},{4,20},{5,21},{6,22},{7,23},{8,24},{9,... | collective-permute-start | bytes 331784 | tf_op jit(solution)/shard_map/ppermute | solution.py:175
  83.5 1.4 %copy-start.1 = (f32[72,384]{1,0:T(8,128)}, f32[72,384]{1,0:T(8,128)S(1)}, u32[]{:S(2)}) copy-start(f32[72,384]{1,0:T(8,128)S(1)} %add.163.mine_ref) | copy-start | bytes 331780
  83.5 1.4 %collective-permute-start.8 = (f32[72,384]{1,0:T(8,128)S(1)}, f32[72,384]{1,0:T(8,128)S(1)}, u32[]{:S(2)}, u32[]{:S(2)}) collective-permute-start(f32[72,384]{1,0:T(8,128)S(1)} %add.163.mine_ref), channel_id=1, source_target_pairs={{0,8},{1,9},{2,10},{3,11},{4,12},{5,13},{6,14},{7,15},{8,0},{9,1},... | collective-permute-start | bytes 331784 | tf_op jit(solution)/shard_map/ppermute | solution.py:177
  84.9 0.7 copy-start.3

commit v13 on v11

--- a/solution.py
+++ b/solution.py
@@ -158,15 +158,17 @@
     )(upper, mine, other, pre, pooled_t)
 
 
-def split_sum(keep, send, n, pair_step):
+def split_sum(keep, send, n, pair_step, carry):
     swap = [(i, i ^ pair_step) for i in range(n)]
     x = keep + lax.ppermute(send, AXES, swap)
     step = 1
     while step < n:
         if step != pair_step:
             x = x + lax.ppermute(x, AXES, [(i, i ^ step) for i in range(n)])
+            if step == 1:
+                x, carry = lax.optimization_barrier((x, carry))
         step *= 2
-    return x, lax.ppermute(x, AXES, swap)
+    return x, lax.ppermute(x, AXES, swap), carry
 
 
 def make_shards(n, n_label):
@@ -207,10 +209,8 @@
         )
         new_log_rates = new_rates[0]
 
-        mine, other = split_sum(keep, send, n, n_label)
-        grad_weight, loss = tail_pass(
-            upper.astype(jnp.int32)[None], mine, other, pre, pooled[docs:].T
-        )
+        mine, other, pooled_t = split_sum(keep, send, n, n_label, pooled[docs:].T)
+        grad_weight, loss = tail_pass(upper.astype(jnp.int32)[None], mine, other, pre, pooled_t)
         loss = loss.reshape(())
         return (loss, grad_weight, new_log_rates)
 

time: 89.4 us -> 89.4 us (level)
  no operation moved by 1% of the time
where the time goes in v13:
time: 89.4 us; the launch traced here: 88.9 us
  waiting for transfers between devices  34.1 us (38%)
  blocking collectives  21.7 us (24%)
  Pallas kernels  12.9 us (14%)
  starting transfers between devices  9.93 us (11%)
  local copies, waits for them, and re-layouts  4.04 us (5%)
  other arithmetic  3.28 us (4%)
  matrix products  2.17 us (2%)
    ppermute x4, waiting for transfers between devices, split_sum(): x = x + lax.ppermute(x, AXES, [(i, i ^ step) for i in range(n)])  19 us
    all_to_all x1, blocking collectives, tree_sum(): lax.all_to_all(x.reshape(n_label, rows // n_label, half), 'label', 0, 0,...  10.9 us
    all_to_all x1, blocking collectives, tree_sum(): x = lax.all_to_all(every, 'label', 0, 0, tiled=False).reshape(rows, half)  10.7 us
    pallas_call x1, Pallas kernels, label_pass(): pl.pallas_call(functools.partial(label_kernel, first), grid_spec=pltpu.Pr...  9.08 us
    all_to_all x1, starting transfers between devices, shards(): lax.all_to_all(spread, AXES, 0, 0, tiled=False)  7.33 us
    all_to_all x1, waiting for transfers between devices, shards(): lax.all_to_all(spread, AXES, 0, 0, tiled=False)  7.15 us
    pallas_call x1, Pallas kernels, tail_pass(): pl.pallas_call(tail_kernel, in_specs=[pl.BlockSpec(memory_space=pltpu.Mem...  3.82 us
    ppermute x1, waiting for transfers between devices, tree_sum(): part = part + lax.ppermute(part, AXES, [(i, i ^ step) for i in range(n)])  3.2 us
  transfers between devices with their start and end apart: 10, of which 10 were waited for; matrix products, arithmetic and copies ran while one was open for 2% of the time, Pallas kernels for 0%

profile of v13, /device:TPU:0, one launch (start us, length us, event | category | flops | bytes accessed | tf_op | source)
XLA Modules:
  0.0 88.9 jit_solution(6094481552894367066)
XLA Ops:
  0.6 0.0 copy-start
  0.6 0.9 reshape.35
  1.5 0.7 copy.17
  2.2 0.8 pad_add_fusion
  3.0 0.6 broadcast_in_dim.12
  3.6 7.3 %all-to-all-start = ((s32[32,2,81]{2,1,0:T(2,128)}), s32[32,2,81]{2,1,0:T(2,128)S(1)}, u32[]{:S(2)}, u32[]{:S(2)}) async-start(s32[32,2,81]{2,1,0:T(2,128)} %broadcast_in_dim.12), calls=%async_computation | async-start | bytes 65536 | tf_op jit(solution)/shard_map/all_to_all | solution.py:189
  11.0 7.2 %all-to-all-done = s32[32,2,81]{2,1,0:T(2,128)S(1)} async-done(((s32[32,2,81]{2,1,0:T(2,128)}), s32[32,2,81]{2,1,0:T(2,128)S(1)}, u32[]{:S(2)}, u32[]{:S(2)}) %all-to-all-start) | async-done | bytes 20768 | tf_op jit(solution)/shard_map/all_to_all | solution.py:189
  18.1 0.0 copy-start.3
  18.2 0.1 copy.18
  18.3 0.1 sub.25
  18.4 1.7 %fusion.2 = f32[128,768]{1,0:T(8,128)S(1)} fusion(bf16[128,768]{1,0:T(8,128)(2,1)} %param.10, s32[128]{0:T(128)S(1)} %get-tuple-element.18, s32[128]{0:T(128)S(1)} %get-tuple-element.19, s32[128]{0:T(128)S(1)} %get-tuple-element.20, s32[128]{0:T(128)S(1)} %get-tuple-element.21, s32[128]{0:T(128)S(1)} %get-tuple-element.22, s32[128]{0:T(128)S(1)} %get-tuple-element.23, ...), kind=kOutput, calls=%fused_computation.41 | convolution fusion | flops 26738688 | bytes 606208 | tf_op jit(solution)/shard_map/dot_general | solution.py:197
  20.2 0.0 copy-done.3
  20.2 0.2 collective-permute-start
  20.4 1.3 %collective-permute-done = f32[128,384]{1,0:T(8,128)S(1)} collective-permute-done((f32[128,384]{1,0:T(8,128)S(1)}, f32[128,384]{1,0:T(8,128)S(1)}, u32[]{:S(2)}, u32[]{:S(2)}) %collective-permute-start) | collective-permute-done | bytes 196640 | tf_op jit(solution)/shard_map/ppermute | solution.py:19
  21.7 10.9 %all_to_all.15 = f32[8,16,384]{2,1,0:T(8,128)S(1)} all-to-all(f32[8,16,384]{2,1,0:T(8,128)S(1)} %bitcast.84), channel_id=1, replica_groups=mesh['dp'=4,'label'=8] {'label'}, dimensions={0} | all-to-all | bytes 393216 | tf_op jit(solution)/shard_map/all_to_all | solution.py:21
  32.7 0.7 collective-permute-start.1
  33.4 3.2 %collective-permute-done.1 = f32[16,384]{1,0:T(8,128)S(1)} collective-permute-done((f32[16,384]{1,0:T(8,128)S(1)}, f32[16,384]{1,0:T(8,128)S(1)}, u32[]{:S(2)}, u32[]{:S(2)}) %collective-permute-start.1) | collective-permute-done | bytes 24608 | tf_op jit(solution)/shard_map/ppermute | solution.py:25
  36.6 10.7 %all_to_all.16 = f32[8,16,384]{2,1,0:T(8,128)S(1)} all-to-all(f32[8,16,384]{2,1,0:T(8,128)S(1)} %broadcast_in_dim.13), channel_id=1, replica_groups=mesh['dp'=4,'label'=8] {'label'}, dimensions={0} | all-to-all | bytes 393216 | tf_op jit(solution)/shard_map/all_to_all | solution.py:28
  47.3 0.1 copy.20
  47.4 0.1 collective-permute-start.2
  47.5 0.6 pad_add_fusion.1.place_ref
  48.1 0.8 collective-permute-done.2
  48.9 0.1 fusion.1
  49.0 0.0 copy-done
  49.0 0.4 multiply_reduce_fusion
  49.5 0.0 copy-start.1
  49.5 0.8 multiply_convert_fusion.emb_ref
  50.3 9.1 %shard_map.94 = (f32[72,384]{1,0:T(8,128)}, f32[72,384]{1,0:T(8,128)}, f32[1,5120]{1,0:T(1,128)}) custom-call(s32[2]{0:T(128)} %pad_add_fusion.1.place_ref, bf16[128,768]{1,0:T(8,128)(2,1)} %multiply_convert_fusion.emb_ref, bf16[5120,768]{1,0:T(8,128)(2,1)} %lab_ref.1, f32[1,5120]{1,0:T(1,128)} %bitcast.88, s32[64,81]{1,0:T(8,128)} %bitcast.86), custom_call_target="tpu_custom_call" | custom-call | tf_op jit(solution)/shard_map/pallas_call | solution.py:90
  59.3 0.0 copy-done.1
  59.4 0.2 collective-permute-start.3
  59.6 1.4 %collective-permute-done.3 = f32[72,384]{1,0:T(8,128)S(1)} collective-permute-done((f32[72,384]{1,0:T(8,128)}, f32[72,384]{1,0:T(8,128)S(1)}, u32[]{:S(2)}, u32[]{:S(2)}) %collective-permute-start.3) | collective-permute-done | bytes 110624 | tf_op jit(solution)/shard_map/ppermute | solution.py:163
  60.9 0.9 %add.172 = f32[72,384]{1,0:T(8,128)S(1)} add(f32[72,384]{1,0:T(8,128)} %get-tuple-element.10, f32[72,384]{1,0:T(8,128)S(1)} %collective-permute-done.3) | non-fusion elementwise | flops 27648 | bytes 331776 | tf_op jit(solution)/shard_map/add | solution.py:163
  61.9 0.1 collective-permute-start.4
  62.0 0.8 slice_bitcast_fusion.pooled_t_ref
  62.8 4.3 %collective-permute-done.4 = f32[72,384]{1,0:T(8,128)S(1)} collective-permute-done((f32[72,384]{1,0:T(8,128)S(1)}, f32[72,384]{1,0:T(8,128)S(1)}, u32[]{:S(2)}, u32[]{:S(2)}) %collective-permute-start.4) | collective-permute-done | bytes 110624 | tf_op jit(solution)/shard_map/ppermute | solution.py:167
  67.1 0.1 collective-permute-start.5
  67.1 4.7 %collective-permute-done.5 = f32[72,384]{1,0:T(8,128)S(1)} collective-permute-done((f32[72,384]{1,0:T(8,128)S(1)}, f32[72,384]{1,0:T(8,128)S(1)}, u32[]{:S(2)}, u32[]{:S(2)}) %collective-permute-start.5) | collective-permute-done | bytes 110624 | tf_op jit(solution)/shard_map/ppermute | solution.py:167
  71.9 0.5 collective-permute-start.6
  72.4 5.8 %collective-permute-done.6 = f32[72,384]{1,0:T(8,128)S(1)} collective-permute-done((f32[72,384]{1,0:T(8,128)S(1)}, f32[72,384]{1,0:T(8,128)S(1)}, u32[]{:S(2)}, u32[]{:S(2)}) %collective-permute-start.6) | collective-permute-done | bytes 110624 | tf_op jit(solution)/shard_map/ppermute | solution.py:167
  78.2 0.7 collective-permute-start.7
  78.9 4.1 %collective-permute-done.7 = f32[72,384]{1,0:T(8,128)S(1)} collective-permute-done((f32[72,384]{1,0:T(8,128)S(1)}, f32[72,384]{1,0:T(8,128)S(1)}, u32[]{:S(2)}, u32[]{:S(2)}) %collective-permute-start.7) | collective-permute-done | bytes 110624 | tf_op jit(solution)/shard_map/ppermute | solution.py:167
  83.1 0.0 copy-start.2
  83.1 0.1 collective-permute-start.8
  83.2 1.3 %collective-permute-done.8.other_ref = f32[72,384]{1,0:T(8,128)S(1)} collective-permute-done((f32[72,384]{1,0:T(8,128)S(1)}, f32[72,384]{1,0:T(8,128)S(1)}, u32[]{:S(2)}, u32[]{:S(2)}) %collective-permute-start.8) | collective-permute-done | bytes 110624 | tf_op jit(solution)/shard_map/ppermute | solution.py:171
  84.5 0.0 copy-done.2
  84.5 0.0 copy-start.4
  84.5 0.6 copy-done.4
  85.1 3.8 %shard_map.95 = (f32[768,768]{1,0:T(8,128)}, f32[1,1]{1,0:T(1,128)}) custom-call(s32[1]{0:T(128)} %bitcast.upper_ref, f32[72,384]{1,0:T(8,128)} %copy-done.2, f32[72,384]{1,0:T(8,128)} %copy-done.4, f32[128,768]{1,0:T(8,128)} %copy-done.1, bf16[768,64]{1,0:T(8,128)(2,1)} %slice_bitcast_fusion.pooled_t_ref), custom_call_target="tpu_custom_call" | custom-call | tf_op jit(solution)/shard_map/pallas_call | solution.py:150
  (14 shorter events, 0.2 us)
Async XLA Ops:
  0.6 48.4 %copy-start = (bf16[768,768]{1,0:T(8,128)(2,1)S(1)}, bf16[768,768]{1,0:T(8,128)(2,1)}, u32[]{:S(2)}) copy-start(bf16[768,768]{1,0:T(8,128)(2,1)} %param.11) | copy-start | bytes 3538948
  3.6 14.5 %all-to-all-start = ((s32[32,2,81]{2,1,0:T(2,128)}), s32[32,2,81]{2,1,0:T(2,128)S(1)}, u32[]{:S(2)}, u32[]{:S(2)}) async-start(s32[32,2,81]{2,1,0:T(2,128)} %broadcast_in_dim.12), calls=%async_computation | async-start | bytes 65536 | tf_op jit(solution)/shard_map/all_to_all | solution.py:189
  18.1 2.0 %copy-start.3 = (s32[32,2,81]{2,1,0:T(2,128)}, s32[32,2,81]{2,1,0:T(2,128)S(1)}, u32[]{:S(2)}) copy-start(s32[32,2,81]{2,1,0:T(2,128)S(1)} %all-to-all-done) | copy-start | bytes 62212
  20.2 1.5 %collective-permute-start = (f32[128,384]{1,0:T(8,128)S(1)}, f32[128,384]{1,0:T(8,128)S(1)}, u32[]{:S(2)}, u32[]{:S(2)}) collective-permute-start(f32[128,384]{1,0:T(8,128)S(1)} %slice_select_fusion), channel_id=1, source_target_pairs={{0,8},{1,9},{2,10},{3,11},{4,12},{5,13},{6,14},{7,15},{8,0},{9,1},... | collective-permute-start | bytes 589832 | tf_op jit(solution)/shard_map/ppermute | solution.py:19
  32.7 3.9 %collective-permute-start.1 = (f32[16,384]{1,0:T(8,128)S(1)}, f32[16,384]{1,0:T(8,128)S(1)}, u32[]{:S(2)}, u32[]{:S(2)}) collective-permute-start(f32[16,384]{1,0:T(8,128)S(1)} %reduce_sum.18), channel_id=1, source_target_pairs={{0,16},{1,17},{2,18},{3,19},{4,20},{5,21},{6,22},{7,23},{8,24},{9,... | collective-permute-start | bytes 73736 | tf_op jit(solution)/shard_map/ppermute | solution.py:25
  47.4 1.5 %collective-permute-start.2 = (f32[128,384]{0,1:T(8,128)S(1)}, f32[128,384]{0,1:T(8,128)S(1)}, u32[]{:S(2)}, u32[]{:S(2)}) collective-permute-start(f32[128,384]{0,1:T(8,128)S(1)} %copy.20), channel_id=1, source_target_pairs={{0,8},{1,9},{2,10},{3,11},{4,12},{5,13},{6,14},{7,15},{8,0},{9,1},... | collective-permute-start | bytes 589832 | tf_op jit(solution)/shard_map/ppermute | solution.py:29
  49.5 9.9 %copy-start.1 = (f32[128,768]{1,0:T(8,128)}, f32[128,768]{1,0:T(8,128)S(1)}, u32[]{:S(2)}) copy-start(f32[128,768]{1,0:T(8,128)S(1)} %get-tuple-element.50.pre_ref) | copy-start | bytes 1179652
  59.4 1.6 %collective-permute-start.3 = (f32[72,384]{1,0:T(8,128)}, f32[72,384]{1,0:T(8,128)S(1)}, u32[]{:S(2)}, u32[]{:S(2)}) collective-permute-start(f32[72,384]{1,0:T(8,128)} %get-tuple-element.11), channel_id=1, source_target_pairs={{0,8},{1,9},{2,10},{3,11},{4,12},{5,13},{6,14},{7,15},{8,0},{9,1},... | collective-permute-start | bytes 331784 | tf_op jit(solution)/shard_map/ppermute | solution.py:163
  61.9 5.2 %collective-permute-start.4 = (f32[72,384]{1,0:T(8,128)S(1)}, f32[72,384]{1,0:T(8,128)S(1)}, u32[]{:S(2)}, u32[]{:S(2)}) collective-permute-start(f32[72,384]{1,0:T(8,128)S(1)} %add.172), channel_id=1, source_target_pairs={{0,1},{1,0},{2,3},{3,2},{4,5},{5,4},{6,7},{7,6},{8,9},{9,8},{10,11... | collective-permute-start | bytes 331784 | tf_op jit(solution)/shard_map/ppermute | solution.py:167
  67.1 4.8 %collective-permute-start.5 = (f32[72,384]{1,0:T(8,128)S(1)}, f32[72,384]{1,0:T(8,128)S(1)}, u32[]{:S(2)}, u32[]{:S(2)}) collective-permute-start(f32[72,384]{1,0:T(8,128)S(1)} %add.173), channel_id=1, source_target_pairs={{0,2},{1,3},{2,0},{3,1},{4,6},{5,7},{6,4},{7,5},{8,10},{9,11},{10,... | collective-permute-start | bytes 331784 | tf_op jit(solution)/shard_map/ppermute | solution.py:167
  71.9 6.3 %collective-permute-start.6 = (f32[72,384]{1,0:T(8,128)S(1)}, f32[72,384]{1,0:T(8,128)S(1)}, u32[]{:S(2)}, u32[]{:S(2)}) collective-permute-start(f32[72,384]{1,0:T(8,128)S(1)} %add.174), channel_id=1, source_target_pairs={{0,4},{1,5},{2,6},{3,7},{4,0},{5,1},{6,2},{7,3},{8,12},{9,13},{10,... | collective-permute-start | bytes 331784 | tf_op jit(solution)/shard_map/ppermute | solution.py:167
  78.2 4.8 %collective-permute-start.7 = (f32[72,384]{1,0:T(8,128)S(1)}, f32[72,384]{1,0:T(8,128)S(1)}, u32[]{:S(2)}, u32[]{:S(2)}) collective-permute-start(f32[72,384]{1,0:T(8,128)S(1)} %add.175), channel_id=1, source_target_pairs={{0,16},{1,17},{2,18},{3,19},{4,20},{5,21},{6,22},{7,23},{8,24},{9,... | collective-permute-start | bytes 331784 | tf_op jit(solution)/shard_map/ppermute | solution.py:167
  83.1 1.4 %copy-start.2 = (f32[72,384]{1,0:T(8,128)}, f32[72,384]{1,0:T(8,128)S(1)}, u32[]{:S(2)}) copy-start(f32[72,384]{1,0:T(8,128)S(1)} %add.176.mine_ref) | copy-start | bytes 331780
  83.1 1.4 %collective-permute-start.8 = (f32[72,384]{1,0:T(8,128)S(1)}, f32[72,384]{1,0:T(8,128)S(1)}, u32[]{:S(2)}, u32[]{:S(2)}) collective-permute-start(f32[72,384]{1,0:T(8,128)S(1)} %add.176.mine_ref), channel_id=1, source_target_pairs={{0,8},{1,9},{2,10},{3,11},{4,12},{5,13},{6,14},{7,15},{8,0},{9,1},... | collective-permute-start | bytes 331784 | tf_op jit(solution)/shard_map/ppermute | solution.py:171
  84.5 0.7 copy-start.4

commit v14 on v13

--- a/solution.py
+++ b/solution.py
@@ -30,10 +30,11 @@
     return jnp.where(upper, jnp.concatenate([other, x], 1), jnp.concatenate([x, other], 1))
 
 
-def label_kernel(first, place_ref, emb_ref, lab_ref, rate_ref, ints_ref, keep_ref, send_ref, rate_out_ref):
+def label_kernel(first, n_label, emb_ref, lab_ref, rate_ref, ints_ref, keep_ref, send_ref, rate_out_ref):
     tile = pl.program_id(0)
-    upper = place_ref[0] == 1
-    base = place_ref[1]
+    me = lax.axis_index(AXES)
+    upper = (me // n_label) % 2 == 1
+    base = me * lab_ref.shape[0] * pl.num_programs(0)
     docs, half = send_ref.shape[0] - 8, send_ref.shape[1]
     width = lab_ref.shape[0]
     n_pos = ints_ref.shape[1] - 1 - first
@@ -81,27 +82,26 @@
         send_ref[...] += send
 
 
-def label_pass(place, emb, label_matrix, log_rates, ints, first):
+def label_pass(emb, label_matrix, log_rates, ints, first, n_label):
     rows, depth = emb.shape
     docs = ints.shape[0]
     labels = label_matrix.shape[0]
     width = 1024 if labels % 1024 == 0 else labels
     half = depth // 2
     return pl.pallas_call(
-        functools.partial(label_kernel, first),
-        grid_spec=pltpu.PrefetchScalarGridSpec(
-            num_scalar_prefetch=1,
+        functools.partial(label_kernel, first, n_label),
+        grid_spec=pl.GridSpec(
             grid=(labels // width,),
             in_specs=[
-                pl.BlockSpec((rows, depth), lambda i, p: (0, 0)),
-                pl.BlockSpec((width, depth), lambda i, p: (i, 0)),
-                pl.BlockSpec((1, width), lambda i, p: (0, i)),
-                pl.BlockSpec(ints.shape, lambda i, p: (0, 0)),
+                pl.BlockSpec((rows, depth), lambda i: (0, 0)),
+                pl.BlockSpec((width, depth), lambda i: (i, 0)),
+                pl.BlockSpec((1, width), lambda i: (0, i)),
+                pl.BlockSpec(ints.shape, lambda i: (0, 0)),
             ],
             out_specs=[
-                pl.BlockSpec((docs + 8, half), lambda i, p: (0, 0)),
-                pl.BlockSpec((docs + 8, half), lambda i, p: (0, 0)),
-                pl.BlockSpec((1, width), lambda i, p: (0, i)),
+                pl.BlockSpec((docs + 8, half), lambda i: (0, 0)),
+                pl.BlockSpec((docs + 8, half), lambda i: (0, 0)),
+                pl.BlockSpec((1, width), lambda i: (0, i)),
             ],
         ),
         out_shape=[
@@ -110,7 +110,7 @@
             jax.ShapeDtypeStruct((1, labels), jnp.float32),
         ],
         compiler_params=pltpu.CompilerParams(dimension_semantics=("arbitrary",)),
-    )(place, emb, label_matrix, log_rates, ints)
+    )(emb, label_matrix, log_rates, ints)
 
 
 def tail_kernel(upper_ref, mine_ref, other_ref, pre_ref, pooled_t_ref, weight_ref, loss_ref):
@@ -203,9 +203,8 @@
         emb = unit.astype(jnp.bfloat16)
 
         upper = (me // n_label) % 2
-        place = jnp.stack([upper, me * label_rows]).astype(jnp.int32)
         keep, send, new_rates = label_pass(
-            place, emb, label_matrix, label_log_rates[None, :], every, views * title
+            emb, label_matrix, label_log_rates[None, :], every, views * title, n_label
         )
         new_log_rates = new_rates[0]
 

time: 89.4 us -> 88.7 us (level)
  transfers between devices with their start and end apart: 10 -> 10, of which waited for: 10 -> 10; matrix products, arithmetic and copies ran while one was open for 2% -> 1% of each run, Pallas kernels for 0% -> 0%
where the time goes in v14:
time: 88.7 us; the launch traced here: 88.3 us
  waiting for transfers between devices  34.8 us (39%)
  blocking collectives  21.7 us (24%)
  Pallas kernels  12.2 us (14%)
  starting transfers between devices  9.93 us (11%)
  local copies, waits for them, and re-layouts  4.04 us (5%)
  other arithmetic  2.66 us (3%)
  matrix products  2.17 us (2%)
    ppermute x4, waiting for transfers between devices, split_sum(): x = x + lax.ppermute(x, AXES, [(i, i ^ step) for i in range(n)])  19 us
    all_to_all x1, blocking collectives, tree_sum(): lax.all_to_all(x.reshape(n_label, rows // n_label, half), 'label', 0, 0,...  10.9 us
    all_to_all x1, blocking collectives, tree_sum(): x = lax.all_to_all(every, 'label', 0, 0, tiled=False).reshape(rows, half)  10.7 us
    pallas_call x1, Pallas kernels, label_pass(): pl.pallas_call(functools.partial(label_kernel, first, n_label), grid_spec...  8.4 us
    all_to_all x1, starting transfers between devices, shards(): lax.all_to_all(spread, AXES, 0, 0, tiled=False)  7.33 us
    all_to_all x1, waiting for transfers between devices, shards(): lax.all_to_all(spread, AXES, 0, 0, tiled=False)  7.15 us
    pallas_call x1, Pallas kernels, tail_pass(): pl.pallas_call(tail_kernel, in_specs=[pl.BlockSpec(memory_space=pltpu.Mem...  3.82 us
    ppermute x1, waiting for transfers between devices, tree_sum(): part = part + lax.ppermute(part, AXES, [(i, i ^ step) for i in range(n)])  3.2 us
  transfers between devices with their start and end apart: 10, of which 10 were waited for; matrix products, arithmetic and copies ran while one was open for 1% of the time, Pallas kernels for 0%

profile of v14, /device:TPU:0, one launch (start us, length us, event | category | flops | bytes accessed | tf_op | source)
XLA Modules:
  0.0 88.3 jit_solution(4776404727684041002)
XLA Ops:
  0.6 0.0 copy-start
  0.6 0.9 reshape.35
  1.5 0.7 copy.17
  2.2 0.8 pad_add_fusion
  3.0 0.6 broadcast_in_dim.12
  3.6 7.3 %all-to-all-start = ((s32[32,2,81]{2,1,0:T(2,128)}), s32[32,2,81]{2,1,0:T(2,128)S(1)}, u32[]{:S(2)}, u32[]{:S(2)}) async-start(s32[32,2,81]{2,1,0:T(2,128)} %broadcast_in_dim.12), calls=%async_computation | async-start | bytes 65536 | tf_op jit(solution)/shard_map/all_to_all | solution.py:189
  11.0 7.2 %all-to-all-done = s32[32,2,81]{2,1,0:T(2,128)S(1)} async-done(((s32[32,2,81]{2,1,0:T(2,128)}), s32[32,2,81]{2,1,0:T(2,128)S(1)}, u32[]{:S(2)}, u32[]{:S(2)}) %all-to-all-start) | async-done | bytes 20768 | tf_op jit(solution)/shard_map/all_to_all | solution.py:189
  18.1 0.0 copy-start.3
  18.2 0.1 copy.18
  18.3 0.1 sub.25
  18.4 1.7 %fusion.2 = f32[128,768]{1,0:T(8,128)S(1)} fusion(bf16[128,768]{1,0:T(8,128)(2,1)} %param.10, s32[128]{0:T(128)S(1)} %get-tuple-element.18, s32[128]{0:T(128)S(1)} %get-tuple-element.19, s32[128]{0:T(128)S(1)} %get-tuple-element.20, s32[128]{0:T(128)S(1)} %get-tuple-element.21, s32[128]{0:T(128)S(1)} %get-tuple-element.22, s32[128]{0:T(128)S(1)} %get-tuple-element.23, ...), kind=kOutput, calls=%fused_computation.41 | convolution fusion | flops 26738688 | bytes 606208 | tf_op jit(solution)/shard_map/dot_general | solution.py:197
  20.2 0.0 copy-done.3
  20.2 0.2 collective-permute-start
  20.4 1.3 %collective-permute-done = f32[128,384]{1,0:T(8,128)S(1)} collective-permute-done((f32[128,384]{1,0:T(8,128)S(1)}, f32[128,384]{1,0:T(8,128)S(1)}, u32[]{:S(2)}, u32[]{:S(2)}) %collective-permute-start) | collective-permute-done | bytes 196640 | tf_op jit(solution)/shard_map/ppermute | solution.py:19
  21.7 10.9 %all_to_all.15 = f32[8,16,384]{2,1,0:T(8,128)S(1)} all-to-all(f32[8,16,384]{2,1,0:T(8,128)S(1)} %bitcast.83), channel_id=1, replica_groups=mesh['dp'=4,'label'=8] {'label'}, dimensions={0} | all-to-all | bytes 393216 | tf_op jit(solution)/shard_map/all_to_all | solution.py:21
  32.7 0.7 collective-permute-start.1
  33.4 3.2 %collective-permute-done.1 = f32[16,384]{1,0:T(8,128)S(1)} collective-permute-done((f32[16,384]{1,0:T(8,128)S(1)}, f32[16,384]{1,0:T(8,128)S(1)}, u32[]{:S(2)}, u32[]{:S(2)}) %collective-permute-start.1) | collective-permute-done | bytes 24608 | tf_op jit(solution)/shard_map/ppermute | solution.py:25
  36.6 10.7 %all_to_all.16 = f32[8,16,384]{2,1,0:T(8,128)S(1)} all-to-all(f32[8,16,384]{2,1,0:T(8,128)S(1)} %broadcast_in_dim.13), channel_id=1, replica_groups=mesh['dp'=4,'label'=8] {'label'}, dimensions={0} | all-to-all | bytes 393216 | tf_op jit(solution)/shard_map/all_to_all | solution.py:28
  47.3 0.1 copy.20
  47.4 0.1 collective-permute-start.2
  47.5 1.4 %collective-permute-done.2 = f32[128,384]{0,1:T(8,128)S(1)} collective-permute-done((f32[128,384]{0,1:T(8,128)S(1)}, f32[128,384]{0,1:T(8,128)S(1)}, u32[]{:S(2)}, u32[]{:S(2)}) %collective-permute-start.2) | collective-permute-done | bytes 196640 | tf_op jit(solution)/shard_map/ppermute | solution.py:29
  48.9 0.1 fusion.1
  49.0 0.0 copy-done
  49.0 0.4 multiply_reduce_fusion
  49.5 0.0 copy-start.1
  49.5 0.8 multiply_convert_fusion.emb_ref
  50.3 8.4 %shard_map.94 = (f32[72,384]{1,0:T(8,128)}, f32[72,384]{1,0:T(8,128)}, f32[1,5120]{1,0:T(1,128)}) custom-call(bf16[128,768]{1,0:T(8,128)(2,1)} %multiply_convert_fusion.emb_ref, bf16[5120,768]{1,0:T(8,128)(2,1)} %lab_ref.1, f32[1,5120]{1,0:T(1,128)} %bitcast.87, s32[64,81]{1,0:T(8,128)} %bitcast.85), custom_call_target="tpu_custom_call" | custom-call | tf_op jit(solution)/shard_map/pallas_call | solution.py:91
  58.7 0.0 copy-done.1
  58.7 0.2 collective-permute-start.3
  58.9 1.4 %collective-permute-done.3 = f32[72,384]{1,0:T(8,128)S(1)} collective-permute-done((f32[72,384]{1,0:T(8,128)}, f32[72,384]{1,0:T(8,128)S(1)}, u32[]{:S(2)}, u32[]{:S(2)}) %collective-permute-start.3) | collective-permute-done | bytes 110624 | tf_op jit(solution)/shard_map/ppermute | solution.py:163
  60.3 0.9 %add.172 = f32[72,384]{1,0:T(8,128)S(1)} add(f32[72,384]{1,0:T(8,128)} %get-tuple-element.10, f32[72,384]{1,0:T(8,128)S(1)} %collective-permute-done.3) | non-fusion elementwise | flops 27648 | bytes 331776 | tf_op jit(solution)/shard_map/add | solution.py:163
  61.2 0.1 collective-permute-start.4
  61.3 0.8 slice_bitcast_fusion.pooled_t_ref
  62.1 4.3 %collective-permute-done.4 = f32[72,384]{1,0:T(8,128)S(1)} collective-permute-done((f32[72,384]{1,0:T(8,128)S(1)}, f32[72,384]{1,0:T(8,128)S(1)}, u32[]{:S(2)}, u32[]{:S(2)}) %collective-permute-start.4) | collective-permute-done | bytes 110624 | tf_op jit(solution)/shard_map/ppermute | solution.py:167
  66.4 0.1 collective-permute-start.5
  66.5 4.7 %collective-permute-done.5 = f32[72,384]{1,0:T(8,128)S(1)} collective-permute-done((f32[72,384]{1,0:T(8,128)S(1)}, f32[72,384]{1,0:T(8,128)S(1)}, u32[]{:S(2)}, u32[]{:S(2)}) %collective-permute-start.5) | collective-permute-done | bytes 110624 | tf_op jit(solution)/shard_map/ppermute | solution.py:167
  71.2 0.5 collective-permute-start.6
  71.7 5.8 %collective-permute-done.6 = f32[72,384]{1,0:T(8,128)S(1)} collective-permute-done((f32[72,384]{1,0:T(8,128)S(1)}, f32[72,384]{1,0:T(8,128)S(1)}, u32[]{:S(2)}, u32[]{:S(2)}) %collective-permute-start.6) | collective-permute-done | bytes 110624 | tf_op jit(solution)/shard_map/ppermute | solution.py:167
  77.6 0.7 collective-permute-start.7
  78.3 4.1 %collective-permute-done.7 = f32[72,384]{1,0:T(8,128)S(1)} collective-permute-done((f32[72,384]{1,0:T(8,128)S(1)}, f32[72,384]{1,0:T(8,128)S(1)}, u32[]{:S(2)}, u32[]{:S(2)}) %collective-permute-start.7) | collective-permute-done | bytes 110624 | tf_op jit(solution)/shard_map/ppermute | solution.py:167
  82.4 0.0 copy-start.2
  82.4 0.1 collective-permute-start.8
  82.5 1.3 %collective-permute-done.8.other_ref = f32[72,384]{1,0:T(8,128)S(1)} collective-permute-done((f32[72,384]{1,0:T(8,128)S(1)}, f32[72,384]{1,0:T(8,128)S(1)}, u32[]{:S(2)}, u32[]{:S(2)}) %collective-permute-start.8) | collective-permute-done | bytes 110624 | tf_op jit(solution)/shard_map/ppermute | solution.py:171
  83.8 0.0 copy-start.4
  83.8 0.0 copy-done.2
  83.8 0.6 copy-done.4
  84.5 3.8 %shard_map.95 = (f32[768,768]{1,0:T(8,128)}, f32[1,1]{1,0:T(1,128)}) custom-call(s32[1]{0:T(128)} %bitcast.upper_ref, f32[72,384]{1,0:T(8,128)} %copy-done.2, f32[72,384]{1,0:T(8,128)} %copy-done.4, f32[128,768]{1,0:T(8,128)} %copy-done.1, bf16[768,64]{1,0:T(8,128)(2,1)} %slice_bitcast_fusion.pooled_t_ref), custom_call_target="tpu_custom_call" | custom-call | tf_op jit(solution)/shard_map/pallas_call | solution.py:150
  (14 shorter events, 0.2 us)
Async XLA Ops:
  0.6 48.4 %copy-start = (bf16[768,768]{1,0:T(8,128)(2,1)S(1)}, bf16[768,768]{1,0:T(8,128)(2,1)}, u32[]{:S(2)}) copy-start(bf16[768,768]{1,0:T(8,128)(2,1)} %param.11) | copy-start | bytes 3538948
  3.6 14.5 %all-to-all-start = ((s32[32,2,81]{2,1,0:T(2,128)}), s32[32,2,81]{2,1,0:T(2,128)S(1)}, u32[]{:S(2)}, u32[]{:S(2)}) async-start(s32[32,2,81]{2,1,0:T(2,128)} %broadcast_in_dim.12), calls=%async_computation | async-start | bytes 65536 | tf_op jit(solution)/shard_map/all_to_all | solution.py:189
  18.1 2.0 %copy-start.3 = (s32[32,2,81]{2,1,0:T(2,128)}, s32[32,2,81]{2,1,0:T(2,128)S(1)}, u32[]{:S(2)}) copy-start(s32[32,2,81]{2,1,0:T(2,128)S(1)} %all-to-all-done) | copy-start | bytes 62212
  20.2 1.5 %collective-permute-start = (f32[128,384]{1,0:T(8,128)S(1)}, f32[128,384]{1,0:T(8,128)S(1)}, u32[]{:S(2)}, u32[]{:S(2)}) collective-permute-start(f32[128,384]{1,0:T(8,128)S(1)} %slice_select_fusion), channel_id=1, source_target_pairs={{0,8},{1,9},{2,10},{3,11},{4,12},{5,13},{6,14},{7,15},{8,0},{9,1},... | collective-permute-start | bytes 589832 | tf_op jit(solution)/shard_map/ppermute | solution.py:19
  32.7 3.9 %collective-permute-start.1 = (f32[16,384]{1,0:T(8,128)S(1)}, f32[16,384]{1,0:T(8,128)S(1)}, u32[]{:S(2)}, u32[]{:S(2)}) collective-permute-start(f32[16,384]{1,0:T(8,128)S(1)} %reduce_sum.18), channel_id=1, source_target_pairs={{0,16},{1,17},{2,18},{3,19},{4,20},{5,21},{6,22},{7,23},{8,24},{9,... | collective-permute-start | bytes 73736 | tf_op jit(solution)/shard_map/ppermute | solution.py:25
  47.4 1.5 %collective-permute-start.2 = (f32[128,384]{0,1:T(8,128)S(1)}, f32[128,384]{0,1:T(8,128)S(1)}, u32[]{:S(2)}, u32[]{:S(2)}) collective-permute-start(f32[128,384]{0,1:T(8,128)S(1)} %copy.20), channel_id=1, source_target_pairs={{0,8},{1,9},{2,10},{3,11},{4,12},{5,13},{6,14},{7,15},{8,0},{9,1},... | collective-permute-start | bytes 589832 | tf_op jit(solution)/shard_map/ppermute | solution.py:29
  49.5 9.2 %copy-start.1 = (f32[128,768]{1,0:T(8,128)}, f32[128,768]{1,0:T(8,128)S(1)}, u32[]{:S(2)}) copy-start(f32[128,768]{1,0:T(8,128)S(1)} %get-tuple-element.50.pre_ref) | copy-start | bytes 1179652
  58.7 1.6 %collective-permute-start.3 = (f32[72,384]{1,0:T(8,128)}, f32[72,384]{1,0:T(8,128)S(1)}, u32[]{:S(2)}, u32[]{:S(2)}) collective-permute-start(f32[72,384]{1,0:T(8,128)} %get-tuple-element.11), channel_id=1, source_target_pairs={{0,8},{1,9},{2,10},{3,11},{4,12},{5,13},{6,14},{7,15},{8,0},{9,1},... | collective-permute-start | bytes 331784 | tf_op jit(solution)/shard_map/ppermute | solution.py:163
  61.2 5.2 %collective-permute-start.4 = (f32[72,384]{1,0:T(8,128)S(1)}, f32[72,384]{1,0:T(8,128)S(1)}, u32[]{:S(2)}, u32[]{:S(2)}) collective-permute-start(f32[72,384]{1,0:T(8,128)S(1)} %add.172), channel_id=1, source_target_pairs={{0,1},{1,0},{2,3},{3,2},{4,5},{5,4},{6,7},{7,6},{8,9},{9,8},{10,11... | collective-permute-start | bytes 331784 | tf_op jit(solution)/shard_map/ppermute | solution.py:167
  66.4 4.8 %collective-permute-start.5 = (f32[72,384]{1,0:T(8,128)S(1)}, f32[72,384]{1,0:T(8,128)S(1)}, u32[]{:S(2)}, u32[]{:S(2)}) collective-permute-start(f32[72,384]{1,0:T(8,128)S(1)} %add.173), channel_id=1, source_target_pairs={{0,2},{1,3},{2,0},{3,1},{4,6},{5,7},{6,4},{7,5},{8,10},{9,11},{10,... | collective-permute-start | bytes 331784 | tf_op jit(solution)/shard_map/ppermute | solution.py:167
  71.2 6.3 %collective-permute-start.6 = (f32[72,384]{1,0:T(8,128)S(1)}, f32[72,384]{1,0:T(8,128)S(1)}, u32[]{:S(2)}, u32[]{:S(2)}) collective-permute-start(f32[72,384]{1,0:T(8,128)S(1)} %add.174), channel_id=1, source_target_pairs={{0,4},{1,5},{2,6},{3,7},{4,0},{5,1},{6,2},{7,3},{8,12},{9,13},{10,... | collective-permute-start | bytes 331784 | tf_op jit(solution)/shard_map/ppermute | solution.py:167
  77.6 4.8 %collective-permute-start.7 = (f32[72,384]{1,0:T(8,128)S(1)}, f32[72,384]{1,0:T(8,128)S(1)}, u32[]{:S(2)}, u32[]{:S(2)}) collective-permute-start(f32[72,384]{1,0:T(8,128)S(1)} %add.175), channel_id=1, source_target_pairs={{0,16},{1,17},{2,18},{3,19},{4,20},{5,21},{6,22},{7,23},{8,24},{9,... | collective-permute-start | bytes 331784 | tf_op jit(solution)/shard_map/ppermute | solution.py:167
  82.4 1.4 %copy-start.2 = (f32[72,384]{1,0:T(8,128)}, f32[72,384]{1,0:T(8,128)S(1)}, u32[]{:S(2)}) copy-start(f32[72,384]{1,0:T(8,128)S(1)} %add.176.mine_ref) | copy-start | bytes 331780
  82.4 1.4 %collective-permute-start.8 = (f32[72,384]{1,0:T(8,128)S(1)}, f32[72,384]{1,0:T(8,128)S(1)}, u32[]{:S(2)}, u32[]{:S(2)}) collective-permute-start(f32[72,384]{1,0:T(8,128)S(1)} %add.176.mine_ref), channel_id=1, source_target_pairs={{0,8},{1,9},{2,10},{3,11},{4,12},{5,13},{6,14},{7,15},{8,0},{9,1},... | collective-permute-start | bytes 331784 | tf_op jit(solution)/shard_map/ppermute | solution.py:171
  83.8 0.7 copy-start.4

commit v15 on v14

--- a/solution.py
+++ b/solution.py
@@ -86,7 +86,7 @@
     rows, depth = emb.shape
     docs = ints.shape[0]
     labels = label_matrix.shape[0]
-    width = 1024 if labels % 1024 == 0 else labels
+    width = 2560 if labels % 2560 == 0 and rows <= 256 else (1024 if labels % 1024 == 0 else labels)
     half = depth // 2
     return pl.pallas_call(
         functools.partial(label_kernel, first, n_label),

time: 88.7 us -> 88.9 us (level)
  no operation moved by 1% of the time
where the time goes in v15:
time: 88.9 us; the launch traced here: 88.6 us
  waiting for transfers between devices  34.8 us (39%)
  blocking collectives  21.7 us (24%)
  Pallas kernels  12.5 us (14%)
  starting transfers between devices  9.93 us (11%)
  local copies, waits for them, and re-layouts  4.04 us (5%)
  other arithmetic  2.66 us (3%)
  matrix products  2.17 us (2%)
    ppermute x4, waiting for transfers between devices, split_sum(): x = x + lax.ppermute(x, AXES, [(i, i ^ step) for i in range(n)])  19 us
    all_to_all x1, blocking collectives, tree_sum(): lax.all_to_all(x.reshape(n_label, rows // n_label, half), 'label', 0, 0,...  10.9 us
    all_to_all x1, blocking collectives, tree_sum(): x = lax.all_to_all(every, 'label', 0, 0, tiled=False).reshape(rows, half)  10.7 us
    pallas_call x1, Pallas kernels, label_pass(): pl.pallas_call(functools.partial(label_kernel, first, n_label), grid_spec...  8.69 us
    all_to_all x1, starting transfers between devices, shards(): lax.all_to_all(spread, AXES, 0, 0, tiled=False)  7.33 us
    all_to_all x1, waiting for transfers between devices, shards(): lax.all_to_all(spread, AXES, 0, 0, tiled=False)  7.15 us
    pallas_call x1, Pallas kernels, tail_pass(): pl.pallas_call(tail_kernel, in_specs=[pl.BlockSpec(memory_space=pltpu.Mem...  3.82 us
    ppermute x1, waiting for transfers between devices, tree_sum(): part = part + lax.ppermute(part, AXES, [(i, i ^ step) for i in range(n)])  3.2 us
  transfers between devices with their start and end apart: 10, of which 10 were waited for; matrix products, arithmetic and copies ran while one was open for 1% of the time, Pallas kernels for 0%

profile of v15, /device:TPU:0, one launch (start us, length us, event | category | flops | bytes accessed | tf_op | source)
XLA Modules:
  0.0 88.6 jit_solution(11337265116683888973)
XLA Ops:
  0.6 0.0 copy-start
  0.6 0.9 reshape.35
  1.5 0.7 copy.17
  2.2 0.8 pad_add_fusion
  3.0 0.6 broadcast_in_dim.12
  3.6 7.3 %all-to-all-start = ((s32[32,2,81]{2,1,0:T(2,128)}), s32[32,2,81]{2,1,0:T(2,128)S(1)}, u32[]{:S(2)}, u32[]{:S(2)}) async-start(s32[32,2,81]{2,1,0:T(2,128)} %broadcast_in_dim.12), calls=%async_computation | async-start | bytes 65536 | tf_op jit(solution)/shard_map/all_to_all | solution.py:189
  11.0 7.2 %all-to-all-done = s32[32,2,81]{2,1,0:T(2,128)S(1)} async-done(((s32[32,2,81]{2,1,0:T(2,128)}), s32[32,2,81]{2,1,0:T(2,128)S(1)}, u32[]{:S(2)}, u32[]{:S(2)}) %all-to-all-start) | async-done | bytes 20768 | tf_op jit(solution)/shard_map/all_to_all | solution.py:189
  18.1 0.0 copy-start.3
  18.2 0.1 copy.18
  18.3 0.1 sub.25
  18.4 1.7 %fusion.2 = f32[128,768]{1,0:T(8,128)S(1)} fusion(bf16[128,768]{1,0:T(8,128)(2,1)} %param.10, s32[128]{0:T(128)S(1)} %get-tuple-element.18, s32[128]{0:T(128)S(1)} %get-tuple-element.19, s32[128]{0:T(128)S(1)} %get-tuple-element.20, s32[128]{0:T(128)S(1)} %get-tuple-element.21, s32[128]{0:T(128)S(1)} %get-tuple-element.22, s32[128]{0:T(128)S(1)} %get-tuple-element.23, ...), kind=kOutput, calls=%fused_computation.41 | convolution fusion | flops 26738688 | bytes 606208 | tf_op jit(solution)/shard_map/dot_general | solution.py:197
  20.2 0.0 copy-done.3
  20.2 0.2 collective-permute-start
  20.4 1.3 %collective-permute-done = f32[128,384]{1,0:T(8,128)S(1)} collective-permute-done((f32[128,384]{1,0:T(8,128)S(1)}, f32[128,384]{1,0:T(8,128)S(1)}, u32[]{:S(2)}, u32[]{:S(2)}) %collective-permute-start) | collective-permute-done | bytes 196640 | tf_op jit(solution)/shard_map/ppermute | solution.py:19
  21.7 10.9 %all_to_all.15 = f32[8,16,384]{2,1,0:T(8,128)S(1)} all-to-all(f32[8,16,384]{2,1,0:T(8,128)S(1)} %bitcast.83), channel_id=1, replica_groups=mesh['dp'=4,'label'=8] {'label'}, dimensions={0} | all-to-all | bytes 393216 | tf_op jit(solution)/shard_map/all_to_all | solution.py:21
  32.7 0.7 collective-permute-start.1
  33.4 3.2 %collective-permute-done.1 = f32[16,384]{1,0:T(8,128)S(1)} collective-permute-done((f32[16,384]{1,0:T(8,128)S(1)}, f32[16,384]{1,0:T(8,128)S(1)}, u32[]{:S(2)}, u32[]{:S(2)}) %collective-permute-start.1) | collective-permute-done | bytes 24608 | tf_op jit(solution)/shard_map/ppermute | solution.py:25
  36.6 10.7 %all_to_all.16 = f32[8,16,384]{2,1,0:T(8,128)S(1)} all-to-all(f32[8,16,384]{2,1,0:T(8,128)S(1)} %broadcast_in_dim.13), channel_id=1, replica_groups=mesh['dp'=4,'label'=8] {'label'}, dimensions={0} | all-to-all | bytes 393216 | tf_op jit(solution)/shard_map/all_to_all | solution.py:28
  47.3 0.1 copy.20
  47.4 0.1 collective-permute-start.2
  47.5 1.4 %collective-permute-done.2 = f32[128,384]{0,1:T(8,128)S(1)} collective-permute-done((f32[128,384]{0,1:T(8,128)S(1)}, f32[128,384]{0,1:T(8,128)S(1)}, u32[]{:S(2)}, u32[]{:S(2)}) %collective-permute-start.2) | collective-permute-done | bytes 196640 | tf_op jit(solution)/shard_map/ppermute | solution.py:29
  48.9 0.1 fusion.1
  49.0 0.0 copy-done
  49.0 0.4 multiply_reduce_fusion
  49.5 0.0 copy-start.1
  49.5 0.8 multiply_convert_fusion.emb_ref
  50.3 8.7 %shard_map.94 = (f32[72,384]{1,0:T(8,128)}, f32[72,384]{1,0:T(8,128)}, f32[1,5120]{1,0:T(1,128)}) custom-call(bf16[128,768]{1,0:T(8,128)(2,1)} %multiply_convert_fusion.emb_ref, bf16[5120,768]{1,0:T(8,128)(2,1)} %lab_ref.1, f32[1,5120]{1,0:T(1,128)} %bitcast.87, s32[64,81]{1,0:T(8,128)} %bitcast.85), custom_call_target="tpu_custom_call" | custom-call | tf_op jit(solution)/shard_map/pallas_call | solution.py:91
  59.0 0.0 copy-done.1
  59.0 0.2 collective-permute-start.3
  59.2 1.4 %collective-permute-done.3 = f32[72,384]{1,0:T(8,128)S(1)} collective-permute-done((f32[72,384]{1,0:T(8,128)}, f32[72,384]{1,0:T(8,128)S(1)}, u32[]{:S(2)}, u32[]{:S(2)}) %collective-permute-start.3) | collective-permute-done | bytes 110624 | tf_op jit(solution)/shard_map/ppermute | solution.py:163
  60.6 0.9 %add.172 = f32[72,384]{1,0:T(8,128)S(1)} add(f32[72,384]{1,0:T(8,128)} %get-tuple-element.10, f32[72,384]{1,0:T(8,128)S(1)} %collective-permute-done.3) | non-fusion elementwise | flops 27648 | bytes 331776 | tf_op jit(solution)/shard_map/add | solution.py:163
  61.5 0.1 collective-permute-start.4
  61.6 0.8 slice_bitcast_fusion.pooled_t_ref
  62.4 4.3 %collective-permute-done.4 = f32[72,384]{1,0:T(8,128)S(1)} collective-permute-done((f32[72,384]{1,0:T(8,128)S(1)}, f32[72,384]{1,0:T(8,128)S(1)}, u32[]{:S(2)}, u32[]{:S(2)}) %collective-permute-start.4) | collective-permute-done | bytes 110624 | tf_op jit(solution)/shard_map/ppermute | solution.py:167
  66.7 0.1 collective-permute-start.5
  66.8 4.7 %collective-permute-done.5 = f32[72,384]{1,0:T(8,128)S(1)} collective-permute-done((f32[72,384]{1,0:T(8,128)S(1)}, f32[72,384]{1,0:T(8,128)S(1)}, u32[]{:S(2)}, u32[]{:S(2)}) %collective-permute-start.5) | collective-permute-done | bytes 110624 | tf_op jit(solution)/shard_map/ppermute | solution.py:167
  71.5 0.5 collective-permute-start.6
  72.0 5.8 %collective-permute-done.6 = f32[72,384]{1,0:T(8,128)S(1)} collective-permute-done((f32[72,384]{1,0:T(8,128)S(1)}, f32[72,384]{1,0:T(8,128)S(1)}, u32[]{:S(2)}, u32[]{:S(2)}) %collective-permute-start.6) | collective-permute-done | bytes 110624 | tf_op jit(solution)/shard_map/ppermute | solution.py:167
  77.9 0.7 collective-permute-start.7
  78.6 4.1 %collective-permute-done.7 = f32[72,384]{1,0:T(8,128)S(1)} collective-permute-done((f32[72,384]{1,0:T(8,128)S(1)}, f32[72,384]{1,0:T(8,128)S(1)}, u32[]{:S(2)}, u32[]{:S(2)}) %collective-permute-start.7) | collective-permute-done | bytes 110624 | tf_op jit(solution)/shard_map/ppermute | solution.py:167
  82.7 0.0 copy-start.2
  82.7 0.1 collective-permute-start.8
  82.8 1.3 %collective-permute-done.8.other_ref = f32[72,384]{1,0:T(8,128)S(1)} collective-permute-done((f32[72,384]{1,0:T(8,128)S(1)}, f32[72,384]{1,0:T(8,128)S(1)}, u32[]{:S(2)}, u32[]{:S(2)}) %collective-permute-start.8) | collective-permute-done | bytes 110624 | tf_op jit(solution)/shard_map/ppermute | solution.py:171
  84.1 0.0 copy-start.4
  84.1 0.0 copy-done.2
  84.1 0.6 copy-done.4
  84.7 3.8 %shard_map.95 = (f32[768,768]{1,0:T(8,128)}, f32[1,1]{1,0:T(1,128)}) custom-call(s32[1]{0:T(128)} %bitcast.upper_ref, f32[72,384]{1,0:T(8,128)} %copy-done.2, f32[72,384]{1,0:T(8,128)} %copy-done.4, f32[128,768]{1,0:T(8,128)} %copy-done.1, bf16[768,64]{1,0:T(8,128)(2,1)} %slice_bitcast_fusion.pooled_t_ref), custom_call_target="tpu_custom_call" | custom-call | tf_op jit(solution)/shard_map/pallas_call | solution.py:150
  (14 shorter events, 0.2 us)
Async XLA Ops:
  0.6 48.4 %copy-start = (bf16[768,768]{1,0:T(8,128)(2,1)S(1)}, bf16[768,768]{1,0:T(8,128)(2,1)}, u32[]{:S(2)}) copy-start(bf16[768,768]{1,0:T(8,128)(2,1)} %param.11) | copy-start | bytes 3538948
  3.6 14.5 %all-to-all-start = ((s32[32,2,81]{2,1,0:T(2,128)}), s32[32,2,81]{2,1,0:T(2,128)S(1)}, u32[]{:S(2)}, u32[]{:S(2)}) async-start(s32[32,2,81]{2,1,0:T(2,128)} %broadcast_in_dim.12), calls=%async_computation | async-start | bytes 65536 | tf_op jit(solution)/shard_map/all_to_all | solution.py:189
  18.1 2.0 %copy-start.3 = (s32[32,2,81]{2,1,0:T(2,128)}, s32[32,2,81]{2,1,0:T(2,128)S(1)}, u32[]{:S(2)}) copy-start(s32[32,2,81]{2,1,0:T(2,128)S(1)} %all-to-all-done) | copy-start | bytes 62212
  20.2 1.5 %collective-permute-start = (f32[128,384]{1,0:T(8,128)S(1)}, f32[128,384]{1,0:T(8,128)S(1)}, u32[]{:S(2)}, u32[]{:S(2)}) collective-permute-start(f32[128,384]{1,0:T(8,128)S(1)} %slice_select_fusion), channel_id=1, source_target_pairs={{0,8},{1,9},{2,10},{3,11},{4,12},{5,13},{6,14},{7,15},{8,0},{9,1},... | collective-permute-start | bytes 589832 | tf_op jit(solution)/shard_map/ppermute | solution.py:19
  32.7 3.9 %collective-permute-start.1 = (f32[16,384]{1,0:T(8,128)S(1)}, f32[16,384]{1,0:T(8,128)S(1)}, u32[]{:S(2)}, u32[]{:S(2)}) collective-permute-start(f32[16,384]{1,0:T(8,128)S(1)} %reduce_sum.18), channel_id=1, source_target_pairs={{0,16},{1,17},{2,18},{3,19},{4,20},{5,21},{6,22},{7,23},{8,24},{9,... | collective-permute-start | bytes 73736 | tf_op jit(solution)/shard_map/ppermute | solution.py:25
  47.4 1.5 %collective-permute-start.2 = (f32[128,384]{0,1:T(8,128)S(1)}, f32[128,384]{0,1:T(8,128)S(1)}, u32[]{:S(2)}, u32[]{:S(2)}) collective-permute-start(f32[128,384]{0,1:T(8,128)S(1)} %copy.20), channel_id=1, source_target_pairs={{0,8},{1,9},{2,10},{3,11},{4,12},{5,13},{6,14},{7,15},{8,0},{9,1},... | collective-permute-start | bytes 589832 | tf_op jit(solution)/shard_map/ppermute | solution.py:29
  49.5 9.5 %copy-start.1 = (f32[128,768]{1,0:T(8,128)}, f32[128,768]{1,0:T(8,128)S(1)}, u32[]{:S(2)}) copy-start(f32[128,768]{1,0:T(8,128)S(1)} %get-tuple-element.50.pre_ref) | copy-start | bytes 1179652
  59.0 1.6 %collective-permute-start.3 = (f32[72,384]{1,0:T(8,128)}, f32[72,384]{1,0:T(8,128)S(1)}, u32[]{:S(2)}, u32[]{:S(2)}) collective-permute-start(f32[72,384]{1,0:T(8,128)} %get-tuple-element.11), channel_id=1, source_target_pairs={{0,8},{1,9},{2,10},{3,11},{4,12},{5,13},{6,14},{7,15},{8,0},{9,1},... | collective-permute-start | bytes 331784 | tf_op jit(solution)/shard_map/ppermute | solution.py:163
  61.5 5.2 %collective-permute-start.4 = (f32[72,384]{1,0:T(8,128)S(1)}, f32[72,384]{1,0:T(8,128)S(1)}, u32[]{:S(2)}, u32[]{:S(2)}) collective-permute-start(f32[72,384]{1,0:T(8,128)S(1)} %add.172), channel_id=1, source_target_pairs={{0,1},{1,0},{2,3},{3,2},{4,5},{5,4},{6,7},{7,6},{8,9},{9,8},{10,11... | collective-permute-start | bytes 331784 | tf_op jit(solution)/shard_map/ppermute | solution.py:167
  66.7 4.8 %collective-permute-start.5 = (f32[72,384]{1,0:T(8,128)S(1)}, f32[72,384]{1,0:T(8,128)S(1)}, u32[]{:S(2)}, u32[]{:S(2)}) collective-permute-start(f32[72,384]{1,0:T(8,128)S(1)} %add.173), channel_id=1, source_target_pairs={{0,2},{1,3},{2,0},{3,1},{4,6},{5,7},{6,4},{7,5},{8,10},{9,11},{10,... | collective-permute-start | bytes 331784 | tf_op jit(solution)/shard_map/ppermute | solution.py:167
  71.5 6.3 %collective-permute-start.6 = (f32[72,384]{1,0:T(8,128)S(1)}, f32[72,384]{1,0:T(8,128)S(1)}, u32[]{:S(2)}, u32[]{:S(2)}) collective-permute-start(f32[72,384]{1,0:T(8,128)S(1)} %add.174), channel_id=1, source_target_pairs={{0,4},{1,5},{2,6},{3,7},{4,0},{5,1},{6,2},{7,3},{8,12},{9,13},{10,... | collective-permute-start | bytes 331784 | tf_op jit(solution)/shard_map/ppermute | solution.py:167
  77.9 4.8 %collective-permute-start.7 = (f32[72,384]{1,0:T(8,128)S(1)}, f32[72,384]{1,0:T(8,128)S(1)}, u32[]{:S(2)}, u32[]{:S(2)}) collective-permute-start(f32[72,384]{1,0:T(8,128)S(1)} %add.175), channel_id=1, source_target_pairs={{0,16},{1,17},{2,18},{3,19},{4,20},{5,21},{6,22},{7,23},{8,24},{9,... | collective-permute-start | bytes 331784 | tf_op jit(solution)/shard_map/ppermute | solution.py:167
  82.7 1.4 %copy-start.2 = (f32[72,384]{1,0:T(8,128)}, f32[72,384]{1,0:T(8,128)S(1)}, u32[]{:S(2)}) copy-start(f32[72,384]{1,0:T(8,128)S(1)} %add.176.mine_ref) | copy-start | bytes 331780
  82.7 1.4 %collective-permute-start.8 = (f32[72,384]{1,0:T(8,128)S(1)}, f32[72,384]{1,0:T(8,128)S(1)}, u32[]{:S(2)}, u32[]{:S(2)}) collective-permute-start(f32[72,384]{1,0:T(8,128)S(1)} %add.176.mine_ref), channel_id=1, source_target_pairs={{0,8},{1,9},{2,10},{3,11},{4,12},{5,13},{6,14},{7,15},{8,0},{9,1},... | collective-permute-start | bytes 331784 | tf_op jit(solution)/shard_map/ppermute | solution.py:171
  84.1 0.7 copy-start.4
